TPU v7x, 32 devices: a whole 2x2x4 slice. The times are simulated.
32 devices in a mesh: dp: 2 (over core), ctx: 16 (over z, y, x).
Axes of the slice: x: 2, y: 2, z: 4, core: 2. Of those that a mesh axis runs over, the one named last changes fastest.
Arguments:
- tokens: bfloat16 [8192, 2880], P(('dp', 'ctx')), parts along dimension 0, may hold values from -6 to 6
- positions: int32 [8192], P(('dp', 'ctx')), parts along dimension 0, may hold values from 0 to 4223, as said below
- norm_gain: float32 [2880], replicated, may hold values from 0.5 to 1.5
- qkv_weight: bfloat16 [2880, 2560], P(None, 'ctx'), may hold values from -4 to 4
- qkv_bias: float32 [2560], replicated, may hold values from -3 to 3
- sinks: float32 [32], replicated, may hold values from 0 to 4
- earlier_keys: bfloat16 [256, 256], P('dp'), parts along dimension 0, may hold values from -6 to 6
- earlier_values: bfloat16 [256, 256], P('dp'), parts along dimension 0, may hold values from -6 to 6
Outputs:
- attended: bfloat16 [8192, 2048], P(('dp', 'ctx')), parts along dimension 0
There are 2 independent parts, one for each index of `dp`. A program takes and returns all parts, laid end to end along the dimension named above; an argument that names none is the same for every part. Nothing has to cross between parts.
Inputs may be any that keep to these rules, and one draw needn't show every extreme that they name: Within each document positions rise by one from token to token and restart at 0 where the next document begins; the first token of the span continues a document of the previous span and has position 128 or more, so that the previous span's last 128 tokens belong to it; at least one document begins inside the span, and the token just before the first such start has position 4223.
All inputs are finite; a program needn't handle non-finite values.
Results may differ from a plain program's by a relative error of at most 0.0074.
Values may be sent and summed in bfloat16 or wider, within the bound.
No kernel may reach another device: no remote copies, remote signals or barrier semaphores. Data moves between devices by JAX's collectives and lax.ppermute only.
A program may use at most 64 MiB of HBM per device.

v0:
```python
import jax
import jax.numpy as jnp
from jax import lax
from jax.sharding import PartitionSpec as P

QUERY_HEADS = 32
KEY_VALUE_HEADS = 4
HEAD_SIZE = 64
WINDOW_TOKENS = 128


def shifted(value, axis, steps):
    count = lax.axis_size(axis)
    leading, last = (max(0, -steps), min(count, count - steps))
    return lax.ppermute(value, axis, [(source, source + steps) for source in range(leading, last)])


def apply_rotation(heads, positions):
    half = heads.shape[-1] // 2
    freq = 150000.0 ** (-(jnp.arange(half, dtype=jnp.float32) * 2.0 / heads.shape[-1]))
    angle = positions.astype(jnp.float32)[:, None] * freq[None, :]
    cosine = jnp.cos(angle)[:, None, :]
    sine = jnp.sin(angle)[:, None, :]
    first = heads[..., :half]
    second = heads[..., half:]
    return jnp.concatenate(
        [first * cosine - second * sine, second * cosine + first * sine], axis=-1
    )


def attend_head(query_rows, key_rows, value_rows, sink_row, visible):
    scores = jnp.einsum(
        "nrgd,nkd->ngrk", query_rows, key_rows, preferred_element_type=jnp.float32
    ) * HEAD_SIZE ** (-0.5)
    scores = jnp.where(visible[:, None], scores, -1e30)
    top = jnp.maximum(jnp.max(scores, axis=-1), sink_row[None, :, None])
    expo = jnp.exp(scores - top[..., None])
    total = jnp.sum(expo, axis=-1) + jnp.exp(sink_row[None, :, None] - top)
    probs = (expo / total[..., None]).astype(jnp.bfloat16)
    out = jnp.einsum("ngrk,nkd->nrgd", probs, value_rows, preferred_element_type=jnp.float32)
    return out.astype(jnp.bfloat16)


def send_rim(window_output, token_rows):
    return shifted(window_output[:, token_rows - WINDOW_TOKENS :], "ctx", 1)


def split_mixed(combined_output, positions, token_rows, query_length, key_length):
    key_rows = apply_rotation(
        combined_output[:, query_length : query_length + key_length].reshape(
            token_rows, KEY_VALUE_HEADS, HEAD_SIZE
        ),
        positions,
    ).astype(jnp.bfloat16)
    value_rows = combined_output[:, query_length + key_length :].astype(jnp.bfloat16)
    window_output = jnp.stack([key_rows.reshape(token_rows, key_length), value_rows])
    received = send_rim(window_output, token_rows)
    query_rows = apply_rotation(
        combined_output[:, :query_length].reshape(token_rows, QUERY_HEADS, HEAD_SIZE), positions
    ).astype(jnp.bfloat16)
    return (window_output, received, query_rows)


def on_device(
    tokens, positions, norm_gain, qkv_weight, qkv_bias, sinks, earlier_keys, earlier_values
):
    token_rows = tokens.shape[0]
    query_group = QUERY_HEADS // KEY_VALUE_HEADS
    query_length = QUERY_HEADS * HEAD_SIZE
    key_length = KEY_VALUE_HEADS * HEAD_SIZE
    flat = tokens.astype(jnp.float32)
    scale = lax.rsqrt(jnp.mean(flat * flat, axis=-1, keepdims=True) + 1e-05)
    normed = (flat * scale * norm_gain[None, :]).astype(jnp.bfloat16)
    combined_output = jnp.dot(
        normed,
        lax.all_gather(qkv_weight, "ctx", axis=1, tiled=True),
        preferred_element_type=jnp.float32,
    )
    combined_output = combined_output + qkv_bias[None, :]
    window_output, received, query_rows = split_mixed(
        combined_output, positions, token_rows, query_length, key_length
    )
    prior = jnp.stack([earlier_keys, earlier_values])
    border_tokens = jnp.where(lax.axis_index("ctx") == 0, prior, received)
    padded_rows = jnp.concatenate([border_tokens, window_output], axis=1).reshape(
        2, WINDOW_TOKENS + token_rows, KEY_VALUE_HEADS, HEAD_SIZE
    )
    joined_keys = padded_rows[0]
    joined_values = padded_rows[1]
    limit = jnp.minimum(positions, WINDOW_TOKENS - 1)
    sink_tokens = sinks.reshape(KEY_VALUE_HEADS, query_group)
    rel = (
        jnp.arange(token_rows, dtype=jnp.int32)[:, None]
        - jnp.arange(WINDOW_TOKENS + token_rows, dtype=jnp.int32)[None, :]
        + WINDOW_TOKENS
    )
    visible = ((rel >= 0) & (rel <= limit[:, None]))[None]
    query_blocks = query_rows.reshape(1, token_rows, KEY_VALUE_HEADS, query_group, HEAD_SIZE)
    window_keys = joined_keys[None]
    window_values = joined_values[None]

    def one_head(items):
        return attend_head(items[0], items[1], items[2], items[3], visible)

    out = lax.map(
        one_head,
        (
            jnp.moveaxis(query_blocks, 2, 0),
            jnp.moveaxis(window_keys, 2, 0),
            jnp.moveaxis(window_values, 2, 0),
            sink_tokens,
        ),
    )
    return jnp.moveaxis(out, 0, 2).reshape(token_rows, query_length)


def solution(mesh):
    placed = (
        P(("dp", "ctx"), None),
        P(("dp", "ctx")),
        P(),
        P(None, "ctx"),
        P(),
        P(),
        P("dp", None),
        P("dp", None),
    )
    return jax.shard_map(
        on_device, mesh=mesh, in_specs=placed, out_specs=P(("dp", "ctx"), None), check_vma=False
    )
```

profile of v0, /device:TPU:4, one launch (start us, length us, event | category | flops | bytes accessed | tf_op | source)
XLA Modules:
  0.0 232.4 jit_solution(17536291176751203206)
XLA Ops:
  6.5 0.0 all-gather.2.cloned.1.call-start
  6.5 0.7 all-gather.2.cloned.1.call-update
  7.3 0.7 reshape.219
  8.0 1.8 fusion.30
  9.8 0.8 broadcast_minimum_fusion
  10.6 0.8 multiply_cosine_fusion
  11.4 175.5 %all-gather.2.cloned.1.call-done = bf16[2880,2560]{0,1:T(8,128)(2,1)} async-done(((bf16[2880,160]{0,1:T(8,128)(2,1)}), bf16[2880,2560]{0,1:T(8,128)(2,1)}) %all-gather.2.cloned.1.call-update) | async-done | bytes 14745616 | tf_op jit(solution)/shard_map/all_gather | solution.py:76
  187.0 9.2 %convolution_add_fusion = f32[256,2560]{1,0:T(8,128)S(1)} fusion(bf16[2880,2560]{0,1:T(8,128)(2,1)} %all-gather.2.cloned.1.call-done, bf16[256,2880]{0,1:T(8,128)(2,1)} %param.10, f32[2880]{0:T(1024)} %param.12, f32[256]{0:T(256)S(1)} %add_rsqrt_fusion, f32[2560]{0:T(1024)} %param.14), kind=kOutput, calls=%fused_computation.30 | convolution fusion | flops 3778478080 | bytes 18864384 | tf_op jit(solution)/shard_map/dot_general | solution.py:74
  196.2 1.5 slice.55
  197.7 1.9 copy.20
  199.7 0.1 copy.16
  199.8 1.1 subtract_convert_fusion
  200.9 0.0 copy-start
  200.9 0.0 copy-start.1
  200.9 0.8 subtract_convert_fusion.1
  201.8 0.1 copy.17
  201.9 2.5 %collective-permute-start = (bf16[2,128,256]{2,1,0:T(8,128)(2,1)S(1)}, bf16[2,128,256]{2,1,0:T(8,128)(2,1)S(1)}, u32[]{:S(2)}, u32[]{:S(2)}) collective-permute-start(bf16[2,128,256]{2,1,0:T(8,128)(2,1)S(1)} %pad_maximum_fusion), channel_id=1, source_target_pairs={{0,1},{1,2},{2,3},{3,4},{4,5},{5,6},{6,7},{7,8},{8,9},{9,10},{10,1... | collective-permute-start | bytes 393224 | tf_op jit(solution)/shard_map/ppermute | solution.py:15
  204.4 0.1 maximum_bitcast_fusion
  204.5 5.2 %collective-permute-done = bf16[2,128,256]{2,1,0:T(8,128)(2,1)S(1)} collective-permute-done((bf16[2,128,256]{2,1,0:T(8,128)(2,1)S(1)}, bf16[2,128,256]{2,1,0:T(8,128)(2,1)S(1)}, u32[]{:S(2)}, u32[]{:S(2)}) %collective-permute-start) | collective-permute-done | bytes 131104 | tf_op jit(solution)/shard_map/ppermute | solution.py:15
  209.7 0.0 copy-done
  209.7 0.0 copy-done.1
  209.8 0.2 copy.19
  209.9 0.2 copy.18
  210.1 13.2 %while.11 = (s32[]{:T(128)}, bf16[4,1,256,8,64]{2,4,3,1,0:T(8,128)(2,1)}, bf16[4,1,384,64]{2,3,1,0:T(8,128)(2,1)S(1)}, bf16[4,1,384,64]{2,3,1,0:T(8,128)(2,1)S(1...) while((s32[]{:T(128)}, ...), condition=%wide.region_4.5_spmd.clone, body=%wide.region_1.4_spmd.clone.sunk | while | flops 211390464 | bytes 10538209 | solution.py:105
  210.1 0.1 fusion.48
  210.2 0.7 fusion.49
  210.9 0.1 broadcast_maximum_fusion.2
  211.0 0.7 fusion.51
  211.7 0.1 exponential_add_fusion.2
  211.7 1.7 fusion.52
  213.4 0.1 fusion.48
  213.5 0.7 fusion.49
  214.2 0.1 broadcast_maximum_fusion.2
  214.3 0.7 fusion.51
  214.9 0.1 exponential_add_fusion.2
  215.0 1.7 fusion.52
  216.7 0.1 fusion.48
  216.8 0.7 fusion.49
  217.5 0.1 broadcast_maximum_fusion.2
  217.6 0.7 fusion.51
  218.2 0.1 exponential_add_fusion.2
  218.3 1.7 fusion.52
  220.0 0.1 fusion.48
  220.1 0.7 fusion.49
  220.8 0.1 broadcast_maximum_fusion.2
  220.9 0.7 fusion.51
  221.5 0.1 exponential_add_fusion.2
  221.6 1.7 fusion.52
  223.3 2.3 copy.26
  (14 shorter events, 0.2 us)
Async XLA Ops:
  6.5 180.4 %all-gather.2.cloned.1.call-start = ((), (), s32[]{:S(2)}) async-start(), calls=%async_computation | async-start | bytes 16015360 | tf_op jit(solution)/shard_map/all_gather | solution.py:76
  200.9 8.8 %copy-start = (bf16[128,256]{1,0:T(8,128)(2,1)S(1)}, bf16[128,256]{1,0:T(8,128)(2,1)}, u32[]{:S(2)}) copy-start(bf16[128,256]{1,0:T(8,128)(2,1)} %param.17) | copy-start | bytes 196612
  200.9 8.8 %copy-start.1 = (bf16[128,256]{1,0:T(8,128)(2,1)S(1)}, bf16[128,256]{1,0:T(8,128)(2,1)}, u32[]{:S(2)}) copy-start(bf16[128,256]{1,0:T(8,128)(2,1)} %param.16) | copy-start | bytes 196612
  201.9 7.8 %collective-permute-start = (bf16[2,128,256]{2,1,0:T(8,128)(2,1)S(1)}, bf16[2,128,256]{2,1,0:T(8,128)(2,1)S(1)}, u32[]{:S(2)}, u32[]{:S(2)}) collective-permute-start(bf16[2,128,256]{2,1,0:T(8,128)(2,1)S(1)} %pad_maximum_fusion), channel_id=1, source_target_pairs={{0,1},{1,2},{2,3},{3,4},{4,5},{5,6},{6,7},{7,8},{8,9},{9,10},{10,1... | collective-permute-start | bytes 393224 | tf_op jit(solution)/shard_map/ppermute | solution.py:15
Sparse Core Ops, SparseCore 0:
  10.1 176.7 all-gather.1
where the time goes:
time: 233 us; the launch traced here: 232 us
  waiting for transfers between devices  181 us (78%)
  matrix products  18.7 us (8%)
  between operations  13.5 us (6%)
  other arithmetic  9.07 us (4%)
  local copies, waits for them, and re-layouts  7.09 us (3%)
  starting transfers between devices  2.47 us (1%)
    all_gather x1, waiting for transfers between devices, on_device(): lax.all_gather(qkv_weight, 'ctx', axis=1, tiled=True)  176 us
    dot_general x1, matrix products, on_device(): jnp.dot(normed, lax.all_gather(qkv_weight, 'ctx', axis=1, tiled=True), pr...  9.19 us
    dot_general x4, matrix products, attend_head(): jnp.einsum('ngrk,nkd->nrgd', probs, value_rows, preferred_element_type=jn...  6.84 us
    ppermute x1, waiting for transfers between devices, shifted(): lax.ppermute(value, axis, [(source, source + steps) for source in range(l...  5.2 us
  transfers between devices with their start and end apart: 2, of which 2 were waited for; matrix products, arithmetic and copies ran while one was open for 2% of the time, Pallas kernels for 0%

commit v1 on v0

--- a/solution.py
+++ b/solution.py
@@ -61,6 +61,16 @@
     return (window_output, received, query_rows)
 
 
+def gather_weight(qkv_weight):
+    pairs = lax.axis_size("dp")
+    columns = qkv_weight.shape[1]
+    if columns % pairs:
+        return lax.all_gather(qkv_weight, "ctx", axis=1, tiled=True)
+    piece = columns // pairs
+    own = lax.dynamic_slice_in_dim(qkv_weight, lax.axis_index("dp") * piece, piece, axis=1)
+    return lax.all_gather(own, ("ctx", "dp"), axis=1, tiled=True)
+
+
 def on_device(
     tokens, positions, norm_gain, qkv_weight, qkv_bias, sinks, earlier_keys, earlier_values
 ):
@@ -72,9 +82,7 @@
     scale = lax.rsqrt(jnp.mean(flat * flat, axis=-1, keepdims=True) + 1e-05)
     normed = (flat * scale * norm_gain[None, :]).astype(jnp.bfloat16)
     combined_output = jnp.dot(
-        normed,
-        lax.all_gather(qkv_weight, "ctx", axis=1, tiled=True),
-        preferred_element_type=jnp.float32,
+        normed, gather_weight(qkv_weight), preferred_element_type=jnp.float32
     )
     combined_output = combined_output + qkv_bias[None, :]
     window_output, received, query_rows = split_mixed(

time: 233 us -> 170 us (0.73)
  waiting for transfers between devices: 181 us -> 109 us
  local copies, waits for them, and re-layouts: 7.09 us -> 10.7 us
  matrix products: 18.7 us -> 21.8 us
  other arithmetic: 9.07 us -> 11.9 us
    all_gather x1, waiting for transfers between devices: 176 us -> 107 us  [gather_weight(): return lax.all_gather(own, ('ctx', 'dp'), axis=1, tiled=True)]
    dot_general x1, matrix products: 9.19 us -> 12.1 us  [on_device(): jnp.dot(normed, gather_weight(qkv_weight), preferred_element_type=jnp.flo...]
    ppermute x1, waiting for transfers between devices: 5.2 us -> 2.41 us  [shifted(): lax.ppermute(value, axis, [(source, source + steps) for source in range(l...]
  transfers between devices with their start and end apart: 2 -> 2, of which waited for: 2 -> 2; matrix products, arithmetic and copies ran while one was open for 2% -> 4% of each run, Pallas kernels for 0% -> 0%
where the time goes in v1:
time: 170 us
  waiting for transfers between devices  109 us (64%)
  matrix products  21.8 us (13%)
  between operations  13.5 us (8%)
  other arithmetic  11.9 us (7%)
  local copies, waits for them, and re-layouts  10.7 us (6%)
  starting transfers between devices  2.46 us (1%)
    all_gather x1, waiting for transfers between devices, gather_weight(): return lax.all_gather(own, ('ctx', 'dp'), axis=1, tiled=True)  107 us
    dot_general x1, matrix products, on_device(): jnp.dot(normed, gather_weight(qkv_weight), preferred_element_type=jnp.flo...  12.1 us
    dot_general x4, matrix products, attend_head(): jnp.einsum('ngrk,nkd->nrgd', probs, value_rows, preferred_element_type=jn...  7.09 us
  transfers between devices with their start and end apart: 2, of which 2 were waited for; matrix products, arithmetic and copies ran while one was open for 4% of the time, Pallas kernels for 0%

profile of v1, /device:TPU:4, one launch (start us, length us, event | category | flops | bytes accessed | tf_op | source)
XLA Modules:
  0.0 169.6 jit_solution(12750827321029584677)
XLA Ops:
  6.5 0.0 copy-start
  6.5 0.0 all-gather.2.cloned.1.call-start
  6.5 1.2 copy-done
  7.7 0.8 constant_dynamic-slice_fusion.1
  8.5 0.0 all-gather.2.cloned.1.call-update
  8.6 0.7 reshape.219
  9.3 1.8 %fusion.30 = f32[256]{0:T(256)S(1)} fusion(bf16[256,2880]{0,1:T(8,128)(2,1)} %param.10), kind=kLoop, calls=%fused_computation.33 | loop fusion | flops 2211584 | bytes 1475584 | tf_op jit(solution)/shard_map/reduce_sum | solution.py:82
  11.1 0.8 broadcast_minimum_fusion
  11.9 0.2 multiply_cosine_fusion
  12.1 106.5 %all-gather.2.cloned.1.call-done = bf16[2880,2560]{0,1:T(8,128)(2,1)} async-done(((bf16[2880,80]{0,1:T(8,128)(2,1)}), bf16[2880,2560]{0,1:T(8,128)(2,1)}) %all-gather.2.cloned.1.call-update) | async-done | bytes 14745616 | tf_op jit(solution)/shard_map/all_gather | solution.py:71
  118.6 12.1 %convolution_add_fusion = f32[256,2560]{1,0:T(8,128)} fusion(bf16[2880,2560]{0,1:T(8,128)(2,1)} %all-gather.2.cloned.1.call-done, bf16[256,2880]{0,1:T(8,128)(2,1)} %param.10, f32[2880]{0:T(1024)} %param.12, f32[256]{0:T(256)S(1)} %add_rsqrt_fusion, f32[2560]{0:T(1024)} %param.14), kind=kOutput, calls=%fused_computation.30 | convolution fusion | flops 3778478080 | bytes 18864384 | tf_op jit(solution)/shard_map/dot_general | solution.py:84
  130.7 0.0 slice-start
  130.7 0.0 slice-start.1
  130.7 1.1 fusion.36
  131.8 0.0 slice-done
  131.8 0.8 copy.16
  132.7 1.0 subtract_convert_fusion.1
  133.7 0.1 copy.17
  133.8 0.0 copy-start.1
  133.8 0.7 pad_maximum_fusion
  134.5 2.5 %collective-permute-start = (bf16[2,128,256]{2,1,0:T(8,128)(2,1)}, bf16[2,128,256]{2,1,0:T(8,128)(2,1)}, u32[]{:S(2)}, u32[]{:S(2)}) collective-permute-start(bf16[2,128,256]{2,1,0:T(8,128)(2,1)} %pad_maximum_fusion), channel_id=1, source_target_pairs={{0,1},{1,2},{2,3},{3,4},{4,5},{5,6},{6,7},{7,8},{8,9},{9,10},{10,1... | collective-permute-start | bytes 393224 | tf_op jit(solution)/shard_map/ppermute | solution.py:15
  137.0 0.0 slice-done.1
  137.0 1.8 %copy.20 = f32[256,2048]{0,1:T(8,128)} copy(f32[256,2048]{1,0:T(8,128)S(1)} %slice-done.1) | data formatting | bytes 4194304 | tf_op jit(solution)/shard_map/slice | solution.py:59
  138.8 0.0 copy-start.3
  138.8 0.0 copy-start.4
  138.8 1.9 %subtract_convert_fusion = (bf16[256,32,32]{0,2,1:T(8,128)(2,1)S(1)}, bf16[256,32,32]{0,2,1:T(8,128)(2,1)S(1)}) fusion(f32[256,32,64]{0,2,1:T(8,128)} %bitcast.104, f32[256,32]{0,1:T(8,128)S(1)} %get-tuple-element.90, f32[256,32]{0,1:T(8,128)S(1)} %get-tuple-element.89), kind=kLoop, calls=%fused_computation.40 | loop fusion | flops 2097152 | bytes 3211264 | tf_op jit(solution)/shard_map/convert.6
  140.7 0.0 copy-done.1
  140.8 0.0 copy-start.2
  140.8 0.1 maximum_bitcast_fusion
  140.9 2.4 %collective-permute-done = bf16[2,128,256]{2,1,0:T(8,128)(2,1)} collective-permute-done((bf16[2,128,256]{2,1,0:T(8,128)(2,1)}, bf16[2,128,256]{2,1,0:T(8,128)(2,1)}, u32[]{:S(2)}, u32[]{:S(2)}) %collective-permute-start) | collective-permute-done | bytes 131104 | tf_op jit(solution)/shard_map/ppermute | solution.py:15
  143.3 0.0 copy-done.3
  143.3 0.0 copy-done.4
  143.3 0.9 maximum_select_fusion
  144.2 0.9 maximum_maximum_fusion
  145.2 0.7 fusion.37
  145.9 1.1 copy.19
  146.9 0.8 copy.18
  147.8 0.0 copy-done.2
  147.8 13.5 %while.11 = (s32[]{:T(128)}, bf16[4,1,256,8,64]{2,4,3,1,0:T(8,128)(2,1)S(1)}, bf16[4,1,384,64]{2,3,1,0:T(8,128)(2,1)}, bf16[4,1,384,64]{2,3,1,0:T(8,128)(2,1)S(1...) while((s32[]{:T(128)}, ...), condition=%wide.region_4.5_spmd.clone, body=%wide.region_1.4_spmd.clone.sunk | while | flops 211390464 | bytes 10538201 | solution.py:113
  147.8 0.1 fusion.48
  147.9 0.7 fusion.49
  148.6 0.1 broadcast_maximum_fusion.2
  148.6 0.7 fusion.51
  149.3 0.1 exponential_add_fusion.2
  149.4 1.8 %fusion.52 = bf16[4,1,256,8,64]{2,4,3,1,0:T(8,128)(2,1)S(1)} fusion(bf16[4,1,256,8,64]{2,4,3,1,0:T(8,128)(2,1)S(1)} %get-tuple-element.149, s32[]{:T(128)} %get-tuple-element.148, f32[8,256]{1,0:T(8,128)S(1)} %exponential_add_fusion.2, f32[8,256]{1,0:T(8,128)S(1)} %broadcast_maximum_fusion.2, f32[384,256,8]{1,0,2:T(8,128)S(1)} %get-tuple-element.138, ...), kind=kOutput, calls=%fused_computation.10.clone.1 | convolution fusion | flops 104726528 | bytes 3572736 | tf_op jit(solution)/shard_map/while/body/eval_jaxpr/ngrk,nkd->nrgd/dot_general | solution.py:40
  151.2 0.1 fusion.48
  151.3 0.7 fusion.49
  151.9 0.1 broadcast_maximum_fusion.2
  152.0 0.7 fusion.51
  152.7 0.1 exponential_add_fusion.2
  152.8 1.8 %fusion.52 = bf16[4,1,256,8,64]{2,4,3,1,0:T(8,128)(2,1)S(1)} fusion(bf16[4,1,256,8,64]{2,4,3,1,0:T(8,128)(2,1)S(1)} %get-tuple-element.149, s32[]{:T(128)} %get-tuple-element.148, f32[8,256]{1,0:T(8,128)S(1)} %exponential_add_fusion.2, f32[8,256]{1,0:T(8,128)S(1)} %broadcast_maximum_fusion.2, f32[384,256,8]{1,0,2:T(8,128)S(1)} %get-tuple-element.138, ...), kind=kOutput, calls=%fused_computation.10.clone.1 | convolution fusion | flops 104726528 | bytes 3572736 | tf_op jit(solution)/shard_map/while/body/eval_jaxpr/ngrk,nkd->nrgd/dot_general | solution.py:40
  154.5 0.1 fusion.48
  154.6 0.7 fusion.49
  155.3 0.1 broadcast_maximum_fusion.2
  155.4 0.7 fusion.51
  156.1 0.1 exponential_add_fusion.2
  156.1 1.8 %fusion.52 = bf16[4,1,256,8,64]{2,4,3,1,0:T(8,128)(2,1)S(1)} fusion(bf16[4,1,256,8,64]{2,4,3,1,0:T(8,128)(2,1)S(1)} %get-tuple-element.149, s32[]{:T(128)} %get-tuple-element.148, f32[8,256]{1,0:T(8,128)S(1)} %exponential_add_fusion.2, f32[8,256]{1,0:T(8,128)S(1)} %broadcast_maximum_fusion.2, f32[384,256,8]{1,0,2:T(8,128)S(1)} %get-tuple-element.138, ...), kind=kOutput, calls=%fused_computation.10.clone.1 | convolution fusion | flops 104726528 | bytes 3572736 | tf_op jit(solution)/shard_map/while/body/eval_jaxpr/ngrk,nkd->nrgd/dot_general | solution.py:40
  157.9 0.1 fusion.48
  158.0 0.7 fusion.49
  158.7 0.1 broadcast_maximum_fusion.2
  158.8 0.7 fusion.51
  159.5 0.1 exponential_add_fusion.2
  159.5 1.8 %fusion.52 = bf16[4,1,256,8,64]{2,4,3,1,0:T(8,128)(2,1)S(1)} fusion(bf16[4,1,256,8,64]{2,4,3,1,0:T(8,128)(2,1)S(1)} %get-tuple-element.149, s32[]{:T(128)} %get-tuple-element.148, f32[8,256]{1,0:T(8,128)S(1)} %exponential_add_fusion.2, f32[8,256]{1,0:T(8,128)S(1)} %broadcast_maximum_fusion.2, f32[384,256,8]{1,0,2:T(8,128)S(1)} %get-tuple-element.138, ...), kind=kOutput, calls=%fused_computation.10.clone.1 | convolution fusion | flops 104726528 | bytes 3572736 | tf_op jit(solution)/shard_map/while/body/eval_jaxpr/ngrk,nkd->nrgd/dot_general | solution.py:40
  161.3 1.4 copy.26
  (8 shorter events, 0.1 us)
Async XLA Ops:
  6.5 1.2 copy-start
  6.5 112.1 %all-gather.2.cloned.1.call-start = ((), (), s32[]{:S(2)}) async-start(), calls=%async_computation | async-start | bytes 15544320 | tf_op jit(solution)/shard_map/all_gather | solution.py:71
  130.7 1.1 slice-start
  130.7 6.3 %slice-start.1 = ((f32[256,2560]{1,0:T(8,128)}), f32[256,2048]{1,0:T(8,128)S(1)}, s32[]{:S(2)}) async-start(f32[256,2560]{1,0:T(8,128)} %convolution_add_fusion), calls=%async_computation.2 | async-start | bytes 4194304 | tf_op jit(solution)/shard_map/slice | solution.py:59
  133.8 6.9 %copy-start.1 = (bf16[1,256,256]{2,1,0:T(8,128)(2,1)}, bf16[1,256,256]{2,1,0:T(8,128)(2,1)S(1)}, u32[]{:S(2)}) copy-start(bf16[1,256,256]{2,1,0:T(8,128)(2,1)S(1)} %copy.17) | copy-start | bytes 393220
  134.5 8.8 %collective-permute-start = (bf16[2,128,256]{2,1,0:T(8,128)(2,1)}, bf16[2,128,256]{2,1,0:T(8,128)(2,1)}, u32[]{:S(2)}, u32[]{:S(2)}) collective-permute-start(bf16[2,128,256]{2,1,0:T(8,128)(2,1)} %pad_maximum_fusion), channel_id=1, source_target_pairs={{0,1},{1,2},{2,3},{3,4},{4,5},{5,6},{6,7},{7,8},{8,9},{9,10},{10,1... | collective-permute-start | bytes 393224 | tf_op jit(solution)/shard_map/ppermute | solution.py:15
  138.8 4.4 %copy-start.3 = (bf16[128,256]{1,0:T(8,128)(2,1)S(1)}, bf16[128,256]{1,0:T(8,128)(2,1)}, u32[]{:S(2)}) copy-start(bf16[128,256]{1,0:T(8,128)(2,1)} %param.17) | copy-start | bytes 196612
  138.8 4.4 %copy-start.4 = (bf16[128,256]{1,0:T(8,128)(2,1)S(1)}, bf16[128,256]{1,0:T(8,128)(2,1)}, u32[]{:S(2)}) copy-start(bf16[128,256]{1,0:T(8,128)(2,1)} %param.16) | copy-start | bytes 196612
  140.8 7.0 %copy-start.2 = (bf16[4,1,256,8,64]{2,4,3,1,0:T(8,128)(2,1)S(1)}, bf16[4,1,256,8,64]{2,4,3,1,0:T(8,128)(2,1)}, u32[]{:S(2)}) copy-start(bf16[4,1,256,8,64]{2,4,3,1,0:T(8,128)(2,1)} %custom-call) | copy-start | bytes 3145732
Sparse Core Ops, SparseCore 0:
  10.2 108.3 all-gather.1

commit v2 on v1

--- a/solution.py
+++ b/solution.py
@@ -65,10 +65,10 @@
     pairs = lax.axis_size("dp")
     columns = qkv_weight.shape[1]
     if columns % pairs:
-        return lax.all_gather(qkv_weight, "ctx", axis=1, tiled=True)
+        return lax.all_gather(qkv_weight.T, "ctx", axis=0, tiled=True)
     piece = columns // pairs
     own = lax.dynamic_slice_in_dim(qkv_weight, lax.axis_index("dp") * piece, piece, axis=1)
-    return lax.all_gather(own, ("ctx", "dp"), axis=1, tiled=True)
+    return lax.all_gather(own.T, ("ctx", "dp"), axis=0, tiled=True)
 
 
 def on_device(
@@ -81,8 +81,11 @@
     flat = tokens.astype(jnp.float32)
     scale = lax.rsqrt(jnp.mean(flat * flat, axis=-1, keepdims=True) + 1e-05)
     normed = (flat * scale * norm_gain[None, :]).astype(jnp.bfloat16)
-    combined_output = jnp.dot(
-        normed, gather_weight(qkv_weight), preferred_element_type=jnp.float32
+    combined_output = lax.dot_general(
+        normed,
+        gather_weight(qkv_weight),
+        (((1,), (1,)), ((), ())),
+        preferred_element_type=jnp.float32,
     )
     combined_output = combined_output + qkv_bias[None, :]
     window_output, received, query_rows = split_mixed(

time: 170 us -> 170 us (level)
  no operation moved by 1% of the time
where the time goes in v2:
time: 170 us
  waiting for transfers between devices  109 us (64%)
  matrix products  21.8 us (13%)
  between operations  13.5 us (8%)
  other arithmetic  11.9 us (7%)
  local copies, waits for them, and re-layouts  10.7 us (6%)
  starting transfers between devices  2.46 us (1%)
    all_gather x1, waiting for transfers between devices, gather_weight(): return lax.all_gather(own.T, ('ctx', 'dp'), axis=0, tiled=True)  107 us
    dot_general x1, matrix products, on_device(): lax.dot_general(normed, gather_weight(qkv_weight), (((1,), (1,)), ((), ()...  12.1 us
    dot_general x4, matrix products, attend_head(): jnp.einsum('ngrk,nkd->nrgd', probs, value_rows, preferred_element_type=jn...  7.09 us
  transfers between devices with their start and end apart: 2, of which 2 were waited for; matrix products, arithmetic and copies ran while one was open for 4% of the time, Pallas kernels for 0%

profile of v2, /device:TPU:4, one launch (start us, length us, event | category | flops | bytes accessed | tf_op | source)
XLA Modules:
  0.0 169.6 jit_solution(12750827321029584677)
XLA Ops:
  6.5 0.0 copy-start
  6.5 0.0 all-gather.2.cloned.1.call-start
  6.5 1.2 copy-done
  7.7 0.8 dynamic-slice_bitcast_fusion
  8.5 0.0 all-gather.2.cloned.1.call-update
  8.6 0.7 reshape.219
  9.3 1.8 %fusion.30 = f32[256]{0:T(256)S(1)} fusion(bf16[256,2880]{0,1:T(8,128)(2,1)} %param.10), kind=kLoop, calls=%fused_computation.33 | loop fusion | flops 2211584 | bytes 1475584 | tf_op jit(solution)/shard_map/reduce_sum | solution.py:82
  11.1 0.8 broadcast_minimum_fusion
  11.9 0.2 multiply_cosine_fusion
  12.1 106.5 %all-gather.2.cloned.1.call-done = bf16[2560,2880]{1,0:T(8,128)(2,1)} async-done(((bf16[80,2880]{1,0:T(8,128)(2,1)}), bf16[2560,2880]{1,0:T(8,128)(2,1)}) %all-gather.2.cloned.1.call-update) | async-done | bytes 14745616 | tf_op jit(solution)/shard_map/all_gather | solution.py:71
  118.6 12.1 %convolution_add_fusion = f32[256,2560]{1,0:T(8,128)} fusion(bf16[2560,2880]{1,0:T(8,128)(2,1)} %all-gather.2.cloned.1.call-done, bf16[256,2880]{0,1:T(8,128)(2,1)} %param.10, f32[2880]{0:T(1024)} %param.12, f32[256]{0:T(256)S(1)} %add_rsqrt_fusion, f32[2560]{0:T(1024)} %param.14), kind=kOutput, calls=%fused_computation.30 | convolution fusion | flops 3778478080 | bytes 18864384 | tf_op jit(solution)/shard_map/dot_general | solution.py:84
  130.7 0.0 slice-start
  130.7 0.0 slice-start.1
  130.7 1.1 fusion.36
  131.8 0.0 slice-done
  131.8 0.8 copy.16
  132.7 1.0 subtract_convert_fusion.1
  133.7 0.1 copy.17
  133.8 0.0 copy-start.1
  133.8 0.7 pad_maximum_fusion
  134.5 2.5 %collective-permute-start = (bf16[2,128,256]{2,1,0:T(8,128)(2,1)}, bf16[2,128,256]{2,1,0:T(8,128)(2,1)}, u32[]{:S(2)}, u32[]{:S(2)}) collective-permute-start(bf16[2,128,256]{2,1,0:T(8,128)(2,1)} %pad_maximum_fusion), channel_id=1, source_target_pairs={{0,1},{1,2},{2,3},{3,4},{4,5},{5,6},{6,7},{7,8},{8,9},{9,10},{10,1... | collective-permute-start | bytes 393224 | tf_op jit(solution)/shard_map/ppermute | solution.py:15
  137.0 0.0 slice-done.1
  137.0 1.8 %copy.20 = f32[256,2048]{0,1:T(8,128)} copy(f32[256,2048]{1,0:T(8,128)S(1)} %slice-done.1) | data formatting | bytes 4194304 | tf_op jit(solution)/shard_map/slice | solution.py:59
  138.8 0.0 copy-start.3
  138.8 0.0 copy-start.4
  138.8 1.9 %subtract_convert_fusion = (bf16[256,32,32]{0,2,1:T(8,128)(2,1)S(1)}, bf16[256,32,32]{0,2,1:T(8,128)(2,1)S(1)}) fusion(f32[256,32,64]{0,2,1:T(8,128)} %bitcast.106, f32[256,32]{0,1:T(8,128)S(1)} %get-tuple-element.90, f32[256,32]{0,1:T(8,128)S(1)} %get-tuple-element.89), kind=kLoop, calls=%fused_computation.40 | loop fusion | flops 2097152 | bytes 3211264 | tf_op jit(solution)/shard_map/convert.6
  140.7 0.0 copy-done.1
  140.8 0.0 copy-start.2
  140.8 0.1 maximum_bitcast_fusion
  140.9 2.4 %collective-permute-done = bf16[2,128,256]{2,1,0:T(8,128)(2,1)} collective-permute-done((bf16[2,128,256]{2,1,0:T(8,128)(2,1)}, bf16[2,128,256]{2,1,0:T(8,128)(2,1)}, u32[]{:S(2)}, u32[]{:S(2)}) %collective-permute-start) | collective-permute-done | bytes 131104 | tf_op jit(solution)/shard_map/ppermute | solution.py:15
  143.3 0.0 copy-done.3
  143.3 0.0 copy-done.4
  143.3 0.9 maximum_select_fusion
  144.2 0.9 maximum_maximum_fusion
  145.2 0.7 fusion.37
  145.9 1.1 copy.19
  146.9 0.8 copy.18
  147.8 0.0 copy-done.2
  147.8 13.5 %while.11 = (s32[]{:T(128)}, bf16[4,1,256,8,64]{2,4,3,1,0:T(8,128)(2,1)S(1)}, bf16[4,1,384,64]{2,3,1,0:T(8,128)(2,1)}, bf16[4,1,384,64]{2,3,1,0:T(8,128)(2,1)S(1...) while((s32[]{:T(128)}, ...), condition=%wide.region_4.5_spmd.clone, body=%wide.region_1.4_spmd.clone.sunk | while | flops 211390464 | bytes 10538201 | solution.py:116
  147.8 0.1 fusion.48
  147.9 0.7 fusion.49
  148.6 0.1 broadcast_maximum_fusion.2
  148.6 0.7 fusion.51
  149.3 0.1 exponential_add_fusion.2
  149.4 1.8 %fusion.52 = bf16[4,1,256,8,64]{2,4,3,1,0:T(8,128)(2,1)S(1)} fusion(bf16[4,1,256,8,64]{2,4,3,1,0:T(8,128)(2,1)S(1)} %get-tuple-element.149, s32[]{:T(128)} %get-tuple-element.148, f32[8,256]{1,0:T(8,128)S(1)} %exponential_add_fusion.2, f32[8,256]{1,0:T(8,128)S(1)} %broadcast_maximum_fusion.2, f32[384,256,8]{1,0,2:T(8,128)S(1)} %get-tuple-element.138, ...), kind=kOutput, calls=%fused_computation.10.clone.1 | convolution fusion | flops 104726528 | bytes 3572736 | tf_op jit(solution)/shard_map/while/body/eval_jaxpr/ngrk,nkd->nrgd/dot_general | solution.py:40
  151.2 0.1 fusion.48
  151.3 0.7 fusion.49
  151.9 0.1 broadcast_maximum_fusion.2
  152.0 0.7 fusion.51
  152.7 0.1 exponential_add_fusion.2
  152.8 1.8 %fusion.52 = bf16[4,1,256,8,64]{2,4,3,1,0:T(8,128)(2,1)S(1)} fusion(bf16[4,1,256,8,64]{2,4,3,1,0:T(8,128)(2,1)S(1)} %get-tuple-element.149, s32[]{:T(128)} %get-tuple-element.148, f32[8,256]{1,0:T(8,128)S(1)} %exponential_add_fusion.2, f32[8,256]{1,0:T(8,128)S(1)} %broadcast_maximum_fusion.2, f32[384,256,8]{1,0,2:T(8,128)S(1)} %get-tuple-element.138, ...), kind=kOutput, calls=%fused_computation.10.clone.1 | convolution fusion | flops 104726528 | bytes 3572736 | tf_op jit(solution)/shard_map/while/body/eval_jaxpr/ngrk,nkd->nrgd/dot_general | solution.py:40
  154.5 0.1 fusion.48
  154.6 0.7 fusion.49
  155.3 0.1 broadcast_maximum_fusion.2
  155.4 0.7 fusion.51
  156.1 0.1 exponential_add_fusion.2
  156.1 1.8 %fusion.52 = bf16[4,1,256,8,64]{2,4,3,1,0:T(8,128)(2,1)S(1)} fusion(bf16[4,1,256,8,64]{2,4,3,1,0:T(8,128)(2,1)S(1)} %get-tuple-element.149, s32[]{:T(128)} %get-tuple-element.148, f32[8,256]{1,0:T(8,128)S(1)} %exponential_add_fusion.2, f32[8,256]{1,0:T(8,128)S(1)} %broadcast_maximum_fusion.2, f32[384,256,8]{1,0,2:T(8,128)S(1)} %get-tuple-element.138, ...), kind=kOutput, calls=%fused_computation.10.clone.1 | convolution fusion | flops 104726528 | bytes 3572736 | tf_op jit(solution)/shard_map/while/body/eval_jaxpr/ngrk,nkd->nrgd/dot_general | solution.py:40
  157.9 0.1 fusion.48
  158.0 0.7 fusion.49
  158.7 0.1 broadcast_maximum_fusion.2
  158.8 0.7 fusion.51
  159.5 0.1 exponential_add_fusion.2
  159.5 1.8 %fusion.52 = bf16[4,1,256,8,64]{2,4,3,1,0:T(8,128)(2,1)S(1)} fusion(bf16[4,1,256,8,64]{2,4,3,1,0:T(8,128)(2,1)S(1)} %get-tuple-element.149, s32[]{:T(128)} %get-tuple-element.148, f32[8,256]{1,0:T(8,128)S(1)} %exponential_add_fusion.2, f32[8,256]{1,0:T(8,128)S(1)} %broadcast_maximum_fusion.2, f32[384,256,8]{1,0,2:T(8,128)S(1)} %get-tuple-element.138, ...), kind=kOutput, calls=%fused_computation.10.clone.1 | convolution fusion | flops 104726528 | bytes 3572736 | tf_op jit(solution)/shard_map/while/body/eval_jaxpr/ngrk,nkd->nrgd/dot_general | solution.py:40
  161.3 1.4 copy.26
  (8 shorter events, 0.1 us)
Async XLA Ops:
  6.5 1.2 copy-start
  6.5 112.1 %all-gather.2.cloned.1.call-start = ((), (), s32[]{:S(2)}) async-start(), calls=%async_computation | async-start | bytes 15544320 | tf_op jit(solution)/shard_map/all_gather | solution.py:71
  130.7 1.1 slice-start
  130.7 6.3 %slice-start.1 = ((f32[256,2560]{1,0:T(8,128)}), f32[256,2048]{1,0:T(8,128)S(1)}, s32[]{:S(2)}) async-start(f32[256,2560]{1,0:T(8,128)} %convolution_add_fusion), calls=%async_computation.2 | async-start | bytes 4194304 | tf_op jit(solution)/shard_map/slice | solution.py:59
  133.8 6.9 %copy-start.1 = (bf16[1,256,256]{2,1,0:T(8,128)(2,1)}, bf16[1,256,256]{2,1,0:T(8,128)(2,1)S(1)}, u32[]{:S(2)}) copy-start(bf16[1,256,256]{2,1,0:T(8,128)(2,1)S(1)} %copy.17) | copy-start | bytes 393220
  134.5 8.8 %collective-permute-start = (bf16[2,128,256]{2,1,0:T(8,128)(2,1)}, bf16[2,128,256]{2,1,0:T(8,128)(2,1)}, u32[]{:S(2)}, u32[]{:S(2)}) collective-permute-start(bf16[2,128,256]{2,1,0:T(8,128)(2,1)} %pad_maximum_fusion), channel_id=1, source_target_pairs={{0,1},{1,2},{2,3},{3,4},{4,5},{5,6},{6,7},{7,8},{8,9},{9,10},{10,1... | collective-permute-start | bytes 393224 | tf_op jit(solution)/shard_map/ppermute | solution.py:15
  138.8 4.4 %copy-start.3 = (bf16[128,256]{1,0:T(8,128)(2,1)S(1)}, bf16[128,256]{1,0:T(8,128)(2,1)}, u32[]{:S(2)}) copy-start(bf16[128,256]{1,0:T(8,128)(2,1)} %param.17) | copy-start | bytes 196612
  138.8 4.4 %copy-start.4 = (bf16[128,256]{1,0:T(8,128)(2,1)S(1)}, bf16[128,256]{1,0:T(8,128)(2,1)}, u32[]{:S(2)}) copy-start(bf16[128,256]{1,0:T(8,128)(2,1)} %param.16) | copy-start | bytes 196612
  140.8 7.0 %copy-start.2 = (bf16[4,1,256,8,64]{2,4,3,1,0:T(8,128)(2,1)S(1)}, bf16[4,1,256,8,64]{2,4,3,1,0:T(8,128)(2,1)}, u32[]{:S(2)}) copy-start(bf16[4,1,256,8,64]{2,4,3,1,0:T(8,128)(2,1)} %custom-call) | copy-start | bytes 3145732
Sparse Core Ops, SparseCore 0:
  10.2 108.3 all-gather.1

commit v3 on v2

--- a/solution.py
+++ b/solution.py
@@ -80,7 +80,7 @@
     key_length = KEY_VALUE_HEADS * HEAD_SIZE
     flat = tokens.astype(jnp.float32)
     scale = lax.rsqrt(jnp.mean(flat * flat, axis=-1, keepdims=True) + 1e-05)
-    normed = (flat * scale * norm_gain[None, :]).astype(jnp.bfloat16)
+    normed = lax.optimization_barrier((flat * scale * norm_gain[None, :]).astype(jnp.bfloat16))
     combined_output = lax.dot_general(
         normed,
         gather_weight(qkv_weight),

time: 170 us -> 163 us (0.959)
  matrix products: 21.8 us -> 17.8 us
    dot_general x1, matrix products: 12.1 us -> 8.05 us  [on_device(): lax.dot_general(normed, gather_weight(qkv_weight), (((1,), (1,)), ((), ()...]
    convert_element_type x0 -> x1, other arithmetic: none -> 2.32 us  [on_device(): (flat * scale * norm_gain[None, :]).astype(jnp.bfloat16)]
  transfers between devices with their start and end apart: 2 -> 2, of which waited for: 2 -> 2; matrix products, arithmetic and copies ran while one was open for 4% -> 5% of each run, Pallas kernels for 0% -> 0%
where the time goes in v3:
time: 163 us
  waiting for transfers between devices  108 us (66%)
  matrix products  17.8 us (11%)
  between operations  13.5 us (8%)
  other arithmetic  11 us (7%)
  local copies, waits for them, and re-layouts  10 us (6%)
  starting transfers between devices  2.51 us (2%)
    all_gather x1, waiting for transfers between devices, gather_weight(): return lax.all_gather(own.T, ('ctx', 'dp'), axis=0, tiled=True)  106 us
    dot_general x1, matrix products, on_device(): lax.dot_general(normed, gather_weight(qkv_weight), (((1,), (1,)), ((), ()...  8.05 us
    dot_general x4, matrix products, attend_head(): jnp.einsum('ngrk,nkd->nrgd', probs, value_rows, preferred_element_type=jn...  7.11 us
  transfers between devices with their start and end apart: 2, of which 2 were waited for; matrix products, arithmetic and copies ran while one was open for 5% of the time, Pallas kernels for 0%

profile of v3, /device:TPU:4, one launch (start us, length us, event | category | flops | bytes accessed | tf_op | source)
XLA Modules:
  0.0 163.0 jit_solution(9684652947211438770)
XLA Ops:
  6.5 0.0 copy-start
  6.5 0.0 copy-start.1
  6.5 0.0 copy-start.6
  6.5 0.0 copy-start.5
  6.5 0.0 copy-start.7
  6.5 0.0 all-gather.2.cloned.1.call-start
  6.6 1.1 copy-done
  7.7 0.8 dynamic-slice_bitcast_fusion
  8.5 0.0 all-gather.2.cloned.1.call-update
  8.6 1.8 %fusion.30 = f32[256]{0:T(256)S(1)} fusion(bf16[256,2880]{0,1:T(8,128)(2,1)} %param.10), kind=kLoop, calls=%fused_computation.33 | loop fusion | flops 2211584 | bytes 1475584 | tf_op jit(solution)/shard_map/reduce_sum | solution.py:82
  10.4 0.0 copy-done.1
  10.4 2.3 %fusion.32 = bf16[256,2880]{0,1:T(8,128)(2,1)} fusion(bf16[256,2880]{0,1:T(8,128)(2,1)S(1)} %copy-done.1, f32[2880]{0:T(1024)} %param.12, f32[256]{0:T(256)S(1)} %add_rsqrt_fusion), kind=kLoop, calls=%fused_computation.35 | loop fusion | flops 2949120 | bytes 2961664 | tf_op jit(solution)/shard_map/convert_element_type | solution.py:83
  12.7 0.0 copy-done.6
  12.7 0.1 reshape.219
  12.8 0.0 copy-done.5
  12.8 0.2 multiply_cosine_fusion
  13.0 105.7 %all-gather.2.cloned.1.call-done = bf16[2560,2880]{1,0:T(8,128)(2,1)} async-done(((bf16[80,2880]{1,0:T(8,128)(2,1)}), bf16[2560,2880]{1,0:T(8,128)(2,1)}) %all-gather.2.cloned.1.call-update) | async-done | bytes 14745616 | tf_op jit(solution)/shard_map/all_gather | solution.py:71
  118.7 0.0 copy-done.7
  118.7 8.1 %convolution_add_fusion = f32[256,2560]{1,0:T(8,128)S(1)} fusion(bf16[256,2880]{0,1:T(8,128)(2,1)} %fusion.32, bf16[2560,2880]{1,0:T(8,128)(2,1)} %all-gather.2.cloned.1.call-done, f32[2560]{0:T(1024)S(1)} %copy-done.7), kind=kOutput, calls=%fused_computation.30 | convolution fusion | flops 3775528960 | bytes 18851840 | tf_op jit(solution)/shard_map/dot_general | solution.py:84
  126.8 0.7 slice.49
  127.5 0.1 slice.55
  127.7 1.1 copy.16
  128.8 0.1 copy.17
  128.9 2.5 %collective-permute-start = (bf16[2,128,256]{2,1,0:T(8,128)(2,1)S(1)}, bf16[2,128,256]{2,1,0:T(8,128)(2,1)}, u32[]{:S(2)}, u32[]{:S(2)}) collective-permute-start(bf16[2,128,256]{2,1,0:T(8,128)(2,1)S(1)} %pad_maximum_fusion), channel_id=1, source_target_pairs={{0,1},{1,2},{2,3},{3,4},{4,5},{5,6},{6,7},{7,8},{8,9},{9,10},{10,1... | collective-permute-start | bytes 393224 | tf_op jit(solution)/shard_map/ppermute | solution.py:15
  131.4 1.9 %copy.20 = f32[256,2048]{0,1:T(8,128)} copy(f32[256,2048]{1,0:T(8,128)S(1)} %slice.55) | data formatting | bytes 4194304 | tf_op jit(solution)/shard_map/slice | solution.py:59
  133.3 0.0 copy-start.3
  133.3 0.0 copy-start.4
  133.3 1.9 %subtract_convert_fusion = (bf16[256,32,32]{0,2,1:T(8,128)(2,1)S(1)}, bf16[256,32,32]{0,2,1:T(8,128)(2,1)S(1)}) fusion(f32[256,32,64]{0,2,1:T(8,128)} %bitcast.107, f32[256,32]{0,1:T(8,128)S(1)} %get-tuple-element.90, f32[256,32]{0,1:T(8,128)S(1)} %get-tuple-element.89), kind=kLoop, calls=%fused_computation.38 | loop fusion | flops 2097152 | bytes 3211264 | tf_op jit(solution)/shard_map/convert.6
  135.2 0.0 copy-start.2
  135.2 0.1 maximum_bitcast_fusion
  135.3 2.2 %collective-permute-done = bf16[2,128,256]{2,1,0:T(8,128)(2,1)} collective-permute-done((bf16[2,128,256]{2,1,0:T(8,128)(2,1)S(1)}, bf16[2,128,256]{2,1,0:T(8,128)(2,1)}, u32[]{:S(2)}, u32[]{:S(2)}) %collective-permute-start) | collective-permute-done | bytes 131104 | tf_op jit(solution)/shard_map/ppermute | solution.py:15
  137.5 0.0 copy-done.3
  137.5 0.0 copy-done.4
  137.5 0.9 maximum_select_fusion
  138.5 0.7 fusion.34
  139.2 1.1 copy.19
  140.3 0.8 copy.18
  141.1 0.0 copy-done.2
  141.1 13.6 %while.11 = (s32[]{:T(128)}, bf16[4,1,256,8,64]{2,4,3,1,0:T(8,128)(2,1)S(1)}, bf16[4,1,384,64]{2,3,1,0:T(8,128)(2,1)}, bf16[4,1,384,64]{2,3,1,0:T(8,128)(2,1)S(1...) while((s32[]{:T(128)}, ...), condition=%wide.region_4.5_spmd.clone, body=%wide.region_1.4_spmd.clone.sunk | while | flops 211390464 | bytes 10538201 | solution.py:116
  141.1 0.1 fusion.46
  141.2 0.7 fusion.47
  141.9 0.1 broadcast_maximum_fusion.2
  141.9 0.7 fusion.49
  142.6 0.1 exponential_add_fusion.2
  142.7 1.8 %fusion.50 = bf16[4,1,256,8,64]{2,4,3,1,0:T(8,128)(2,1)S(1)} fusion(bf16[4,1,256,8,64]{2,4,3,1,0:T(8,128)(2,1)S(1)} %get-tuple-element.149, s32[]{:T(128)} %get-tuple-element.148, f32[8,256]{1,0:T(8,128)S(1)} %exponential_add_fusion.2, f32[8,256]{1,0:T(8,128)S(1)} %broadcast_maximum_fusion.2, f32[384,256,8]{1,0,2:T(8,128)S(1)} %get-tuple-element.138, ...), kind=kOutput, calls=%fused_computation.10.clone.1 | convolution fusion | flops 104726528 | bytes 3572736 | tf_op jit(solution)/shard_map/while/body/eval_jaxpr/ngrk,nkd->nrgd/dot_general | solution.py:40
  144.5 0.1 fusion.46
  144.6 0.7 fusion.47
  145.3 0.1 broadcast_maximum_fusion.2
  145.3 0.7 fusion.49
  146.0 0.1 exponential_add_fusion.2
  146.1 1.8 %fusion.50 = bf16[4,1,256,8,64]{2,4,3,1,0:T(8,128)(2,1)S(1)} fusion(bf16[4,1,256,8,64]{2,4,3,1,0:T(8,128)(2,1)S(1)} %get-tuple-element.149, s32[]{:T(128)} %get-tuple-element.148, f32[8,256]{1,0:T(8,128)S(1)} %exponential_add_fusion.2, f32[8,256]{1,0:T(8,128)S(1)} %broadcast_maximum_fusion.2, f32[384,256,8]{1,0,2:T(8,128)S(1)} %get-tuple-element.138, ...), kind=kOutput, calls=%fused_computation.10.clone.1 | convolution fusion | flops 104726528 | bytes 3572736 | tf_op jit(solution)/shard_map/while/body/eval_jaxpr/ngrk,nkd->nrgd/dot_general | solution.py:40
  147.9 0.1 fusion.46
  148.0 0.7 fusion.47
  148.7 0.1 broadcast_maximum_fusion.2
  148.7 0.7 fusion.49
  149.4 0.1 exponential_add_fusion.2
  149.5 1.8 %fusion.50 = bf16[4,1,256,8,64]{2,4,3,1,0:T(8,128)(2,1)S(1)} fusion(bf16[4,1,256,8,64]{2,4,3,1,0:T(8,128)(2,1)S(1)} %get-tuple-element.149, s32[]{:T(128)} %get-tuple-element.148, f32[8,256]{1,0:T(8,128)S(1)} %exponential_add_fusion.2, f32[8,256]{1,0:T(8,128)S(1)} %broadcast_maximum_fusion.2, f32[384,256,8]{1,0,2:T(8,128)S(1)} %get-tuple-element.138, ...), kind=kOutput, calls=%fused_computation.10.clone.1 | convolution fusion | flops 104726528 | bytes 3572736 | tf_op jit(solution)/shard_map/while/body/eval_jaxpr/ngrk,nkd->nrgd/dot_general | solution.py:40
  151.3 0.1 fusion.46
  151.4 0.7 fusion.47
  152.1 0.1 broadcast_maximum_fusion.2
  152.1 0.7 fusion.49
  152.8 0.1 exponential_add_fusion.2
  152.9 1.8 %fusion.50 = bf16[4,1,256,8,64]{2,4,3,1,0:T(8,128)(2,1)S(1)} fusion(bf16[4,1,256,8,64]{2,4,3,1,0:T(8,128)(2,1)S(1)} %get-tuple-element.149, s32[]{:T(128)} %get-tuple-element.148, f32[8,256]{1,0:T(8,128)S(1)} %exponential_add_fusion.2, f32[8,256]{1,0:T(8,128)S(1)} %broadcast_maximum_fusion.2, f32[384,256,8]{1,0,2:T(8,128)S(1)} %get-tuple-element.138, ...), kind=kOutput, calls=%fused_computation.10.clone.1 | convolution fusion | flops 104726528 | bytes 3572736 | tf_op jit(solution)/shard_map/while/body/eval_jaxpr/ngrk,nkd->nrgd/dot_general | solution.py:40
  154.7 1.4 copy.26
  (13 shorter events, 0.2 us)
Async XLA Ops:
  6.5 1.2 copy-start
  6.5 3.8 %copy-start.1 = (bf16[256,2880]{0,1:T(8,128)(2,1)S(1)}, bf16[256,2880]{0,1:T(8,128)(2,1)}, u32[]{:S(2)}) copy-start(bf16[256,2880]{0,1:T(8,128)(2,1)} %param.10) | copy-start | bytes 4423684
  6.5 6.1 %copy-start.6 = (f32[32]{0:T(128)S(1)}, f32[32]{0:T(128)}, u32[]{:S(2)}) copy-start(f32[32]{0:T(128)} %param.15) | copy-start | bytes 388
  6.5 6.2 %copy-start.5 = (s32[256]{0:T(256)S(1)}, s32[256]{0:T(256)}, u32[]{:S(2)}) copy-start(s32[256]{0:T(256)} %param.11) | copy-start | bytes 3076
  6.5 112.2 %copy-start.7 = (f32[2560]{0:T(1024)S(1)}, f32[2560]{0:T(1024)}, u32[]{:S(2)}) copy-start(f32[2560]{0:T(1024)} %param.14) | copy-start | bytes 30724
  6.5 112.1 %all-gather.2.cloned.1.call-start = ((), (), s32[]{:S(2)}) async-start(), calls=%async_computation | async-start | bytes 15544320 | tf_op jit(solution)/shard_map/all_gather | solution.py:71
  128.9 8.6 %collective-permute-start = (bf16[2,128,256]{2,1,0:T(8,128)(2,1)S(1)}, bf16[2,128,256]{2,1,0:T(8,128)(2,1)}, u32[]{:S(2)}, u32[]{:S(2)}) collective-permute-start(bf16[2,128,256]{2,1,0:T(8,128)(2,1)S(1)} %pad_maximum_fusion), channel_id=1, source_target_pairs={{0,1},{1,2},{2,3},{3,4},{4,5},{5,6},{6,7},{7,8},{8,9},{9,10},{10,1... | collective-permute-start | bytes 393224 | tf_op jit(solution)/shard_map/ppermute | solution.py:15
  133.3 4.2 %copy-start.3 = (bf16[128,256]{1,0:T(8,128)(2,1)S(1)}, bf16[128,256]{1,0:T(8,128)(2,1)}, u32[]{:S(2)}) copy-start(bf16[128,256]{1,0:T(8,128)(2,1)} %param.17) | copy-start | bytes 196612
  133.3 4.2 %copy-start.4 = (bf16[128,256]{1,0:T(8,128)(2,1)S(1)}, bf16[128,256]{1,0:T(8,128)(2,1)}, u32[]{:S(2)}) copy-start(bf16[128,256]{1,0:T(8,128)(2,1)} %param.16) | copy-start | bytes 196612
  135.2 5.9 %copy-start.2 = (bf16[4,1,256,8,64]{2,4,3,1,0:T(8,128)(2,1)S(1)}, bf16[4,1,256,8,64]{2,4,3,1,0:T(8,128)(2,1)}, u32[]{:S(2)}) copy-start(bf16[4,1,256,8,64]{2,4,3,1,0:T(8,128)(2,1)} %custom-call) | copy-start | bytes 3145732
Sparse Core Ops, SparseCore 0:
  10.3 108.3 all-gather.1

commit v4 on v3

--- a/solution.py
+++ b/solution.py
@@ -1,6 +1,8 @@
 import jax
 import jax.numpy as jnp
 from jax import lax
+from jax.experimental import pallas as pl
+from jax.experimental.pallas import tpu as pltpu
 from jax.sharding import PartitionSpec as P
 
 QUERY_HEADS = 32
@@ -39,6 +41,94 @@
     probs = (expo / total[..., None]).astype(jnp.bfloat16)
     out = jnp.einsum("ngrk,nkd->nrgd", probs, value_rows, preferred_element_type=jnp.float32)
     return out.astype(jnp.bfloat16)
+
+
+def attention_kernel(sinks_ref, limit_ref, cos_ref, sin_ref, q_ref, k_ref, v_ref, out_ref):
+    group = pl.program_id(0)
+    rows = q_ref.shape[0]
+    query_group = q_ref.shape[1] // HEAD_SIZE
+    half = HEAD_SIZE // 2
+    lanes = cos_ref.shape[1]
+    cosine = cos_ref[...]
+    sine = sin_ref[...]
+    lane = lax.broadcasted_iota(jnp.int32, (rows, lanes), 1)
+    source = pltpu.roll(lane, half, 1)
+    partner_lane = jnp.where(lane % HEAD_SIZE < half, lane + half, lane - half)
+    take_first = source == partner_lane
+    block = WINDOW_TOKENS
+    query_index = lax.broadcasted_iota(jnp.int32, (block, 2 * block), 0)
+    key_index = lax.broadcasted_iota(jnp.int32, (block, 2 * block), 1)
+    rel = query_index - key_index + block
+    visible = []
+    for part in range(rows // block):
+        limit = limit_ref[part * block : (part + 1) * block, :]
+        visible.append((rel >= 0) & (rel <= limit))
+    heads_per_chunk = lanes // HEAD_SIZE
+    for chunk in range(q_ref.shape[1] // lanes):
+        x = q_ref[:, chunk * lanes : (chunk + 1) * lanes]
+        first = pltpu.roll(x, half, 1)
+        second = pltpu.roll(x, lanes - half, 1)
+        partner = jnp.where(take_first, first, second)
+        rotated = (x * cosine + partner * sine).astype(jnp.bfloat16)
+        for inner in range(heads_per_chunk):
+            head = chunk * heads_per_chunk + inner
+            sink = sinks_ref[group * query_group + head]
+            query_head = rotated[:, inner * HEAD_SIZE : (inner + 1) * HEAD_SIZE]
+            for part in range(rows // block):
+                queries = query_head[part * block : (part + 1) * block]
+                keys = k_ref[0, part * block : part * block + 2 * block, :]
+                values = v_ref[0, part * block : part * block + 2 * block, :]
+                scores = lax.dot_general(
+                    queries, keys, (((1,), (1,)), ((), ())), preferred_element_type=jnp.float32
+                ) * HEAD_SIZE ** (-0.5)
+                scores = jnp.where(visible[part], scores, -1e30)
+                top = jnp.maximum(jnp.max(scores, axis=1, keepdims=True), sink)
+                expo = jnp.exp(scores - top)
+                total = jnp.sum(expo, axis=1, keepdims=True) + jnp.exp(sink - top)
+                probs = (expo / total).astype(jnp.bfloat16)
+                out = jnp.dot(probs, values, preferred_element_type=jnp.float32)
+                out_ref[part * block : (part + 1) * block, head * HEAD_SIZE : (head + 1) * HEAD_SIZE] = out.astype(
+                    jnp.bfloat16
+                )
+
+
+def rotation_tables(positions, lanes):
+    half = HEAD_SIZE // 2
+    freq = 150000.0 ** (-(jnp.arange(half, dtype=jnp.float32) * 2.0 / HEAD_SIZE))
+    angle = positions.astype(jnp.float32)[:, None] * freq[None, :]
+    cosine = jnp.cos(angle)
+    sine = jnp.sin(angle)
+    repeats = lanes // HEAD_SIZE
+    cos_table = jnp.tile(jnp.concatenate([cosine, cosine], axis=1), (1, repeats))
+    sin_table = jnp.tile(jnp.concatenate([-sine, sine], axis=1), (1, repeats))
+    return cos_table, sin_table
+
+
+def attend(combined_output, joined_keys, joined_values, positions, sinks):
+    token_rows = combined_output.shape[0]
+    query_group = QUERY_HEADS // KEY_VALUE_HEADS
+    group_width = query_group * HEAD_SIZE
+    lanes = 128
+    cos_table, sin_table = rotation_tables(positions, lanes)
+    limit = jnp.minimum(positions, WINDOW_TOKENS - 1).astype(jnp.int32)[:, None]
+    keys = jnp.moveaxis(joined_keys, 1, 0)
+    values = jnp.moveaxis(joined_values, 1, 0)
+    key_rows = keys.shape[1]
+    return pl.pallas_call(
+        attention_kernel,
+        grid=(KEY_VALUE_HEADS,),
+        in_specs=[
+            pl.BlockSpec(memory_space=pltpu.SMEM),
+            pl.BlockSpec((token_rows, 1), lambda g: (0, 0)),
+            pl.BlockSpec((token_rows, lanes), lambda g: (0, 0)),
+            pl.BlockSpec((token_rows, lanes), lambda g: (0, 0)),
+            pl.BlockSpec((token_rows, group_width), lambda g: (0, g)),
+            pl.BlockSpec((1, key_rows, HEAD_SIZE), lambda g: (g, 0, 0)),
+            pl.BlockSpec((1, key_rows, HEAD_SIZE), lambda g: (g, 0, 0)),
+        ],
+        out_specs=pl.BlockSpec((token_rows, group_width), lambda g: (0, g)),
+        out_shape=jax.ShapeDtypeStruct((token_rows, QUERY_HEADS * HEAD_SIZE), jnp.bfloat16),
+    )(sinks, limit, cos_table, sin_table, combined_output, keys, values)
 
 
 def send_rim(window_output, token_rows):
@@ -88,41 +178,21 @@
         preferred_element_type=jnp.float32,
     )
     combined_output = combined_output + qkv_bias[None, :]
-    window_output, received, query_rows = split_mixed(
-        combined_output, positions, token_rows, query_length, key_length
-    )
+    key_rows = apply_rotation(
+        combined_output[:, query_length : query_length + key_length].reshape(
+            token_rows, KEY_VALUE_HEADS, HEAD_SIZE
+        ),
+        positions,
+    ).astype(jnp.bfloat16)
+    value_rows = combined_output[:, query_length + key_length :].astype(jnp.bfloat16)
+    window_output = jnp.stack([key_rows.reshape(token_rows, key_length), value_rows])
+    received = send_rim(window_output, token_rows)
     prior = jnp.stack([earlier_keys, earlier_values])
     border_tokens = jnp.where(lax.axis_index("ctx") == 0, prior, received)
     padded_rows = jnp.concatenate([border_tokens, window_output], axis=1).reshape(
         2, WINDOW_TOKENS + token_rows, KEY_VALUE_HEADS, HEAD_SIZE
     )
-    joined_keys = padded_rows[0]
-    joined_values = padded_rows[1]
-    limit = jnp.minimum(positions, WINDOW_TOKENS - 1)
-    sink_tokens = sinks.reshape(KEY_VALUE_HEADS, query_group)
-    rel = (
-        jnp.arange(token_rows, dtype=jnp.int32)[:, None]
-        - jnp.arange(WINDOW_TOKENS + token_rows, dtype=jnp.int32)[None, :]
-        + WINDOW_TOKENS
-    )
-    visible = ((rel >= 0) & (rel <= limit[:, None]))[None]
-    query_blocks = query_rows.reshape(1, token_rows, KEY_VALUE_HEADS, query_group, HEAD_SIZE)
-    window_keys = joined_keys[None]
-    window_values = joined_values[None]
-
-    def one_head(items):
-        return attend_head(items[0], items[1], items[2], items[3], visible)
-
-    out = lax.map(
-        one_head,
-        (
-            jnp.moveaxis(query_blocks, 2, 0),
-            jnp.moveaxis(window_keys, 2, 0),
-            jnp.moveaxis(window_values, 2, 0),
-            sink_tokens,
-        ),
-    )
-    return jnp.moveaxis(out, 0, 2).reshape(token_rows, query_length)
+    return attend(combined_output, padded_rows[0], padded_rows[1], positions, sinks)
 
 
 def solution(mesh):

time: 163 us -> 159 us (0.975)
  Pallas kernels: 0 us -> 12.6 us
  matrix products: 17.8 us -> 8.05 us
  other arithmetic: 11 us -> 3.71 us
  waiting for transfers between devices: 108 us -> 110 us
  local copies, waits for them, and re-layouts: 10 us -> 8.25 us
    pallas_call x0 -> x1, Pallas kernels: none -> 12.6 us  [attend(): pl.pallas_call(attention_kernel, grid=(KEY_VALUE_HEADS,), in_specs=[pl.Bl...]
    dot_general x8 -> x0, matrix products: 9.78 us -> none  [the longest x4 7.11 us: attend_head(): jnp.einsum('ngrk,nkd->nrgd', probs, value_rows, preferred_element_type=jn...]
    slice x7 -> x5, local copies, waits for them, and re-layouts: 6.42 us -> 0.5 us  [the longest x2 0.19 us: on_device(): padded_rows[1]]
    reduce_sum x4 -> x0, other arithmetic: 2.67 us -> none  [attend_head(): total = jnp.sum(expo, axis=-1) + jnp.exp(sink_row[None, :, None] - top)]
    another operation x3 -> x2, other arithmetic: 1.96 us -> 0.05 us
    squeeze x0 -> x2, local copies, waits for them, and re-layouts: none -> 1.88 us  [the longest x1 0.96 us: on_device(): padded_rows[0]]
  transfers between devices with their start and end apart: 2 -> 2, of which waited for: 2 -> 2; matrix products, arithmetic and copies ran while one was open for 5% -> 4% of each run, Pallas kernels for 0% -> 0%
where the time goes in v4:
time: 159 us
  waiting for transfers between devices  110 us (69%)
  between operations  13.6 us (9%)
  Pallas kernels  12.6 us (8%)
  local copies, waits for them, and re-layouts  8.25 us (5%)
  matrix products  8.05 us (5%)
  other arithmetic  3.71 us (2%)
  starting transfers between devices  2.47 us (2%)
    all_gather x1, waiting for transfers between devices, gather_weight(): return lax.all_gather(own.T, ('ctx', 'dp'), axis=0, tiled=True)  106 us
    pallas_call x1, Pallas kernels, attend(): pl.pallas_call(attention_kernel, grid=(KEY_VALUE_HEADS,), in_specs=[pl.Bl...  12.6 us
    dot_general x1, matrix products, on_device(): lax.dot_general(normed, gather_weight(qkv_weight), (((1,), (1,)), ((), ()...  8.05 us
    ppermute x1, waiting for transfers between devices, shifted(): lax.ppermute(value, axis, [(source, source + steps) for source in range(l...  3.64 us
  transfers between devices with their start and end apart: 2, of which 2 were waited for; matrix products, arithmetic and copies ran while one was open for 4% of the time, Pallas kernels for 0%

profile of v4, /device:TPU:4, one launch (start us, length us, event | category | flops | bytes accessed | tf_op | source)
XLA Modules:
  0.0 158.8 jit_solution(9482832565052817810)
XLA Ops:
  6.5 0.0 copy-start
  6.5 0.0 copy-start.1
  6.5 0.0 copy-start.5
  6.5 0.0 all-gather.2.cloned.1.call-start
  6.6 1.2 copy-done
  7.7 0.8 dynamic-slice_bitcast_fusion
  8.5 0.0 copy-start.6
  8.5 0.0 copy-start.7
  8.5 0.0 all-gather.2.cloned.1.call-update
  8.6 1.8 %fusion = f32[256]{0:T(256)S(1)} fusion(bf16[256,2880]{0,1:T(8,128)(2,1)} %param.8), kind=kLoop, calls=%fused_computation.3 | loop fusion | flops 2211584 | bytes 1475584 | tf_op jit(solution)/shard_map/reduce_sum | solution.py:172
  10.4 0.0 copy-done.1
  10.4 0.0 copy-done.5
  10.4 1.6 %fusion.2 = bf16[256,2880]{0,1:T(8,128)(2,1)} fusion(bf16[256,2880]{0,1:T(8,128)(2,1)S(1)} %copy-done.1, f32[2880]{0:T(1024)S(1)} %copy-done.5, f32[256]{0:T(256)S(1)} %add_rsqrt_fusion), kind=kLoop, calls=%fused_computation.5 | loop fusion | flops 2949120 | bytes 2961664 | tf_op jit(solution)/shard_map/convert_element_type | solution.py:173
  12.0 0.0 copy-done.6
  12.0 0.2 fusion.4
  12.2 106.4 %all-gather.2.cloned.1.call-done = bf16[2560,2880]{1,0:T(8,128)(2,1)} async-done(((bf16[80,2880]{1,0:T(8,128)(2,1)}), bf16[2560,2880]{1,0:T(8,128)(2,1)}) %all-gather.2.cloned.1.call-update) | async-done | bytes 14745616 | tf_op jit(solution)/shard_map/all_gather | solution.py:161
  118.6 0.0 copy-done.7
  118.6 8.1 %convolution_add_fusion.q_ref = f32[256,2560]{1,0:T(8,128)S(1)} fusion(bf16[256,2880]{0,1:T(8,128)(2,1)} %fusion.2, bf16[2560,2880]{1,0:T(8,128)(2,1)} %all-gather.2.cloned.1.call-done, f32[2560]{0:T(1024)S(1)} %copy-done.7), kind=kOutput, calls=%fused_computation | convolution fusion | flops 3775528960 | bytes 18851840 | tf_op jit(solution)/shard_map/dot_general | solution.py:174
  126.7 0.0 copy-start.2
  126.7 0.0 copy-start.3
  126.7 0.0 copy-start.4
  126.7 1.4 copy-done.2
  128.2 0.1 copy.9
  128.4 0.1 copy.10
  128.5 2.5 %collective-permute-start = (bf16[2,128,256]{2,1,0:T(8,128)(2,1)S(1)}, bf16[2,128,256]{2,1,0:T(8,128)(2,1)S(1)}, u32[]{:S(2)}, u32[]{:S(2)}) collective-permute-start(bf16[2,128,256]{2,1,0:T(8,128)(2,1)S(1)} %pad_maximum_fusion), channel_id=1, source_target_pairs={{0,1},{1,2},{2,3},{3,4},{4,5},{5,6},{6,7},{7,8},{8,9},{9,10},{10,1... | collective-permute-start | bytes 393224 | tf_op jit(solution)/shard_map/ppermute | solution.py:17
  131.0 0.7 copy.16.cos_ref
  131.8 0.7 copy.17.sin_ref
  132.6 0.8 copy.15.limit_ref
  133.3 3.6 %collective-permute-done = bf16[2,128,256]{2,1,0:T(8,128)(2,1)S(1)} collective-permute-done((bf16[2,128,256]{2,1,0:T(8,128)(2,1)S(1)}, bf16[2,128,256]{2,1,0:T(8,128)(2,1)S(1)}, u32[]{:S(2)}, u32[]{:S(2)}) %collective-permute-start) | collective-permute-done | bytes 131104 | tf_op jit(solution)/shard_map/ppermute | solution.py:17
  137.0 0.0 copy-done.3
  137.0 0.0 copy-done.4
  137.1 0.2 copy.11
  137.3 1.0 copy.12
  138.2 0.2 copy.13
  138.4 0.9 copy.14
  139.3 12.6 %shard_map.82 = bf16[256,2048]{1,0:T(8,128)(2,1)} custom-call(f32[32]{0:T(128)} %sinks_ref.1, s32[256,1]{1,0:T(8,128)} %copy.15.limit_ref, f32[256,128]{1,0:T(8,128)} %copy.16.cos_ref, f32[256,128]{1,0:T(8,128)} %copy.17.sin_ref, f32[256,2560]{1,0:T(8,128)} %copy-done.2, bf16[4,384,64]{2,1,0:T(8,128)(2,1)} %bitcast.17, bf16[4,384,64]{2,1,0:T(8,128)(2,1)} %bitcast.18), custom_call_target="tpu_custom_call" | custom-call | tf_op jit(solution)/shard_map/pallas_call | solution.py:117
  (14 shorter events, 0.2 us)
Async XLA Ops:
  6.5 1.2 copy-start
  6.5 3.8 %copy-start.1 = (bf16[256,2880]{0,1:T(8,128)(2,1)S(1)}, bf16[256,2880]{0,1:T(8,128)(2,1)}, u32[]{:S(2)}) copy-start(bf16[256,2880]{0,1:T(8,128)(2,1)} %param.8) | copy-start | bytes 4423684
  6.5 3.8 %copy-start.5 = (f32[2880]{0:T(1024)S(1)}, f32[2880]{0:T(1024)}, u32[]{:S(2)}) copy-start(f32[2880]{0:T(1024)} %param.10) | copy-start | bytes 34564
  6.5 112.1 %all-gather.2.cloned.1.call-start = ((), (), s32[]{:S(2)}) async-start(), calls=%async_computation | async-start | bytes 15544320 | tf_op jit(solution)/shard_map/all_gather | solution.py:161
  8.5 3.4 %copy-start.6 = (s32[256]{0:T(256)S(1)}, s32[256]{0:T(256)}, u32[]{:S(2)}) copy-start(s32[256]{0:T(256)} %param.9) | copy-start | bytes 3076
  8.5 110.1 %copy-start.7 = (f32[2560]{0:T(1024)S(1)}, f32[2560]{0:T(1024)}, u32[]{:S(2)}) copy-start(f32[2560]{0:T(1024)} %param.12) | copy-start | bytes 30724
  126.7 1.5 copy-start.2
  126.7 10.3 %copy-start.3 = (bf16[128,256]{1,0:T(8,128)(2,1)S(1)}, bf16[128,256]{1,0:T(8,128)(2,1)}, u32[]{:S(2)}) copy-start(bf16[128,256]{1,0:T(8,128)(2,1)} %param.15) | copy-start | bytes 196612
  126.7 10.3 %copy-start.4 = (bf16[128,256]{1,0:T(8,128)(2,1)S(1)}, bf16[128,256]{1,0:T(8,128)(2,1)}, u32[]{:S(2)}) copy-start(bf16[128,256]{1,0:T(8,128)(2,1)} %param.14) | copy-start | bytes 196612
  128.5 8.5 %collective-permute-start = (bf16[2,128,256]{2,1,0:T(8,128)(2,1)S(1)}, bf16[2,128,256]{2,1,0:T(8,128)(2,1)S(1)}, u32[]{:S(2)}, u32[]{:S(2)}) collective-permute-start(bf16[2,128,256]{2,1,0:T(8,128)(2,1)S(1)} %pad_maximum_fusion), channel_id=1, source_target_pairs={{0,1},{1,2},{2,3},{3,4},{4,5},{5,6},{6,7},{7,8},{8,9},{9,10},{10,1... | collective-permute-start | bytes 393224 | tf_op jit(solution)/shard_map/ppermute | solution.py:17
Sparse Core Ops, SparseCore 0:
  10.2 108.3 all-gather.1

commit v5 on v4

--- a/solution.py
+++ b/solution.py
@@ -104,13 +104,12 @@
     return cos_table, sin_table
 
 
-def attend(combined_output, joined_keys, joined_values, positions, sinks):
+def attend(combined_output, joined_keys, joined_values, tables, sinks):
     token_rows = combined_output.shape[0]
     query_group = QUERY_HEADS // KEY_VALUE_HEADS
     group_width = query_group * HEAD_SIZE
-    lanes = 128
-    cos_table, sin_table = rotation_tables(positions, lanes)
-    limit = jnp.minimum(positions, WINDOW_TOKENS - 1).astype(jnp.int32)[:, None]
+    cos_table, sin_table, limit = tables
+    lanes = cos_table.shape[1]
     keys = jnp.moveaxis(joined_keys, 1, 0)
     values = jnp.moveaxis(joined_values, 1, 0)
     key_rows = keys.shape[1]
@@ -170,7 +169,11 @@
     key_length = KEY_VALUE_HEADS * HEAD_SIZE
     flat = tokens.astype(jnp.float32)
     scale = lax.rsqrt(jnp.mean(flat * flat, axis=-1, keepdims=True) + 1e-05)
-    normed = lax.optimization_barrier((flat * scale * norm_gain[None, :]).astype(jnp.bfloat16))
+    normed = (flat * scale * norm_gain[None, :]).astype(jnp.bfloat16)
+    tables = rotation_tables(positions, 128) + (
+        jnp.minimum(positions, WINDOW_TOKENS - 1).astype(jnp.int32)[:, None],
+    )
+    normed, tables = lax.optimization_barrier((normed, tables))
     combined_output = lax.dot_general(
         normed,
         gather_weight(qkv_weight),
@@ -192,7 +195,7 @@
     padded_rows = jnp.concatenate([border_tokens, window_output], axis=1).reshape(
         2, WINDOW_TOKENS + token_rows, KEY_VALUE_HEADS, HEAD_SIZE
     )
-    return attend(combined_output, padded_rows[0], padded_rows[1], positions, sinks)
+    return attend(combined_output, padded_rows[0], padded_rows[1], tables, sinks)
 
 
 def solution(mesh):

time: 159 us -> 159 us (level)
    optimization_barrier x0 -> x3, local copies, waits for them, and re-layouts: none -> 2.28 us  [on_device(): normed, tables = lax.optimization_barrier((normed, tables))]
  transfers between devices with their start and end apart: 2 -> 2, of which waited for: 2 -> 2; matrix products, arithmetic and copies ran while one was open for 4% -> 3% of each run, Pallas kernels for 0% -> 0%
where the time goes in v5:
time: 159 us
  waiting for transfers between devices  111 us (70%)
  between operations  13.6 us (9%)
  Pallas kernels  12.6 us (8%)
  local copies, waits for them, and re-layouts  8.25 us (5%)
  matrix products  8.05 us (5%)
  other arithmetic  3.1 us (2%)
  starting transfers between devices  2.47 us (2%)
    all_gather x1, waiting for transfers between devices, gather_weight(): return lax.all_gather(own.T, ('ctx', 'dp'), axis=0, tiled=True)  107 us
    pallas_call x1, Pallas kernels, attend(): pl.pallas_call(attention_kernel, grid=(KEY_VALUE_HEADS,), in_specs=[pl.Bl...  12.6 us
    dot_general x1, matrix products, on_device(): lax.dot_general(normed, gather_weight(qkv_weight), (((1,), (1,)), ((), ()...  8.05 us
    ppermute x1, waiting for transfers between devices, shifted(): lax.ppermute(value, axis, [(source, source + steps) for source in range(l...  3.69 us
  transfers between devices with their start and end apart: 2, of which 2 were waited for; matrix products, arithmetic and copies ran while one was open for 3% of the time, Pallas kernels for 0%

profile of v5, /device:TPU:4, one launch (start us, length us, event | category | flops | bytes accessed | tf_op | source)
XLA Modules:
  0.0 158.8 jit_solution(165349598805127870)
XLA Ops:
  6.5 0.0 copy-start
  6.5 0.0 copy-start.1
  6.5 0.0 copy-start.5
  6.5 0.0 all-gather.2.cloned.1.call-start
  6.6 1.2 copy-done
  7.7 0.8 dynamic-slice_bitcast_fusion
  8.5 0.0 all-gather.2.cloned.1.call-update
  8.6 0.0 copy-start.6
  8.6 0.8 broadcast_minimum_fusion
  9.3 0.2 fusion.4
  9.6 0.0 copy-done.1
  9.6 0.4 fusion
  10.0 0.0 copy-done.5
  10.0 1.6 %fusion.2 = bf16[256,2880]{0,1:T(8,128)(2,1)} fusion(bf16[256,2880]{0,1:T(8,128)(2,1)S(1)} %copy-done.1, f32[2880]{0:T(1024)S(1)} %copy-done.5, f32[256]{0:T(256)S(1)} %add_rsqrt_fusion), kind=kLoop, calls=%fused_computation.5 | loop fusion | flops 2949120 | bytes 2961664 | tf_op jit(solution)/shard_map/convert_element_type | solution.py:172
  11.6 107.0 %all-gather.2.cloned.1.call-done = bf16[2560,2880]{1,0:T(8,128)(2,1)} async-done(((bf16[80,2880]{1,0:T(8,128)(2,1)}), bf16[2560,2880]{1,0:T(8,128)(2,1)}) %all-gather.2.cloned.1.call-update) | async-done | bytes 14745616 | tf_op jit(solution)/shard_map/all_gather | solution.py:160
  118.6 0.0 copy-done.6
  118.6 8.1 %convolution_add_fusion.q_ref = f32[256,2560]{1,0:T(8,128)S(1)} fusion(bf16[256,2880]{0,1:T(8,128)(2,1)} %fusion.2, bf16[2560,2880]{1,0:T(8,128)(2,1)} %all-gather.2.cloned.1.call-done, f32[2560]{0:T(1024)S(1)} %copy-done.6), kind=kOutput, calls=%fused_computation | convolution fusion | flops 3775528960 | bytes 18851840 | tf_op jit(solution)/shard_map/dot_general | solution.py:177
  126.7 0.0 copy-start.2
  126.7 0.0 copy-start.3
  126.7 0.0 copy-start.4
  126.7 1.4 copy-done.2
  128.2 0.1 copy.9
  128.4 0.1 copy.10
  128.5 2.5 %collective-permute-start = (bf16[2,128,256]{2,1,0:T(8,128)(2,1)S(1)}, bf16[2,128,256]{2,1,0:T(8,128)(2,1)S(1)}, u32[]{:S(2)}, u32[]{:S(2)}) collective-permute-start(bf16[2,128,256]{2,1,0:T(8,128)(2,1)S(1)} %pad_maximum_fusion), channel_id=1, source_target_pairs={{0,1},{1,2},{2,3},{3,4},{4,5},{5,6},{6,7},{7,8},{8,9},{9,10},{10,1... | collective-permute-start | bytes 393224 | tf_op jit(solution)/shard_map/ppermute | solution.py:17
  131.0 0.8 copy.15.limit_ref
  131.8 0.7 copy.16.cos_ref
  132.6 0.7 copy.17.sin_ref
  133.3 3.7 %collective-permute-done = bf16[2,128,256]{2,1,0:T(8,128)(2,1)S(1)} collective-permute-done((bf16[2,128,256]{2,1,0:T(8,128)(2,1)S(1)}, bf16[2,128,256]{2,1,0:T(8,128)(2,1)S(1)}, u32[]{:S(2)}, u32[]{:S(2)}) %collective-permute-start) | collective-permute-done | bytes 131104 | tf_op jit(solution)/shard_map/ppermute | solution.py:17
  137.0 0.0 copy-done.3
  137.0 0.0 copy-done.4
  137.1 0.2 copy.13
  137.3 0.9 copy.14
  138.2 0.2 copy.11
  138.4 1.0 copy.12
  139.3 12.6 %shard_map.82 = bf16[256,2048]{1,0:T(8,128)(2,1)} custom-call(f32[32]{0:T(128)} %sinks_ref.1, s32[256,1]{1,0:T(8,128)} %copy.15.limit_ref, f32[256,128]{1,0:T(8,128)} %copy.16.cos_ref, f32[256,128]{1,0:T(8,128)} %copy.17.sin_ref, f32[256,2560]{1,0:T(8,128)} %copy-done.2, bf16[4,384,64]{2,1,0:T(8,128)(2,1)} %bitcast.18, bf16[4,384,64]{2,1,0:T(8,128)(2,1)} %bitcast.17), custom_call_target="tpu_custom_call" | custom-call | tf_op jit(solution)/shard_map/pallas_call | solution.py:116
  (13 shorter events, 0.2 us)
Async XLA Ops:
  6.5 1.2 copy-start
  6.5 3.0 %copy-start.1 = (bf16[256,2880]{0,1:T(8,128)(2,1)S(1)}, bf16[256,2880]{0,1:T(8,128)(2,1)}, u32[]{:S(2)}) copy-start(bf16[256,2880]{0,1:T(8,128)(2,1)} %param.8) | copy-start | bytes 4423684
  6.5 3.5 %copy-start.5 = (f32[2880]{0:T(1024)S(1)}, f32[2880]{0:T(1024)}, u32[]{:S(2)}) copy-start(f32[2880]{0:T(1024)} %param.10) | copy-start | bytes 34564
  6.5 112.1 %all-gather.2.cloned.1.call-start = ((), (), s32[]{:S(2)}) async-start(), calls=%async_computation | async-start | bytes 15544320 | tf_op jit(solution)/shard_map/all_gather | solution.py:160
  8.6 110.1 %copy-start.6 = (f32[2560]{0:T(1024)S(1)}, f32[2560]{0:T(1024)}, u32[]{:S(2)}) copy-start(f32[2560]{0:T(1024)} %param.12) | copy-start | bytes 30724
  126.7 1.5 copy-start.2
  126.7 10.3 %copy-start.3 = (bf16[128,256]{1,0:T(8,128)(2,1)S(1)}, bf16[128,256]{1,0:T(8,128)(2,1)}, u32[]{:S(2)}) copy-start(bf16[128,256]{1,0:T(8,128)(2,1)} %param.15) | copy-start | bytes 196612
  126.7 10.3 %copy-start.4 = (bf16[128,256]{1,0:T(8,128)(2,1)S(1)}, bf16[128,256]{1,0:T(8,128)(2,1)}, u32[]{:S(2)}) copy-start(bf16[128,256]{1,0:T(8,128)(2,1)} %param.14) | copy-start | bytes 196612
  128.5 8.5 %collective-permute-start = (bf16[2,128,256]{2,1,0:T(8,128)(2,1)S(1)}, bf16[2,128,256]{2,1,0:T(8,128)(2,1)S(1)}, u32[]{:S(2)}, u32[]{:S(2)}) collective-permute-start(bf16[2,128,256]{2,1,0:T(8,128)(2,1)S(1)} %pad_maximum_fusion), channel_id=1, source_target_pairs={{0,1},{1,2},{2,3},{3,4},{4,5},{5,6},{6,7},{7,8},{8,9},{9,10},{10,1... | collective-permute-start | bytes 393224 | tf_op jit(solution)/shard_map/ppermute | solution.py:17
Sparse Core Ops, SparseCore 0:
  10.2 108.3 all-gather.1

commit v6 on v5

--- a/solution.py
+++ b/solution.py
@@ -64,6 +64,7 @@
         limit = limit_ref[part * block : (part + 1) * block, :]
         visible.append((rel >= 0) & (rel <= limit))
     heads_per_chunk = lanes // HEAD_SIZE
+    rotated_heads = []
     for chunk in range(q_ref.shape[1] // lanes):
         x = q_ref[:, chunk * lanes : (chunk + 1) * lanes]
         first = pltpu.roll(x, half, 1)
@@ -71,25 +72,31 @@
         partner = jnp.where(take_first, first, second)
         rotated = (x * cosine + partner * sine).astype(jnp.bfloat16)
         for inner in range(heads_per_chunk):
-            head = chunk * heads_per_chunk + inner
-            sink = sinks_ref[group * query_group + head]
-            query_head = rotated[:, inner * HEAD_SIZE : (inner + 1) * HEAD_SIZE]
-            for part in range(rows // block):
-                queries = query_head[part * block : (part + 1) * block]
-                keys = k_ref[0, part * block : part * block + 2 * block, :]
-                values = v_ref[0, part * block : part * block + 2 * block, :]
-                scores = lax.dot_general(
-                    queries, keys, (((1,), (1,)), ((), ())), preferred_element_type=jnp.float32
-                ) * HEAD_SIZE ** (-0.5)
-                scores = jnp.where(visible[part], scores, -1e30)
-                top = jnp.maximum(jnp.max(scores, axis=1, keepdims=True), sink)
-                expo = jnp.exp(scores - top)
-                total = jnp.sum(expo, axis=1, keepdims=True) + jnp.exp(sink - top)
-                probs = (expo / total).astype(jnp.bfloat16)
-                out = jnp.dot(probs, values, preferred_element_type=jnp.float32)
-                out_ref[part * block : (part + 1) * block, head * HEAD_SIZE : (head + 1) * HEAD_SIZE] = out.astype(
-                    jnp.bfloat16
-                )
+            rotated_heads.append(rotated[:, inner * HEAD_SIZE : (inner + 1) * HEAD_SIZE])
+    sink_rows = jnp.concatenate(
+        [jnp.full((block, 1), sinks_ref[group * query_group + head], jnp.float32) for head in range(query_group)],
+        axis=0,
+    )
+    for part in range(rows // block):
+        queries = jnp.concatenate(
+            [head_rows[part * block : (part + 1) * block] for head_rows in rotated_heads], axis=0
+        )
+        keys = k_ref[0, part * block : part * block + 2 * block, :]
+        values = v_ref[0, part * block : part * block + 2 * block, :]
+        scores = lax.dot_general(
+            queries, keys, (((1,), (1,)), ((), ())), preferred_element_type=jnp.float32
+        ) * HEAD_SIZE ** (-0.5)
+        seen = jnp.concatenate([visible[part]] * query_group, axis=0)
+        scores = jnp.where(seen, scores, -1e30)
+        top = jnp.maximum(jnp.max(scores, axis=1, keepdims=True), sink_rows)
+        expo = jnp.exp(scores - top)
+        total = jnp.sum(expo, axis=1, keepdims=True) + jnp.exp(sink_rows - top)
+        probs = (expo / total).astype(jnp.bfloat16)
+        out = jnp.dot(probs, values, preferred_element_type=jnp.float32).astype(jnp.bfloat16)
+        for head in range(query_group):
+            out_ref[part * block : (part + 1) * block, head * HEAD_SIZE : (head + 1) * HEAD_SIZE] = out[
+                head * block : (head + 1) * block
+            ]
 
 
 def rotation_tables(positions, lanes):

time: 159 us -> 160 us (level)
  no operation moved by 1% of the time
where the time goes in v6:
time: 160 us
  waiting for transfers between devices  111 us (69%)
  Pallas kernels  13.9 us (9%)
  between operations  13.6 us (8%)
  local copies, waits for them, and re-layouts  8.25 us (5%)
  matrix products  8.05 us (5%)
  other arithmetic  3.1 us (2%)
  starting transfers between devices  2.47 us (2%)
    all_gather x1, waiting for transfers between devices, gather_weight(): return lax.all_gather(own.T, ('ctx', 'dp'), axis=0, tiled=True)  107 us
    pallas_call x1, Pallas kernels, attend(): pl.pallas_call(attention_kernel, grid=(KEY_VALUE_HEADS,), in_specs=[pl.Bl...  13.9 us
    dot_general x1, matrix products, on_device(): lax.dot_general(normed, gather_weight(qkv_weight), (((1,), (1,)), ((), ()...  8.05 us
    ppermute x1, waiting for transfers between devices, shifted(): lax.ppermute(value, axis, [(source, source + steps) for source in range(l...  3.69 us
  transfers between devices with their start and end apart: 2, of which 2 were waited for; matrix products, arithmetic and copies ran while one was open for 3% of the time, Pallas kernels for 0%

profile of v6, /device:TPU:4, one launch (start us, length us, event | category | flops | bytes accessed | tf_op | source)
XLA Modules:
  0.0 160.0 jit_solution(16694805201325277923)
XLA Ops:
  6.5 0.0 copy-start
  6.5 0.0 copy-start.1
  6.5 0.0 copy-start.5
  6.5 0.0 all-gather.2.cloned.1.call-start
  6.6 1.2 copy-done
  7.7 0.8 dynamic-slice_bitcast_fusion
  8.5 0.0 all-gather.2.cloned.1.call-update
  8.6 0.0 copy-start.6
  8.6 0.8 broadcast_minimum_fusion
  9.3 0.2 fusion.4
  9.6 0.0 copy-done.1
  9.6 0.4 fusion
  10.0 0.0 copy-done.5
  10.0 1.6 fusion.2
  11.6 107.0 %all-gather.2.cloned.1.call-done = bf16[2560,2880]{1,0:T(8,128)(2,1)} async-done(((bf16[80,2880]{1,0:T(8,128)(2,1)}), bf16[2560,2880]{1,0:T(8,128)(2,1)}) %all-gather.2.cloned.1.call-update) | async-done | bytes 14745616 | tf_op jit(solution)/shard_map/all_gather | solution.py:167
  118.6 0.0 copy-done.6
  118.6 8.1 %convolution_add_fusion.q_ref = f32[256,2560]{1,0:T(8,128)S(1)} fusion(bf16[256,2880]{0,1:T(8,128)(2,1)} %fusion.2, bf16[2560,2880]{1,0:T(8,128)(2,1)} %all-gather.2.cloned.1.call-done, f32[2560]{0:T(1024)S(1)} %copy-done.6), kind=kOutput, calls=%fused_computation | convolution fusion | flops 3775528960 | bytes 18851840 | tf_op jit(solution)/shard_map/dot_general | solution.py:184
  126.7 0.0 copy-start.2
  126.7 0.0 copy-start.3
  126.7 0.0 copy-start.4
  126.7 1.4 copy-done.2
  128.2 0.1 copy.9
  128.4 0.1 copy.10
  128.5 2.5 %collective-permute-start = (bf16[2,128,256]{2,1,0:T(8,128)(2,1)S(1)}, bf16[2,128,256]{2,1,0:T(8,128)(2,1)S(1)}, u32[]{:S(2)}, u32[]{:S(2)}) collective-permute-start(bf16[2,128,256]{2,1,0:T(8,128)(2,1)S(1)} %pad_maximum_fusion), channel_id=1, source_target_pairs={{0,1},{1,2},{2,3},{3,4},{4,5},{5,6},{6,7},{7,8},{8,9},{9,10},{10,1... | collective-permute-start | bytes 393224 | tf_op jit(solution)/shard_map/ppermute | solution.py:17
  131.0 0.8 copy.15.limit_ref
  131.8 0.7 copy.16.cos_ref
  132.6 0.7 copy.17.sin_ref
  133.3 3.7 %collective-permute-done = bf16[2,128,256]{2,1,0:T(8,128)(2,1)S(1)} collective-permute-done((bf16[2,128,256]{2,1,0:T(8,128)(2,1)S(1)}, bf16[2,128,256]{2,1,0:T(8,128)(2,1)S(1)}, u32[]{:S(2)}, u32[]{:S(2)}) %collective-permute-start) | collective-permute-done | bytes 131104 | tf_op jit(solution)/shard_map/ppermute | solution.py:17
  137.0 0.0 copy-done.3
  137.0 0.0 copy-done.4
  137.1 0.2 copy.13
  137.3 0.9 copy.14
  138.2 0.2 copy.11
  138.4 1.0 copy.12
  139.3 13.9 %shard_map.82 = bf16[256,2048]{1,0:T(8,128)(2,1)} custom-call(f32[32]{0:T(128)} %sinks_ref.1, s32[256,1]{1,0:T(8,128)} %copy.15.limit_ref, f32[256,128]{1,0:T(8,128)} %copy.16.cos_ref, f32[256,128]{1,0:T(8,128)} %copy.17.sin_ref, f32[256,2560]{1,0:T(8,128)} %copy-done.2, bf16[4,384,64]{2,1,0:T(8,128)(2,1)} %bitcast.18, bf16[4,384,64]{2,1,0:T(8,128)(2,1)} %bitcast.17), custom_call_target="tpu_custom_call" | custom-call | tf_op jit(solution)/shard_map/pallas_call | solution.py:123
  (13 shorter events, 0.2 us)
Async XLA Ops:
  6.5 1.2 copy-start
  6.5 3.0 %copy-start.1 = (bf16[256,2880]{0,1:T(8,128)(2,1)S(1)}, bf16[256,2880]{0,1:T(8,128)(2,1)}, u32[]{:S(2)}) copy-start(bf16[256,2880]{0,1:T(8,128)(2,1)} %param.8) | copy-start | bytes 4423684
  6.5 3.5 %copy-start.5 = (f32[2880]{0:T(1024)S(1)}, f32[2880]{0:T(1024)}, u32[]{:S(2)}) copy-start(f32[2880]{0:T(1024)} %param.10) | copy-start | bytes 34564
  6.5 112.1 %all-gather.2.cloned.1.call-start = ((), (), s32[]{:S(2)}) async-start(), calls=%async_computation | async-start | bytes 15544320 | tf_op jit(solution)/shard_map/all_gather | solution.py:167
  8.6 110.1 %copy-start.6 = (f32[2560]{0:T(1024)S(1)}, f32[2560]{0:T(1024)}, u32[]{:S(2)}) copy-start(f32[2560]{0:T(1024)} %param.12) | copy-start | bytes 30724
  126.7 1.5 copy-start.2
  126.7 10.3 %copy-start.3 = (bf16[128,256]{1,0:T(8,128)(2,1)S(1)}, bf16[128,256]{1,0:T(8,128)(2,1)}, u32[]{:S(2)}) copy-start(bf16[128,256]{1,0:T(8,128)(2,1)} %param.15) | copy-start | bytes 196612
  126.7 10.3 %copy-start.4 = (bf16[128,256]{1,0:T(8,128)(2,1)S(1)}, bf16[128,256]{1,0:T(8,128)(2,1)}, u32[]{:S(2)}) copy-start(bf16[128,256]{1,0:T(8,128)(2,1)} %param.14) | copy-start | bytes 196612
  128.5 8.5 %collective-permute-start = (bf16[2,128,256]{2,1,0:T(8,128)(2,1)S(1)}, bf16[2,128,256]{2,1,0:T(8,128)(2,1)S(1)}, u32[]{:S(2)}, u32[]{:S(2)}) collective-permute-start(bf16[2,128,256]{2,1,0:T(8,128)(2,1)S(1)} %pad_maximum_fusion), channel_id=1, source_target_pairs={{0,1},{1,2},{2,3},{3,4},{4,5},{5,6},{6,7},{7,8},{8,9},{9,10},{10,1... | collective-permute-start | bytes 393224 | tf_op jit(solution)/shard_map/ppermute | solution.py:17
Sparse Core Ops, SparseCore 0:
  10.2 108.3 all-gather.1

commit v7 on v5

--- a/solution.py
+++ b/solution.py
@@ -69,7 +69,7 @@
         first = pltpu.roll(x, half, 1)
         second = pltpu.roll(x, lanes - half, 1)
         partner = jnp.where(take_first, first, second)
-        rotated = (x * cosine + partner * sine).astype(jnp.bfloat16)
+        rotated = ((x * cosine + partner * sine) * HEAD_SIZE ** (-0.5)).astype(jnp.bfloat16)
         for inner in range(heads_per_chunk):
             head = chunk * heads_per_chunk + inner
             sink = sinks_ref[group * query_group + head]
@@ -80,12 +80,12 @@
                 values = v_ref[0, part * block : part * block + 2 * block, :]
                 scores = lax.dot_general(
                     queries, keys, (((1,), (1,)), ((), ())), preferred_element_type=jnp.float32
-                ) * HEAD_SIZE ** (-0.5)
+                )
                 scores = jnp.where(visible[part], scores, -1e30)
                 top = jnp.maximum(jnp.max(scores, axis=1, keepdims=True), sink)
                 expo = jnp.exp(scores - top)
                 total = jnp.sum(expo, axis=1, keepdims=True) + jnp.exp(sink - top)
-                probs = (expo / total).astype(jnp.bfloat16)
+                probs = (expo * (1.0 / total)).astype(jnp.bfloat16)
                 out = jnp.dot(probs, values, preferred_element_type=jnp.float32)
                 out_ref[part * block : (part + 1) * block, head * HEAD_SIZE : (head + 1) * HEAD_SIZE] = out.astype(
                     jnp.bfloat16

time: 159 us -> 159 us (level)
  no operation moved by 1% of the time
where the time goes in v7:
time: 159 us
  waiting for transfers between devices  111 us (70%)
  between operations  13.6 us (9%)
  Pallas kernels  12.8 us (8%)
  local copies, waits for them, and re-layouts  8.25 us (5%)
  matrix products  8.05 us (5%)
  other arithmetic  3.1 us (2%)
  starting transfers between devices  2.47 us (2%)
    all_gather x1, waiting for transfers between devices, gather_weight(): return lax.all_gather(own.T, ('ctx', 'dp'), axis=0, tiled=True)  107 us
    pallas_call x1, Pallas kernels, attend(): pl.pallas_call(attention_kernel, grid=(KEY_VALUE_HEADS,), in_specs=[pl.Bl...  12.8 us
    dot_general x1, matrix products, on_device(): lax.dot_general(normed, gather_weight(qkv_weight), (((1,), (1,)), ((), ()...  8.05 us
    ppermute x1, waiting for transfers between devices, shifted(): lax.ppermute(value, axis, [(source, source + steps) for source in range(l...  3.69 us
  transfers between devices with their start and end apart: 2, of which 2 were waited for; matrix products, arithmetic and copies ran while one was open for 3% of the time, Pallas kernels for 0%

profile of v7, /device:TPU:4, one launch (start us, length us, event | category | flops | bytes accessed | tf_op | source)
XLA Modules:
  0.0 159.0 jit_solution(5751572175870137638)
XLA Ops:
  6.5 0.0 copy-start
  6.5 0.0 copy-start.1
  6.5 0.0 copy-start.5
  6.5 0.0 all-gather.2.cloned.1.call-start
  6.6 1.2 copy-done
  7.7 0.8 dynamic-slice_bitcast_fusion
  8.5 0.0 all-gather.2.cloned.1.call-update
  8.6 0.0 copy-start.6
  8.6 0.8 broadcast_minimum_fusion
  9.3 0.2 fusion.4
  9.6 0.0 copy-done.1
  9.6 0.4 fusion
  10.0 0.0 copy-done.5
  10.0 1.6 %fusion.2 = bf16[256,2880]{0,1:T(8,128)(2,1)} fusion(bf16[256,2880]{0,1:T(8,128)(2,1)S(1)} %copy-done.1, f32[2880]{0:T(1024)S(1)} %copy-done.5, f32[256]{0:T(256)S(1)} %add_rsqrt_fusion), kind=kLoop, calls=%fused_computation.5 | loop fusion | flops 2949120 | bytes 2961664 | tf_op jit(solution)/shard_map/convert_element_type | solution.py:172
  11.6 107.0 %all-gather.2.cloned.1.call-done = bf16[2560,2880]{1,0:T(8,128)(2,1)} async-done(((bf16[80,2880]{1,0:T(8,128)(2,1)}), bf16[2560,2880]{1,0:T(8,128)(2,1)}) %all-gather.2.cloned.1.call-update) | async-done | bytes 14745616 | tf_op jit(solution)/shard_map/all_gather | solution.py:160
  118.6 0.0 copy-done.6
  118.6 8.1 %convolution_add_fusion.q_ref = f32[256,2560]{1,0:T(8,128)S(1)} fusion(bf16[256,2880]{0,1:T(8,128)(2,1)} %fusion.2, bf16[2560,2880]{1,0:T(8,128)(2,1)} %all-gather.2.cloned.1.call-done, f32[2560]{0:T(1024)S(1)} %copy-done.6), kind=kOutput, calls=%fused_computation | convolution fusion | flops 3775528960 | bytes 18851840 | tf_op jit(solution)/shard_map/dot_general | solution.py:177
  126.7 0.0 copy-start.2
  126.7 0.0 copy-start.3
  126.7 0.0 copy-start.4
  126.7 1.4 copy-done.2
  128.2 0.1 copy.9
  128.4 0.1 copy.10
  128.5 2.5 %collective-permute-start = (bf16[2,128,256]{2,1,0:T(8,128)(2,1)S(1)}, bf16[2,128,256]{2,1,0:T(8,128)(2,1)S(1)}, u32[]{:S(2)}, u32[]{:S(2)}) collective-permute-start(bf16[2,128,256]{2,1,0:T(8,128)(2,1)S(1)} %pad_maximum_fusion), channel_id=1, source_target_pairs={{0,1},{1,2},{2,3},{3,4},{4,5},{5,6},{6,7},{7,8},{8,9},{9,10},{10,1... | collective-permute-start | bytes 393224 | tf_op jit(solution)/shard_map/ppermute | solution.py:17
  131.0 0.8 copy.15.limit_ref
  131.8 0.7 copy.16.cos_ref
  132.6 0.7 copy.17.sin_ref
  133.3 3.7 %collective-permute-done = bf16[2,128,256]{2,1,0:T(8,128)(2,1)S(1)} collective-permute-done((bf16[2,128,256]{2,1,0:T(8,128)(2,1)S(1)}, bf16[2,128,256]{2,1,0:T(8,128)(2,1)S(1)}, u32[]{:S(2)}, u32[]{:S(2)}) %collective-permute-start) | collective-permute-done | bytes 131104 | tf_op jit(solution)/shard_map/ppermute | solution.py:17
  137.0 0.0 copy-done.3
  137.0 0.0 copy-done.4
  137.1 0.2 copy.13
  137.3 0.9 copy.14
  138.2 0.2 copy.11
  138.4 1.0 copy.12
  139.3 12.8 %shard_map.82 = bf16[256,2048]{1,0:T(8,128)(2,1)} custom-call(f32[32]{0:T(128)} %sinks_ref.1, s32[256,1]{1,0:T(8,128)} %copy.15.limit_ref, f32[256,128]{1,0:T(8,128)} %copy.16.cos_ref, f32[256,128]{1,0:T(8,128)} %copy.17.sin_ref, f32[256,2560]{1,0:T(8,128)} %copy-done.2, bf16[4,384,64]{2,1,0:T(8,128)(2,1)} %bitcast.18, bf16[4,384,64]{2,1,0:T(8,128)(2,1)} %bitcast.17), custom_call_target="tpu_custom_call" | custom-call | tf_op jit(solution)/shard_map/pallas_call | solution.py:116
  (13 shorter events, 0.2 us)
Async XLA Ops:
  6.5 1.2 copy-start
  6.5 3.0 %copy-start.1 = (bf16[256,2880]{0,1:T(8,128)(2,1)S(1)}, bf16[256,2880]{0,1:T(8,128)(2,1)}, u32[]{:S(2)}) copy-start(bf16[256,2880]{0,1:T(8,128)(2,1)} %param.8) | copy-start | bytes 4423684
  6.5 3.5 %copy-start.5 = (f32[2880]{0:T(1024)S(1)}, f32[2880]{0:T(1024)}, u32[]{:S(2)}) copy-start(f32[2880]{0:T(1024)} %param.10) | copy-start | bytes 34564
  6.5 112.1 %all-gather.2.cloned.1.call-start = ((), (), s32[]{:S(2)}) async-start(), calls=%async_computation | async-start | bytes 15544320 | tf_op jit(solution)/shard_map/all_gather | solution.py:160
  8.6 110.1 %copy-start.6 = (f32[2560]{0:T(1024)S(1)}, f32[2560]{0:T(1024)}, u32[]{:S(2)}) copy-start(f32[2560]{0:T(1024)} %param.12) | copy-start | bytes 30724
  126.7 1.5 copy-start.2
  126.7 10.3 %copy-start.3 = (bf16[128,256]{1,0:T(8,128)(2,1)S(1)}, bf16[128,256]{1,0:T(8,128)(2,1)}, u32[]{:S(2)}) copy-start(bf16[128,256]{1,0:T(8,128)(2,1)} %param.15) | copy-start | bytes 196612
  126.7 10.3 %copy-start.4 = (bf16[128,256]{1,0:T(8,128)(2,1)S(1)}, bf16[128,256]{1,0:T(8,128)(2,1)}, u32[]{:S(2)}) copy-start(bf16[128,256]{1,0:T(8,128)(2,1)} %param.14) | copy-start | bytes 196612
  128.5 8.5 %collective-permute-start = (bf16[2,128,256]{2,1,0:T(8,128)(2,1)S(1)}, bf16[2,128,256]{2,1,0:T(8,128)(2,1)S(1)}, u32[]{:S(2)}, u32[]{:S(2)}) collective-permute-start(bf16[2,128,256]{2,1,0:T(8,128)(2,1)S(1)} %pad_maximum_fusion), channel_id=1, source_target_pairs={{0,1},{1,2},{2,3},{3,4},{4,5},{5,6},{6,7},{7,8},{8,9},{9,10},{10,1... | collective-permute-start | bytes 393224 | tf_op jit(solution)/shard_map/ppermute | solution.py:17
Sparse Core Ops, SparseCore 0:
  10.2 108.3 all-gather.1

commit v8 on v5

--- a/solution.py
+++ b/solution.py
@@ -157,7 +157,8 @@
         return lax.all_gather(qkv_weight.T, "ctx", axis=0, tiled=True)
     piece = columns // pairs
     own = lax.dynamic_slice_in_dim(qkv_weight, lax.axis_index("dp") * piece, piece, axis=1)
-    return lax.all_gather(own.T, ("ctx", "dp"), axis=0, tiled=True)
+    flat = lax.all_gather(own.T.reshape(-1), ("ctx", "dp"), axis=0, tiled=True)
+    return flat.reshape(columns * lax.axis_size("ctx"), qkv_weight.shape[0])
 
 
 def on_device(

time: 159 us -> 183 us (1.15)
  local copies, waits for them, and re-layouts: 8.25 us -> 34 us
  waiting for transfers between devices: 111 us -> 109 us
    reshape x0 -> x2, local copies, waits for them, and re-layouts: none -> 26.5 us  [the longest x1 25.2 us: gather_weight(): return flat.reshape(columns * lax.axis_size('ctx'), qkv_weight.shape[0])]
    all_gather x1, waiting for transfers between devices: 107 us -> 105 us  [gather_weight(): flat = lax.all_gather(own.T.reshape(-1), ('ctx', 'dp'), axis=0, tiled=True)]
where the time goes in v8:
time: 183 us
  waiting for transfers between devices  109 us (60%)
  local copies, waits for them, and re-layouts  34 us (19%)
  between operations  13.6 us (7%)
  Pallas kernels  12.6 us (7%)
  matrix products  7.91 us (4%)
  other arithmetic  3.06 us (2%)
  starting transfers between devices  2.46 us (1%)
    all_gather x1, waiting for transfers between devices, gather_weight(): flat = lax.all_gather(own.T.reshape(-1), ('ctx', 'dp'), axis=0, tiled=True)  105 us
    reshape x1, local copies, waits for them, and re-layouts, gather_weight(): return flat.reshape(columns * lax.axis_size('ctx'), qkv_weight.shape[0])  25.2 us
    pallas_call x1, Pallas kernels, attend(): pl.pallas_call(attention_kernel, grid=(KEY_VALUE_HEADS,), in_specs=[pl.Bl...  12.6 us
    dot_general x1, matrix products, on_device(): lax.dot_general(normed, gather_weight(qkv_weight), (((1,), (1,)), ((), ()...  7.91 us
    ppermute x1, waiting for transfers between devices, shifted(): lax.ppermute(value, axis, [(source, source + steps) for source in range(l...  3.7 us
  transfers between devices with their start and end apart: 2, of which 2 were waited for; matrix products, arithmetic and copies ran while one was open for 3% of the time, Pallas kernels for 0%

profile of v8, /device:TPU:4, one launch (start us, length us, event | category | flops | bytes accessed | tf_op | source)
XLA Modules:
  0.0 182.5 jit_solution(13284651546316694891)
XLA Ops:
  6.5 0.0 copy-start
  6.5 0.0 copy-start.1
  6.5 0.0 copy-start.6
  6.5 0.0 all-gather.2.cloned.1.call-start
  6.6 1.2 copy-done
  7.8 1.4 reshape.93
  9.1 0.0 all-gather.2.cloned.1.call-update
  9.2 0.8 broadcast_minimum_fusion
  9.9 0.2 fusion.4
  10.1 0.0 copy-done.1
  10.2 0.4 fusion
  10.6 0.0 copy-done.6
  10.6 1.6 fusion.2
  12.2 0.0 copy-start.3
  12.2 0.0 copy-start.7
  12.2 105.1 %all-gather.2.cloned.1.call-done = bf16[7372800]{0:T(1024)(128)(2,1)} async-done(((bf16[230400]{0:T(1024)(128)(2,1)}), bf16[7372800]{0:T(1024)(128)(2,1)}) %all-gather.2.cloned.1.call-update) | async-done | bytes 14745616 | tf_op jit(solution)/shard_map/all_gather | solution.py:160
  117.3 25.2 %reshape.94 = bf16[2560,2880]{1,0:T(8,128)(2,1)} reshape(bf16[7372800]{0:T(1024)(128)(2,1)} %all-gather.2.cloned.1.call-done) | data formatting | bytes 29491200 | tf_op jit(solution)/shard_map/reshape | solution.py:161
  142.5 0.0 copy-done.3
  142.5 0.0 copy-done.7
  142.5 7.9 %convolution_add_fusion.q_ref = f32[256,2560]{1,0:T(8,128)S(1)} fusion(bf16[256,2880]{0,1:T(8,128)(2,1)S(1)} %copy-done.3, bf16[2560,2880]{1,0:T(8,128)(2,1)} %reshape.94, f32[2560]{0:T(1024)S(1)} %copy-done.7), kind=kOutput, calls=%fused_computation | convolution fusion | flops 3775528960 | bytes 18851840 | tf_op jit(solution)/shard_map/dot_general | solution.py:178
  150.4 0.0 copy-start.2
  150.4 0.0 copy-start.4
  150.5 0.0 copy-start.5
  150.5 1.4 copy-done.2
  152.0 0.1 copy.18
  152.2 0.1 copy.19
  152.3 2.5 %collective-permute-start = (bf16[2,128,256]{2,1,0:T(8,128)(2,1)S(1)}, bf16[2,128,256]{2,1,0:T(8,128)(2,1)S(1)}, u32[]{:S(2)}, u32[]{:S(2)}) collective-permute-start(bf16[2,128,256]{2,1,0:T(8,128)(2,1)S(1)} %pad_maximum_fusion), channel_id=1, source_target_pairs={{0,1},{1,2},{2,3},{3,4},{4,5},{5,6},{6,7},{7,8},{8,9},{9,10},{10,1... | collective-permute-start | bytes 393224 | tf_op jit(solution)/shard_map/ppermute | solution.py:17
  154.8 0.8 copy.24.limit_ref
  155.6 0.7 copy.25.cos_ref
  156.3 0.7 copy.26.sin_ref
  157.0 3.7 %collective-permute-done = bf16[2,128,256]{2,1,0:T(8,128)(2,1)S(1)} collective-permute-done((bf16[2,128,256]{2,1,0:T(8,128)(2,1)S(1)}, bf16[2,128,256]{2,1,0:T(8,128)(2,1)S(1)}, u32[]{:S(2)}, u32[]{:S(2)}) %collective-permute-start) | collective-permute-done | bytes 131104 | tf_op jit(solution)/shard_map/ppermute | solution.py:17
  160.7 0.0 copy-done.4
  160.8 0.0 copy-done.5
  160.8 0.2 copy.22
  161.0 0.9 copy.23
  161.9 0.2 copy.20
  162.1 1.0 copy.21
  163.1 12.6 %shard_map.82 = bf16[256,2048]{1,0:T(8,128)(2,1)} custom-call(f32[32]{0:T(128)} %sinks_ref.1, s32[256,1]{1,0:T(8,128)} %copy.24.limit_ref, f32[256,128]{1,0:T(8,128)} %copy.25.cos_ref, f32[256,128]{1,0:T(8,128)} %copy.26.sin_ref, f32[256,2560]{1,0:T(8,128)} %copy-done.2, bf16[4,384,64]{2,1,0:T(8,128)(2,1)} %bitcast.18, bf16[4,384,64]{2,1,0:T(8,128)(2,1)} %bitcast.17), custom_call_target="tpu_custom_call" | custom-call | tf_op jit(solution)/shard_map/pallas_call | solution.py:116
  (14 shorter events, 0.3 us)
Async XLA Ops:
  6.5 1.2 copy-start
  6.5 3.6 %copy-start.1 = (bf16[256,2880]{0,1:T(8,128)(2,1)S(1)}, bf16[256,2880]{0,1:T(8,128)(2,1)}, u32[]{:S(2)}) copy-start(bf16[256,2880]{0,1:T(8,128)(2,1)} %param.8) | copy-start | bytes 4423684
  6.5 4.0 %copy-start.6 = (f32[2880]{0:T(1024)S(1)}, f32[2880]{0:T(1024)}, u32[]{:S(2)}) copy-start(f32[2880]{0:T(1024)} %param.10) | copy-start | bytes 34564
  6.5 110.8 %all-gather.2.cloned.1.call-start = ((), (), s32[]{:S(2)}) async-start(), calls=%async_computation | async-start | bytes 15206400 | tf_op jit(solution)/shard_map/all_gather | solution.py:160
  12.2 130.3 %copy-start.3 = (bf16[256,2880]{0,1:T(8,128)(2,1)S(1)}, bf16[256,2880]{0,1:T(8,128)(2,1)}, u32[]{:S(2)}) copy-start(bf16[256,2880]{0,1:T(8,128)(2,1)} %fusion.2) | copy-start | bytes 4423684
  12.2 130.3 %copy-start.7 = (f32[2560]{0:T(1024)S(1)}, f32[2560]{0:T(1024)}, u32[]{:S(2)}) copy-start(f32[2560]{0:T(1024)} %param.12) | copy-start | bytes 30724
  150.4 1.5 copy-start.2
  150.4 10.3 %copy-start.4 = (bf16[128,256]{1,0:T(8,128)(2,1)S(1)}, bf16[128,256]{1,0:T(8,128)(2,1)}, u32[]{:S(2)}) copy-start(bf16[128,256]{1,0:T(8,128)(2,1)} %param.15) | copy-start | bytes 196612
  150.5 10.3 %copy-start.5 = (bf16[128,256]{1,0:T(8,128)(2,1)S(1)}, bf16[128,256]{1,0:T(8,128)(2,1)}, u32[]{:S(2)}) copy-start(bf16[128,256]{1,0:T(8,128)(2,1)} %param.14) | copy-start | bytes 196612
  152.3 8.5 %collective-permute-start = (bf16[2,128,256]{2,1,0:T(8,128)(2,1)S(1)}, bf16[2,128,256]{2,1,0:T(8,128)(2,1)S(1)}, u32[]{:S(2)}, u32[]{:S(2)}) collective-permute-start(bf16[2,128,256]{2,1,0:T(8,128)(2,1)S(1)} %pad_maximum_fusion), channel_id=1, source_target_pairs={{0,1},{1,2},{2,3},{3,4},{4,5},{5,6},{6,7},{7,8},{8,9},{9,10},{10,1... | collective-permute-start | bytes 393224 | tf_op jit(solution)/shard_map/ppermute | solution.py:17
Sparse Core Ops, SparseCore 0:
  10.3 107.0 all-gather.1

commit v9 on v7

--- a/solution.py
+++ b/solution.py
@@ -56,12 +56,12 @@
     partner_lane = jnp.where(lane % HEAD_SIZE < half, lane + half, lane - half)
     take_first = source == partner_lane
     block = WINDOW_TOKENS
-    query_index = lax.broadcasted_iota(jnp.int32, (block, 2 * block), 0)
-    key_index = lax.broadcasted_iota(jnp.int32, (block, 2 * block), 1)
+    key_index = lax.broadcasted_iota(jnp.int32, (2 * block, block), 0)
+    query_index = lax.broadcasted_iota(jnp.int32, (2 * block, block), 1)
     rel = query_index - key_index + block
     visible = []
     for part in range(rows // block):
-        limit = limit_ref[part * block : (part + 1) * block, :]
+        limit = limit_ref[part : part + 1, :]
         visible.append((rel >= 0) & (rel <= limit))
     heads_per_chunk = lanes // HEAD_SIZE
     for chunk in range(q_ref.shape[1] // lanes):
@@ -77,17 +77,17 @@
             for part in range(rows // block):
                 queries = query_head[part * block : (part + 1) * block]
                 keys = k_ref[0, part * block : part * block + 2 * block, :]
-                values = v_ref[0, part * block : part * block + 2 * block, :]
+                values = v_ref[0, :, part * block : part * block + 2 * block]
                 scores = lax.dot_general(
-                    queries, keys, (((1,), (1,)), ((), ())), preferred_element_type=jnp.float32
+                    keys, queries, (((1,), (1,)), ((), ())), preferred_element_type=jnp.float32
                 )
                 scores = jnp.where(visible[part], scores, -1e30)
-                top = jnp.maximum(jnp.max(scores, axis=1, keepdims=True), sink)
+                top = jnp.maximum(jnp.max(scores, axis=0, keepdims=True), sink)
                 expo = jnp.exp(scores - top)
-                total = jnp.sum(expo, axis=1, keepdims=True) + jnp.exp(sink - top)
+                total = jnp.sum(expo, axis=0, keepdims=True) + jnp.exp(sink - top)
                 probs = (expo * (1.0 / total)).astype(jnp.bfloat16)
-                out = jnp.dot(probs, values, preferred_element_type=jnp.float32)
-                out_ref[part * block : (part + 1) * block, head * HEAD_SIZE : (head + 1) * HEAD_SIZE] = out.astype(
+                out = jnp.dot(values, probs, preferred_element_type=jnp.float32)
+                out_ref[part * block : (part + 1) * block, head * HEAD_SIZE : (head + 1) * HEAD_SIZE] = out.T.astype(
                     jnp.bfloat16
                 )
 
@@ -111,19 +111,19 @@
     cos_table, sin_table, limit = tables
     lanes = cos_table.shape[1]
     keys = jnp.moveaxis(joined_keys, 1, 0)
-    values = jnp.moveaxis(joined_values, 1, 0)
+    values = jnp.transpose(joined_values, (1, 2, 0))
     key_rows = keys.shape[1]
     return pl.pallas_call(
         attention_kernel,
         grid=(KEY_VALUE_HEADS,),
         in_specs=[
             pl.BlockSpec(memory_space=pltpu.SMEM),
-            pl.BlockSpec((token_rows, 1), lambda g: (0, 0)),
+            pl.BlockSpec(limit.shape, lambda g: (0, 0)),
             pl.BlockSpec((token_rows, lanes), lambda g: (0, 0)),
             pl.BlockSpec((token_rows, lanes), lambda g: (0, 0)),
             pl.BlockSpec((token_rows, group_width), lambda g: (0, g)),
             pl.BlockSpec((1, key_rows, HEAD_SIZE), lambda g: (g, 0, 0)),
-            pl.BlockSpec((1, key_rows, HEAD_SIZE), lambda g: (g, 0, 0)),
+            pl.BlockSpec((1, HEAD_SIZE, key_rows), lambda g: (g, 0, 0)),
         ],
         out_specs=pl.BlockSpec((token_rows, group_width), lambda g: (0, g)),
         out_shape=jax.ShapeDtypeStruct((token_rows, QUERY_HEADS * HEAD_SIZE), jnp.bfloat16),
@@ -171,7 +171,7 @@
     scale = lax.rsqrt(jnp.mean(flat * flat, axis=-1, keepdims=True) + 1e-05)
     normed = (flat * scale * norm_gain[None, :]).astype(jnp.bfloat16)
     tables = rotation_tables(positions, 128) + (
-        jnp.minimum(positions, WINDOW_TOKENS - 1).astype(jnp.int32)[:, None],
+        jnp.minimum(positions, WINDOW_TOKENS - 1).astype(jnp.int32).reshape(-1, WINDOW_TOKENS),
     )
     normed, tables = lax.optimization_barrier((normed, tables))
     combined_output = lax.dot_general(

time: 159 us -> 161 us (1.013)
  Pallas kernels: 12.8 us -> 14.5 us
    pallas_call x1, Pallas kernels: 12.8 us -> 14.5 us  [attend(): pl.pallas_call(attention_kernel, grid=(KEY_VALUE_HEADS,), in_specs=[pl.Bl...]
where the time goes in v9:
time: 161 us; the launch traced here: 160 us
  waiting for transfers between devices  111 us (69%)
  Pallas kernels  14.5 us (9%)
  between operations  13.6 us (8%)
  matrix products  8.05 us (5%)
  local copies, waits for them, and re-layouts  7.19 us (4%)
  other arithmetic  3.68 us (2%)
  starting transfers between devices  2.47 us (2%)
    all_gather x1, waiting for transfers between devices, gather_weight(): return lax.all_gather(own.T, ('ctx', 'dp'), axis=0, tiled=True)  106 us
    pallas_call x1, Pallas kernels, attend(): pl.pallas_call(attention_kernel, grid=(KEY_VALUE_HEADS,), in_specs=[pl.Bl...  14.5 us
    dot_general x1, matrix products, on_device(): lax.dot_general(normed, gather_weight(qkv_weight), (((1,), (1,)), ((), ()...  8.05 us
    ppermute x1, waiting for transfers between devices, shifted(): lax.ppermute(value, axis, [(source, source + steps) for source in range(l...  4.48 us
  transfers between devices with their start and end apart: 2, of which 2 were waited for; matrix products, arithmetic and copies ran while one was open for 3% of the time, Pallas kernels for 0%

profile of v9, /device:TPU:4, one launch (start us, length us, event | category | flops | bytes accessed | tf_op | source)
XLA Modules:
  0.0 160.4 jit_solution(6159299677033108209)
XLA Ops:
  6.5 0.0 copy-start
  6.5 0.0 copy-start.1
  6.5 0.0 copy-start.5
  6.5 0.0 all-gather.2.cloned.1.call-start
  6.6 1.2 copy-done
  7.7 0.8 dynamic-slice_bitcast_fusion
  8.5 0.0 all-gather.2.cloned.1.call-update
  8.6 0.0 copy-start.6
  8.6 1.3 minimum_bitcast_fusion
  9.9 0.2 fusion.4
  10.1 0.0 copy-done.1
  10.1 0.4 fusion
  10.6 0.0 copy-done.5
  10.6 1.6 fusion.2
  12.2 106.4 %all-gather.2.cloned.1.call-done = bf16[2560,2880]{1,0:T(8,128)(2,1)} async-done(((bf16[80,2880]{1,0:T(8,128)(2,1)}), bf16[2560,2880]{1,0:T(8,128)(2,1)}) %all-gather.2.cloned.1.call-update) | async-done | bytes 14745616 | tf_op jit(solution)/shard_map/all_gather | solution.py:160
  118.6 0.0 copy-done.6
  118.6 8.1 %convolution_add_fusion.q_ref = f32[256,2560]{1,0:T(8,128)S(1)} fusion(bf16[256,2880]{0,1:T(8,128)(2,1)} %fusion.2, bf16[2560,2880]{1,0:T(8,128)(2,1)} %all-gather.2.cloned.1.call-done, f32[2560]{0:T(1024)S(1)} %copy-done.6), kind=kOutput, calls=%fused_computation | convolution fusion | flops 3775528960 | bytes 18851840 | tf_op jit(solution)/shard_map/dot_general | solution.py:177
  126.7 0.0 copy-start.2
  126.7 0.0 copy-start.3
  126.7 0.0 copy-start.4
  126.7 1.4 copy-done.2
  128.2 0.1 copy.10
  128.4 0.1 copy.11
  128.5 2.5 %collective-permute-start = (bf16[2,128,256]{2,1,0:T(8,128)(2,1)S(1)}, bf16[2,128,256]{2,1,0:T(8,128)(2,1)S(1)}, u32[]{:S(2)}, u32[]{:S(2)}) collective-permute-start(bf16[2,128,256]{2,1,0:T(8,128)(2,1)S(1)} %pad_maximum_fusion), channel_id=1, source_target_pairs={{0,1},{1,2},{2,3},{3,4},{4,5},{5,6},{6,7},{7,8},{8,9},{9,10},{10,1... | collective-permute-start | bytes 393224 | tf_op jit(solution)/shard_map/ppermute | solution.py:17
  131.0 0.8 copy.15.cos_ref
  131.8 0.7 copy.16.sin_ref
  132.5 4.5 %collective-permute-done = bf16[2,128,256]{2,1,0:T(8,128)(2,1)S(1)} collective-permute-done((bf16[2,128,256]{2,1,0:T(8,128)(2,1)S(1)}, bf16[2,128,256]{2,1,0:T(8,128)(2,1)S(1)}, u32[]{:S(2)}, u32[]{:S(2)}) %collective-permute-start) | collective-permute-done | bytes 131104 | tf_op jit(solution)/shard_map/ppermute | solution.py:17
  137.0 0.0 copy-done.3
  137.0 0.0 copy-done.4
  137.1 0.2 copy.12
  137.3 1.0 copy.13
  138.2 0.8 copy.14
  139.0 14.5 %shard_map.82 = bf16[256,2048]{1,0:T(8,128)(2,1)} custom-call(f32[32]{0:T(128)} %sinks_ref.1, s32[2,128]{1,0:T(2,128)} %get-tuple-element.9.limit_ref, f32[256,128]{1,0:T(8,128)} %copy.15.cos_ref, f32[256,128]{1,0:T(8,128)} %copy.16.sin_ref, f32[256,2560]{1,0:T(8,128)} %copy-done.2, bf16[4,384,64]{2,1,0:T(8,128)(2,1)} %bitcast.19, bf16[4,64,384]{2,1,0:T(8,128)(2,1)} %bitcast.22), custom_call_target="tpu_custom_call" | custom-call | tf_op jit(solution)/shard_map/pallas_call | solution.py:116
  (13 shorter events, 0.2 us)
Async XLA Ops:
  6.5 1.2 copy-start
  6.5 3.6 %copy-start.1 = (bf16[256,2880]{0,1:T(8,128)(2,1)S(1)}, bf16[256,2880]{0,1:T(8,128)(2,1)}, u32[]{:S(2)}) copy-start(bf16[256,2880]{0,1:T(8,128)(2,1)} %param.8) | copy-start | bytes 4423684
  6.5 4.0 %copy-start.5 = (f32[2880]{0:T(1024)S(1)}, f32[2880]{0:T(1024)}, u32[]{:S(2)}) copy-start(f32[2880]{0:T(1024)} %param.10) | copy-start | bytes 34564
  6.5 112.1 %all-gather.2.cloned.1.call-start = ((), (), s32[]{:S(2)}) async-start(), calls=%async_computation | async-start | bytes 15544320 | tf_op jit(solution)/shard_map/all_gather | solution.py:160
  8.6 110.1 %copy-start.6 = (f32[2560]{0:T(1024)S(1)}, f32[2560]{0:T(1024)}, u32[]{:S(2)}) copy-start(f32[2560]{0:T(1024)} %param.12) | copy-start | bytes 30724
  126.7 1.5 copy-start.2
  126.7 10.3 %copy-start.3 = (bf16[128,256]{1,0:T(8,128)(2,1)S(1)}, bf16[128,256]{1,0:T(8,128)(2,1)}, u32[]{:S(2)}) copy-start(bf16[128,256]{1,0:T(8,128)(2,1)} %param.15) | copy-start | bytes 196612
  126.7 10.3 %copy-start.4 = (bf16[128,256]{1,0:T(8,128)(2,1)S(1)}, bf16[128,256]{1,0:T(8,128)(2,1)}, u32[]{:S(2)}) copy-start(bf16[128,256]{1,0:T(8,128)(2,1)} %param.14) | copy-start | bytes 196612
  128.5 8.5 %collective-permute-start = (bf16[2,128,256]{2,1,0:T(8,128)(2,1)S(1)}, bf16[2,128,256]{2,1,0:T(8,128)(2,1)S(1)}, u32[]{:S(2)}, u32[]{:S(2)}) collective-permute-start(bf16[2,128,256]{2,1,0:T(8,128)(2,1)S(1)} %pad_maximum_fusion), channel_id=1, source_target_pairs={{0,1},{1,2},{2,3},{3,4},{4,5},{5,6},{6,7},{7,8},{8,9},{9,10},{10,1... | collective-permute-start | bytes 393224 | tf_op jit(solution)/shard_map/ppermute | solution.py:17
Sparse Core Ops, SparseCore 0:
  10.2 108.3 all-gather.1

commit v10 on v7

--- a/solution.py
+++ b/solution.py
@@ -160,6 +160,12 @@
     return lax.all_gather(own.T, ("ctx", "dp"), axis=0, tiled=True)
 
 
+def norm_rows(rows, norm_gain):
+    flat = rows.astype(jnp.float32)
+    scale = lax.rsqrt(jnp.mean(flat * flat, axis=-1, keepdims=True) + 1e-05)
+    return (flat * scale * norm_gain[None, :]).astype(jnp.bfloat16)
+
+
 def on_device(
     tokens, positions, norm_gain, qkv_weight, qkv_bias, sinks, earlier_keys, earlier_values
 ):
@@ -167,20 +173,31 @@
     query_group = QUERY_HEADS // KEY_VALUE_HEADS
     query_length = QUERY_HEADS * HEAD_SIZE
     key_length = KEY_VALUE_HEADS * HEAD_SIZE
-    flat = tokens.astype(jnp.float32)
-    scale = lax.rsqrt(jnp.mean(flat * flat, axis=-1, keepdims=True) + 1e-05)
-    normed = (flat * scale * norm_gain[None, :]).astype(jnp.bfloat16)
+    rim_tokens = shifted(tokens[token_rows - WINDOW_TOKENS :], "ctx", 1)
+    rim_positions = shifted(positions[token_rows - WINDOW_TOKENS :], "ctx", 1)
+    normed = norm_rows(tokens, norm_gain)
+    rim_normed = norm_rows(rim_tokens, norm_gain)
     tables = rotation_tables(positions, 128) + (
         jnp.minimum(positions, WINDOW_TOKENS - 1).astype(jnp.int32)[:, None],
     )
-    normed, tables = lax.optimization_barrier((normed, tables))
+    normed, rim_normed, tables = lax.optimization_barrier((normed, rim_normed, tables))
+    weight_rows = gather_weight(qkv_weight)
     combined_output = lax.dot_general(
-        normed,
-        gather_weight(qkv_weight),
+        normed, weight_rows, (((1,), (1,)), ((), ())), preferred_element_type=jnp.float32
+    )
+    combined_output = combined_output + qkv_bias[None, :]
+    rim_output = lax.dot_general(
+        rim_normed,
+        weight_rows[query_length:],
         (((1,), (1,)), ((), ())),
         preferred_element_type=jnp.float32,
     )
-    combined_output = combined_output + qkv_bias[None, :]
+    rim_output = rim_output + qkv_bias[None, query_length:]
+    rim_keys = apply_rotation(
+        rim_output[:, :key_length].reshape(WINDOW_TOKENS, KEY_VALUE_HEADS, HEAD_SIZE), rim_positions
+    ).astype(jnp.bfloat16)
+    rim_values = rim_output[:, key_length:].astype(jnp.bfloat16)
+    computed_rim = jnp.stack([rim_keys.reshape(WINDOW_TOKENS, key_length), rim_values])
     key_rows = apply_rotation(
         combined_output[:, query_length : query_length + key_length].reshape(
             token_rows, KEY_VALUE_HEADS, HEAD_SIZE
@@ -189,9 +206,8 @@
     ).astype(jnp.bfloat16)
     value_rows = combined_output[:, query_length + key_length :].astype(jnp.bfloat16)
     window_output = jnp.stack([key_rows.reshape(token_rows, key_length), value_rows])
-    received = send_rim(window_output, token_rows)
     prior = jnp.stack([earlier_keys, earlier_values])
-    border_tokens = jnp.where(lax.axis_index("ctx") == 0, prior, received)
+    border_tokens = jnp.where(lax.axis_index("ctx") == 0, prior, computed_rim)
     padded_rows = jnp.concatenate([border_tokens, window_output], axis=1).reshape(
         2, WINDOW_TOKENS + token_rows, KEY_VALUE_HEADS, HEAD_SIZE
     )

time: 159 us -> 162 us (1.019); the launches traced: 159 us -> 160 us
  waiting for transfers between devices: 111 us -> 101 us
  starting transfers between devices: 2.47 us -> 6.82 us
  matrix products: 8.05 us -> 11.1 us
  local copies, waits for them, and re-layouts: 8.25 us -> 10.5 us
    all_gather x1, waiting for transfers between devices: 107 us -> 85.5 us  [gather_weight(): return lax.all_gather(own.T, ('ctx', 'dp'), axis=0, tiled=True)]
    ppermute x1 -> x2, waiting for transfers between devices: 3.69 us -> 15.6 us  [shifted(): lax.ppermute(value, axis, [(source, source + steps) for source in range(l...]
    ppermute x1 -> x2, starting transfers between devices: 2.47 us -> 6.79 us  [shifted(): lax.ppermute(value, axis, [(source, source + steps) for source in range(l...]
    dot_general x1 -> x2, matrix products: 8.05 us -> 11.1 us  [the longest x1 7.92 us: on_device(): lax.dot_general(normed, weight_rows, (((1,), (1,)), ((), ())), preferred_...]
    slice x0 -> x6, local copies, waits for them, and re-layouts: none -> 2.14 us  [the longest x1 2.03 us: on_device(): rim_tokens = shifted(tokens[token_rows - WINDOW_TOKENS:], 'ctx', 1)]
  transfers between devices with their start and end apart: 2 -> 3, of which waited for: 2 -> 2; matrix products, arithmetic and copies ran while one was open for 3% -> 5% of each run, Pallas kernels for 0% -> 0%
where the time goes in v10:
time: 162 us; the launch traced here: 160 us
  waiting for transfers between devices  101 us (62%)
  between operations  13.7 us (8%)
  Pallas kernels  12.8 us (8%)
  matrix products  11.1 us (7%)
  local copies, waits for them, and re-layouts  10.5 us (6%)
  starting transfers between devices  6.82 us (4%)
  other arithmetic  4.22 us (3%)
    all_gather x1, waiting for transfers between devices, gather_weight(): return lax.all_gather(own.T, ('ctx', 'dp'), axis=0, tiled=True)  85.5 us
    ppermute x2, waiting for transfers between devices, shifted(): lax.ppermute(value, axis, [(source, source + steps) for source in range(l...  15.6 us
    pallas_call x1, Pallas kernels, attend(): pl.pallas_call(attention_kernel, grid=(KEY_VALUE_HEADS,), in_specs=[pl.Bl...  12.8 us
    dot_general x1, matrix products, on_device(): lax.dot_general(normed, weight_rows, (((1,), (1,)), ((), ())), preferred_...  7.92 us
    ppermute x2, starting transfers between devices, shifted(): lax.ppermute(value, axis, [(source, source + steps) for source in range(l...  6.79 us
  transfers between devices with their start and end apart: 3, of which 2 were waited for; matrix products, arithmetic and copies ran while one was open for 5% of the time, Pallas kernels for 0%

profile of v10, /device:TPU:4, one launch (start us, length us, event | category | flops | bytes accessed | tf_op | source)
XLA Modules:
  0.0 160.3 jit_solution(15697450952587467481)
XLA Ops:
  6.5 0.0 copy-start
  6.5 0.0 copy-start.1
  6.5 0.0 copy-start.8
  6.5 0.0 copy-start.6
  6.5 0.0 all-gather.2.cloned.1.call-start
  6.6 1.1 copy-done
  7.7 0.8 dynamic-slice_bitcast_fusion
  8.5 0.0 all-gather.2.cloned.1.call-update
  8.6 2.0 %slice.46 = bf16[128,2880]{0,1:T(8,128)(2,1)} slice(bf16[256,2880]{0,1:T(8,128)(2,1)} %param.8), slice={[128:256], [0:2880]} | slice | bytes 1474560 | tf_op jit(solution)/shard_map/slice | solution.py:176
  10.6 3.4 %collective-permute-start = (bf16[128,2880]{0,1:T(8,128)(2,1)}, bf16[128,2880]{0,1:T(8,128)(2,1)S(1)}, u32[]{:S(2)}, u32[]{:S(2)}) collective-permute-start(bf16[128,2880]{0,1:T(8,128)(2,1)} %slice.46), channel_id=1, source_target_pairs={{0,1},{1,2},{2,3},{3,4},{4,5},{5,6},{6,7},{7,8},{8,9},{9,10},{10,1... | collective-permute-start | bytes 2211848 | tf_op jit(solution)/shard_map/ppermute | solution.py:17
  14.0 0.0 copy-done.8
  14.0 3.4 %collective-permute-start.1 = (s32[128]{0:T(128)S(1)}, s32[128]{0:T(128)S(1)}, u32[]{:S(2)}, u32[]{:S(2)}) collective-permute-start(s32[128]{0:T(128)S(1)} %slice.51), channel_id=1, source_target_pairs={{0,1},{1,2},{2,3},{3,4},{4,5},{5,6},{6,7},{7,8},{8,9},{9,10},{10,1... | collective-permute-start | bytes 1544 | tf_op jit(solution)/shard_map/ppermute | solution.py:17
  17.4 0.0 copy-done.1
  17.4 0.4 fusion.2
  17.9 0.0 copy-done.6
  17.9 0.0 slice-start
  17.9 1.6 fusion.4
  19.5 0.2 fusion.13
  19.7 15.6 %collective-permute-done.1 = s32[128]{0:T(128)S(1)} collective-permute-done((s32[128]{0:T(128)S(1)}, s32[128]{0:T(128)S(1)}, u32[]{:S(2)}, u32[]{:S(2)}) %collective-permute-start.1) | collective-permute-done | bytes 544 | tf_op jit(solution)/shard_map/ppermute | solution.py:17
  35.3 0.1 multiply_cosine_fusion.1
  35.4 0.0 collective-permute-done
  35.4 0.4 fusion.5
  35.8 1.3 fusion.7
  37.2 0.8 copy.17.limit_ref
  38.0 0.8 copy.18.cos_ref
  38.7 0.8 copy.19.sin_ref
  39.5 0.0 copy-start.3
  39.5 0.0 copy-start.7
  39.5 85.5 %all-gather.2.cloned.1.call-done = bf16[2560,2880]{1,0:T(8,128)(2,1)} async-done(((bf16[80,2880]{1,0:T(8,128)(2,1)}), bf16[2560,2880]{1,0:T(8,128)(2,1)}) %all-gather.2.cloned.1.call-update) | async-done | bytes 14745616 | tf_op jit(solution)/shard_map/all_gather | solution.py:160
  125.0 0.0 slice-done
  125.0 3.2 %fusion.8 = f32[128,512]{1,0:T(8,128)S(1)} fusion(bf16[128,2880]{0,1:T(8,128)(2,1)} %fusion.7, bf16[2560,2880]{1,0:T(8,128)(2,1)} %all-gather.2.cloned.1.call-done, f32[512]{0:T(512)S(1)} %slice-done), kind=kOutput, calls=%fused_computation.13 | convolution fusion | flops 377552896 | bytes 4016128 | tf_op jit(solution)/shard_map/dot_general | solution.py:189
  128.2 0.0 copy-done.3
  128.2 0.0 copy-done.7
  128.2 7.9 %convolution_add_fusion.q_ref = f32[256,2560]{1,0:T(8,128)S(1)} fusion(bf16[256,2880]{0,1:T(8,128)(2,1)S(1)} %copy-done.3, bf16[2560,2880]{1,0:T(8,128)(2,1)} %all-gather.2.cloned.1.call-done, f32[2560]{0:T(1024)S(1)} %copy-done.7), kind=kOutput, calls=%fused_computation | convolution fusion | flops 3775528960 | bytes 18851840 | tf_op jit(solution)/shard_map/dot_general | solution.py:185
  136.2 0.0 copy-start.2
  136.2 0.0 copy-start.4
  136.2 0.0 copy-start.5
  136.2 1.4 copy-done.2
  137.7 0.1 copy.9
  137.8 0.1 copy.10
  137.9 0.1 copy.11
  138.1 0.1 copy.12
  138.3 0.0 copy-done.4
  138.3 0.0 copy-done.5
  138.4 0.2 copy.13
  138.6 0.9 copy.14
  139.5 0.2 copy.15
  139.7 0.9 copy.16
  140.6 12.8 %shard_map.82 = bf16[256,2048]{1,0:T(8,128)(2,1)} custom-call(f32[32]{0:T(128)} %sinks_ref.1, s32[256,1]{1,0:T(8,128)} %copy.17.limit_ref, f32[256,128]{1,0:T(8,128)} %copy.18.cos_ref, f32[256,128]{1,0:T(8,128)} %copy.19.sin_ref, f32[256,2560]{1,0:T(8,128)} %copy-done.2, bf16[4,384,64]{2,1,0:T(8,128)(2,1)} %bitcast.22, bf16[4,384,64]{2,1,0:T(8,128)(2,1)} %bitcast.23), custom_call_target="tpu_custom_call" | custom-call | tf_op jit(solution)/shard_map/pallas_call | solution.py:116
  (20 shorter events, 0.3 us)
Async XLA Ops:
  6.5 1.2 copy-start
  6.5 10.9 %copy-start.1 = (bf16[256,2880]{0,1:T(8,128)(2,1)S(1)}, bf16[256,2880]{0,1:T(8,128)(2,1)}, u32[]{:S(2)}) copy-start(bf16[256,2880]{0,1:T(8,128)(2,1)} %param.8) | copy-start | bytes 4423684
  6.5 7.5 %copy-start.8 = (s32[256]{0:T(256)S(1)}, s32[256]{0:T(256)}, u32[]{:S(2)}) copy-start(s32[256]{0:T(256)} %param.9) | copy-start | bytes 3076
  6.5 11.3 %copy-start.6 = (f32[2880]{0:T(1024)S(1)}, f32[2880]{0:T(1024)}, u32[]{:S(2)}) copy-start(f32[2880]{0:T(1024)} %param.10) | copy-start | bytes 34564
  6.5 118.4 %all-gather.2.cloned.1.call-start = ((), (), s32[]{:S(2)}) async-start(), calls=%async_computation | async-start | bytes 15544320 | tf_op jit(solution)/shard_map/all_gather | solution.py:160
  10.6 24.8 %collective-permute-start = (bf16[128,2880]{0,1:T(8,128)(2,1)}, bf16[128,2880]{0,1:T(8,128)(2,1)S(1)}, u32[]{:S(2)}, u32[]{:S(2)}) collective-permute-start(bf16[128,2880]{0,1:T(8,128)(2,1)} %slice.46), channel_id=1, source_target_pairs={{0,1},{1,2},{2,3},{3,4},{4,5},{5,6},{6,7},{7,8},{8,9},{9,10},{10,1... | collective-permute-start | bytes 2211848 | tf_op jit(solution)/shard_map/ppermute | solution.py:17
  14.0 21.2 %collective-permute-start.1 = (s32[128]{0:T(128)S(1)}, s32[128]{0:T(128)S(1)}, u32[]{:S(2)}, u32[]{:S(2)}) collective-permute-start(s32[128]{0:T(128)S(1)} %slice.51), channel_id=1, source_target_pairs={{0,1},{1,2},{2,3},{3,4},{4,5},{5,6},{6,7},{7,8},{8,9},{9,10},{10,1... | collective-permute-start | bytes 1544 | tf_op jit(solution)/shard_map/ppermute | solution.py:17
  17.9 107.1 %slice-start = ((f32[2560]{0:T(1024)}), f32[512]{0:T(512)S(1)}, s32[]{:S(2)}) async-start(f32[2560]{0:T(1024)} %param.12), calls=%async_computation.1 | async-start | bytes 4096 | tf_op jit(solution)/shard_map/slice | solution.py:195
  39.5 88.7 %copy-start.3 = (bf16[256,2880]{0,1:T(8,128)(2,1)S(1)}, bf16[256,2880]{0,1:T(8,128)(2,1)}, u32[]{:S(2)}) copy-start(bf16[256,2880]{0,1:T(8,128)(2,1)} %fusion.4) | copy-start | bytes 4423684
  39.5 88.7 %copy-start.7 = (f32[2560]{0:T(1024)S(1)}, f32[2560]{0:T(1024)}, u32[]{:S(2)}) copy-start(f32[2560]{0:T(1024)} %param.12) | copy-start | bytes 30724
  136.2 1.5 copy-start.2
  136.2 2.1 %copy-start.4 = (bf16[128,256]{1,0:T(8,128)(2,1)S(1)}, bf16[128,256]{1,0:T(8,128)(2,1)}, u32[]{:S(2)}) copy-start(bf16[128,256]{1,0:T(8,128)(2,1)} %param.15) | copy-start | bytes 196612
  136.2 2.1 %copy-start.5 = (bf16[128,256]{1,0:T(8,128)(2,1)S(1)}, bf16[128,256]{1,0:T(8,128)(2,1)}, u32[]{:S(2)}) copy-start(bf16[128,256]{1,0:T(8,128)(2,1)} %param.14) | copy-start | bytes 196612
Sparse Core Ops, SparseCore 0:
  10.2 114.6 all-gather.1

commit v11 on v7

--- a/solution.py
+++ b/solution.py
@@ -174,20 +174,26 @@
         jnp.minimum(positions, WINDOW_TOKENS - 1).astype(jnp.int32)[:, None],
     )
     normed, tables = lax.optimization_barrier((normed, tables))
+    weight_rows = gather_weight(qkv_weight)
+    key_value_output = lax.dot_general(
+        normed,
+        weight_rows[query_length:],
+        (((1,), (1,)), ((), ())),
+        preferred_element_type=jnp.float32,
+    )
+    key_value_output = key_value_output + qkv_bias[None, query_length:]
+    key_rows = apply_rotation(
+        key_value_output[:, :key_length].reshape(token_rows, KEY_VALUE_HEADS, HEAD_SIZE),
+        positions,
+    ).astype(jnp.bfloat16)
+    value_rows = key_value_output[:, key_length:].astype(jnp.bfloat16)
     combined_output = lax.dot_general(
         normed,
-        gather_weight(qkv_weight),
+        weight_rows[:query_length],
         (((1,), (1,)), ((), ())),
         preferred_element_type=jnp.float32,
     )
-    combined_output = combined_output + qkv_bias[None, :]
-    key_rows = apply_rotation(
-        combined_output[:, query_length : query_length + key_length].reshape(
-            token_rows, KEY_VALUE_HEADS, HEAD_SIZE
-        ),
-        positions,
-    ).astype(jnp.bfloat16)
-    value_rows = combined_output[:, query_length + key_length :].astype(jnp.bfloat16)
+    combined_output = combined_output + qkv_bias[None, :query_length]
     window_output = jnp.stack([key_rows.reshape(token_rows, key_length), value_rows])
     received = send_rim(window_output, token_rows)
     prior = jnp.stack([earlier_keys, earlier_values])

time: 159 us -> 159 us (level); the launches traced: 159 us -> 156 us
  waiting for transfers between devices: 111 us -> 103 us
  matrix products: 8.05 us -> 12.7 us
    dot_general x1 -> x2, matrix products: 8.05 us -> 12.7 us  [the longest x1 9.37 us: on_device(): lax.dot_general(normed, weight_rows[:query_length], (((1,), (1,)), ((), (...]
    ppermute x1, waiting for transfers between devices: 3.69 us -> 0.01 us  [shifted(): lax.ppermute(value, axis, [(source, source + steps) for source in range(l...]
    all_gather x1, waiting for transfers between devices: 107 us -> 103 us  [gather_weight(): return lax.all_gather(own.T, ('ctx', 'dp'), axis=0, tiled=True)]
  transfers between devices with their start and end apart: 2 -> 2, of which waited for: 2 -> 1; matrix products, arithmetic and copies ran while one was open for 3% -> 10% of each run, Pallas kernels for 0% -> 0%
where the time goes in v11:
time: 159 us; the launch traced here: 156 us
  waiting for transfers between devices  103 us (65%)
  between operations  13.6 us (9%)
  Pallas kernels  12.8 us (8%)
  matrix products  12.7 us (8%)
  local copies, waits for them, and re-layouts  6.86 us (4%)
  other arithmetic  4.47 us (3%)
  starting transfers between devices  2.6 us (2%)
    all_gather x1, waiting for transfers between devices, gather_weight(): return lax.all_gather(own.T, ('ctx', 'dp'), axis=0, tiled=True)  103 us
    pallas_call x1, Pallas kernels, attend(): pl.pallas_call(attention_kernel, grid=(KEY_VALUE_HEADS,), in_specs=[pl.Bl...  12.8 us
    dot_general x1, matrix products, on_device(): lax.dot_general(normed, weight_rows[:query_length], (((1,), (1,)), ((), (...  9.37 us
    dot_general x1, matrix products, on_device(): lax.dot_general(normed, weight_rows[query_length:], (((1,), (1,)), ((), (...  3.32 us
  transfers between devices with their start and end apart: 2, of which 1 were waited for; matrix products, arithmetic and copies ran while one was open for 10% of the time, Pallas kernels for 0%

profile of v11, /device:TPU:4, one launch (start us, length us, event | category | flops | bytes accessed | tf_op | source)
XLA Modules:
  0.0 156.4 jit_solution(7022806733039617933)
XLA Ops:
  6.5 0.0 copy-start
  6.5 0.0 copy-start.1
  6.5 0.0 copy-start.5
  6.5 0.0 all-gather.2.cloned.1.call-start
  6.6 1.2 copy-done
  7.7 0.8 dynamic-slice_bitcast_fusion
  8.5 0.0 all-gather.2.cloned.1.call-update
  8.6 0.0 slice-start.1
  8.6 0.8 broadcast_minimum_fusion
  9.3 0.2 fusion.14
  9.6 1.8 %fusion.4 = f32[256]{0:T(256)S(1)} fusion(bf16[256,2880]{0,1:T(8,128)(2,1)} %param.8), kind=kLoop, calls=%fused_computation.6 | loop fusion | flops 2211584 | bytes 1475584 | tf_op jit(solution)/shard_map/reduce_sum | solution.py:171
  11.4 0.0 copy-done.1
  11.4 0.0 copy-done.5
  11.4 1.6 %fusion.6 = bf16[256,2880]{0,1:T(8,128)(2,1)} fusion(bf16[256,2880]{0,1:T(8,128)(2,1)S(1)} %copy-done.1, f32[2880]{0:T(1024)S(1)} %copy-done.5, f32[256]{0:T(256)S(1)} %add_rsqrt_fusion), kind=kLoop, calls=%fused_computation.8 | loop fusion | flops 2949120 | bytes 2961664 | tf_op jit(solution)/shard_map/convert_element_type | solution.py:172
  13.0 0.8 copy.15.limit_ref
  13.8 0.8 copy.16.cos_ref
  14.6 0.8 copy.17.sin_ref
  15.3 0.0 copy-start.2
  15.3 0.0 slice-start
  15.3 103.3 %all-gather.2.cloned.1.call-done = bf16[2560,2880]{1,0:T(8,128)(2,1)} async-done(((bf16[80,2880]{1,0:T(8,128)(2,1)}), bf16[2560,2880]{1,0:T(8,128)(2,1)}) %all-gather.2.cloned.1.call-update) | async-done | bytes 14745616 | tf_op jit(solution)/shard_map/all_gather | solution.py:160
  118.6 0.0 slice-done.1
  118.6 3.3 %fusion.10 = f32[256,512]{1,0:T(8,128)S(1)} fusion(bf16[256,2880]{0,1:T(8,128)(2,1)} %fusion.6, bf16[2560,2880]{1,0:T(8,128)(2,1)} %all-gather.2.cloned.1.call-done, f32[512]{0:T(512)S(1)} %slice-done.1), kind=kOutput, calls=%fused_computation.10 | convolution fusion | flops 755105792 | bytes 5015552 | tf_op jit(solution)/shard_map/dot_general | solution.py:178
  122.0 0.1 copy.9
  122.2 0.1 copy.10
  122.3 0.0 copy-start.3
  122.3 0.0 copy-start.4
  122.4 2.6 %collective-permute-start = (bf16[2,128,256]{2,1,0:T(8,128)(2,1)S(1)}, bf16[2,128,256]{2,1,0:T(8,128)(2,1)S(1)}, u32[]{:S(2)}, u32[]{:S(2)}) collective-permute-start(bf16[2,128,256]{2,1,0:T(8,128)(2,1)S(1)} %pad_maximum_fusion), channel_id=1, source_target_pairs={{0,1},{1,2},{2,3},{3,4},{4,5},{5,6},{6,7},{7,8},{8,9},{9,10},{10,1... | collective-permute-start | bytes 393224 | tf_op jit(solution)/shard_map/ppermute | solution.py:17
  125.0 0.0 copy-done.2
  125.0 0.0 slice-done
  125.0 9.4 %fusion.7.q_ref = f32[256,2048]{1,0:T(8,128)} fusion(bf16[256,2880]{0,1:T(8,128)(2,1)S(1)} %copy-done.2, bf16[2560,2880]{1,0:T(8,128)(2,1)} %all-gather.2.cloned.1.call-done, f32[2048]{0:T(1024)S(1)} %slice-done), kind=kOutput, calls=%fused_computation.9 | convolution fusion | flops 3020423168 | bytes 15638528 | tf_op jit(solution)/shard_map/dot_general | solution.py:190
  134.3 0.0 collective-permute-done
  134.4 0.0 copy-done.3
  134.4 0.0 copy-done.4
  134.5 0.2 copy.11
  134.6 0.9 copy.12
  135.6 0.2 copy.13
  135.7 0.9 copy.14
  136.7 12.8 %shard_map.82 = bf16[256,2048]{1,0:T(8,128)(2,1)} custom-call(f32[32]{0:T(128)} %sinks_ref.1, s32[256,1]{1,0:T(8,128)} %copy.15.limit_ref, f32[256,128]{1,0:T(8,128)} %copy.16.cos_ref, f32[256,128]{1,0:T(8,128)} %copy.17.sin_ref, f32[256,2048]{1,0:T(8,128)} %fusion.7.q_ref, bf16[4,384,64]{2,1,0:T(8,128)(2,1)} %bitcast.17, bf16[4,384,64]{2,1,0:T(8,128)(2,1)} %bitcast.18), custom_call_target="tpu_custom_call" | custom-call | tf_op jit(solution)/shard_map/pallas_call | solution.py:116
  (13 shorter events, 0.2 us)
Async XLA Ops:
  6.5 1.2 copy-start
  6.5 4.8 %copy-start.1 = (bf16[256,2880]{0,1:T(8,128)(2,1)S(1)}, bf16[256,2880]{0,1:T(8,128)(2,1)}, u32[]{:S(2)}) copy-start(bf16[256,2880]{0,1:T(8,128)(2,1)} %param.8) | copy-start | bytes 4423684
  6.5 4.8 %copy-start.5 = (f32[2880]{0:T(1024)S(1)}, f32[2880]{0:T(1024)}, u32[]{:S(2)}) copy-start(f32[2880]{0:T(1024)} %param.10) | copy-start | bytes 34564
  6.5 112.1 %all-gather.2.cloned.1.call-start = ((), (), s32[]{:S(2)}) async-start(), calls=%async_computation | async-start | bytes 15544320 | tf_op jit(solution)/shard_map/all_gather | solution.py:160
  8.6 110.1 %slice-start.1 = ((f32[2560]{0:T(1024)}), f32[512]{0:T(512)S(1)}, s32[]{:S(2)}) async-start(f32[2560]{0:T(1024)} %param.12), calls=%async_computation.2 | async-start | bytes 4096 | tf_op jit(solution)/shard_map/slice | solution.py:184
  15.3 109.7 %copy-start.2 = (bf16[256,2880]{0,1:T(8,128)(2,1)S(1)}, bf16[256,2880]{0,1:T(8,128)(2,1)}, u32[]{:S(2)}) copy-start(bf16[256,2880]{0,1:T(8,128)(2,1)} %fusion.6) | copy-start | bytes 4423684
  15.3 109.7 %slice-start = ((f32[2560]{0:T(1024)}), f32[2048]{0:T(1024)S(1)}, s32[]{:S(2)}) async-start(f32[2560]{0:T(1024)} %param.12), calls=%async_computation.1 | async-start | bytes 16384 | tf_op jit(solution)/shard_map/slice | solution.py:196
  122.3 12.0 %copy-start.3 = (bf16[128,256]{1,0:T(8,128)(2,1)S(1)}, bf16[128,256]{1,0:T(8,128)(2,1)}, u32[]{:S(2)}) copy-start(bf16[128,256]{1,0:T(8,128)(2,1)} %param.15) | copy-start | bytes 196612
  122.3 12.0 %copy-start.4 = (bf16[128,256]{1,0:T(8,128)(2,1)S(1)}, bf16[128,256]{1,0:T(8,128)(2,1)}, u32[]{:S(2)}) copy-start(bf16[128,256]{1,0:T(8,128)(2,1)} %param.14) | copy-start | bytes 196612
  122.4 12.0 %collective-permute-start = (bf16[2,128,256]{2,1,0:T(8,128)(2,1)S(1)}, bf16[2,128,256]{2,1,0:T(8,128)(2,1)S(1)}, u32[]{:S(2)}, u32[]{:S(2)}) collective-permute-start(bf16[2,128,256]{2,1,0:T(8,128)(2,1)S(1)} %pad_maximum_fusion), channel_id=1, source_target_pairs={{0,1},{1,2},{2,3},{3,4},{4,5},{5,6},{6,7},{7,8},{8,9},{9,10},{10,1... | collective-permute-start | bytes 393224 | tf_op jit(solution)/shard_map/ppermute | solution.py:17
Sparse Core Ops, SparseCore 0:
  10.2 108.3 all-gather.1

commit v12 on v7

--- a/solution.py
+++ b/solution.py
@@ -44,9 +44,9 @@
 
 
 def attention_kernel(sinks_ref, limit_ref, cos_ref, sin_ref, q_ref, k_ref, v_ref, out_ref):
-    group = pl.program_id(0)
     rows = q_ref.shape[0]
-    query_group = q_ref.shape[1] // HEAD_SIZE
+    query_group = QUERY_HEADS // KEY_VALUE_HEADS
+    group_width = query_group * HEAD_SIZE
     half = HEAD_SIZE // 2
     lanes = cos_ref.shape[1]
     cosine = cos_ref[...]
@@ -64,32 +64,34 @@
         limit = limit_ref[part * block : (part + 1) * block, :]
         visible.append((rel >= 0) & (rel <= limit))
     heads_per_chunk = lanes // HEAD_SIZE
-    for chunk in range(q_ref.shape[1] // lanes):
-        x = q_ref[:, chunk * lanes : (chunk + 1) * lanes]
-        first = pltpu.roll(x, half, 1)
-        second = pltpu.roll(x, lanes - half, 1)
-        partner = jnp.where(take_first, first, second)
-        rotated = ((x * cosine + partner * sine) * HEAD_SIZE ** (-0.5)).astype(jnp.bfloat16)
-        for inner in range(heads_per_chunk):
-            head = chunk * heads_per_chunk + inner
-            sink = sinks_ref[group * query_group + head]
-            query_head = rotated[:, inner * HEAD_SIZE : (inner + 1) * HEAD_SIZE]
-            for part in range(rows // block):
-                queries = query_head[part * block : (part + 1) * block]
-                keys = k_ref[0, part * block : part * block + 2 * block, :]
-                values = v_ref[0, part * block : part * block + 2 * block, :]
-                scores = lax.dot_general(
-                    queries, keys, (((1,), (1,)), ((), ())), preferred_element_type=jnp.float32
-                )
-                scores = jnp.where(visible[part], scores, -1e30)
-                top = jnp.maximum(jnp.max(scores, axis=1, keepdims=True), sink)
-                expo = jnp.exp(scores - top)
-                total = jnp.sum(expo, axis=1, keepdims=True) + jnp.exp(sink - top)
-                probs = (expo * (1.0 / total)).astype(jnp.bfloat16)
-                out = jnp.dot(probs, values, preferred_element_type=jnp.float32)
-                out_ref[part * block : (part + 1) * block, head * HEAD_SIZE : (head + 1) * HEAD_SIZE] = out.astype(
-                    jnp.bfloat16
-                )
+    for group in range(KEY_VALUE_HEADS):
+        for chunk in range(group_width // lanes):
+            offset = group * group_width + chunk * lanes
+            x = q_ref[:, offset : offset + lanes]
+            first = pltpu.roll(x, half, 1)
+            second = pltpu.roll(x, lanes - half, 1)
+            partner = jnp.where(take_first, first, second)
+            rotated = ((x * cosine + partner * sine) * HEAD_SIZE ** (-0.5)).astype(jnp.bfloat16)
+            for inner in range(heads_per_chunk):
+                head = group * query_group + chunk * heads_per_chunk + inner
+                sink = sinks_ref[head]
+                query_head = rotated[:, inner * HEAD_SIZE : (inner + 1) * HEAD_SIZE]
+                for part in range(rows // block):
+                    queries = query_head[part * block : (part + 1) * block]
+                    keys = k_ref[group, part * block : part * block + 2 * block, :]
+                    values = v_ref[group, part * block : part * block + 2 * block, :]
+                    scores = lax.dot_general(
+                        queries, keys, (((1,), (1,)), ((), ())), preferred_element_type=jnp.float32
+                    )
+                    scores = jnp.where(visible[part], scores, -1e30)
+                    top = jnp.maximum(jnp.max(scores, axis=1, keepdims=True), sink)
+                    expo = jnp.exp(scores - top)
+                    total = jnp.sum(expo, axis=1, keepdims=True) + jnp.exp(sink - top)
+                    probs = (expo * (1.0 / total)).astype(jnp.bfloat16)
+                    out = jnp.dot(probs, values, preferred_element_type=jnp.float32)
+                    out_ref[part * block : (part + 1) * block, head * HEAD_SIZE : (head + 1) * HEAD_SIZE] = (
+                        out.astype(jnp.bfloat16)
+                    )
 
 
 def rotation_tables(positions, lanes):
@@ -113,19 +115,11 @@
     keys = jnp.moveaxis(joined_keys, 1, 0)
     values = jnp.moveaxis(joined_values, 1, 0)
     key_rows = keys.shape[1]
+    in_vmem = pl.BlockSpec(memory_space=pltpu.VMEM)
     return pl.pallas_call(
         attention_kernel,
-        grid=(KEY_VALUE_HEADS,),
-        in_specs=[
-            pl.BlockSpec(memory_space=pltpu.SMEM),
-            pl.BlockSpec((token_rows, 1), lambda g: (0, 0)),
-            pl.BlockSpec((token_rows, lanes), lambda g: (0, 0)),
-            pl.BlockSpec((token_rows, lanes), lambda g: (0, 0)),
-            pl.BlockSpec((token_rows, group_width), lambda g: (0, g)),
-            pl.BlockSpec((1, key_rows, HEAD_SIZE), lambda g: (g, 0, 0)),
-            pl.BlockSpec((1, key_rows, HEAD_SIZE), lambda g: (g, 0, 0)),
-        ],
-        out_specs=pl.BlockSpec((token_rows, group_width), lambda g: (0, g)),
+        in_specs=[pl.BlockSpec(memory_space=pltpu.SMEM)] + [in_vmem] * 6,
+        out_specs=in_vmem,
         out_shape=jax.ShapeDtypeStruct((token_rows, QUERY_HEADS * HEAD_SIZE), jnp.bfloat16),
     )(sinks, limit, cos_table, sin_table, combined_output, keys, values)
 

time: 159 us -> 169 us (1.063)
  Pallas kernels: 12.8 us -> 22.5 us
    pallas_call x1, Pallas kernels: 12.8 us -> 22.5 us  [attend(): pl.pallas_call(attention_kernel, in_specs=[pl.BlockSpec(memory_space=pltp...]
where the time goes in v12:
time: 169 us
  waiting for transfers between devices  111 us (66%)
  Pallas kernels  22.5 us (13%)
  between operations  13.6 us (8%)
  local copies, waits for them, and re-layouts  8.25 us (5%)
  matrix products  8.06 us (5%)
  other arithmetic  3.1 us (2%)
  starting transfers between devices  2.65 us (2%)
    all_gather x1, waiting for transfers between devices, gather_weight(): return lax.all_gather(own.T, ('ctx', 'dp'), axis=0, tiled=True)  107 us
    pallas_call x1, Pallas kernels, attend(): pl.pallas_call(attention_kernel, in_specs=[pl.BlockSpec(memory_space=pltp...  22.5 us
    dot_general x1, matrix products, on_device(): lax.dot_general(normed, gather_weight(qkv_weight), (((1,), (1,)), ((), ()...  8.06 us
    ppermute x1, waiting for transfers between devices, shifted(): lax.ppermute(value, axis, [(source, source + steps) for source in range(l...  3.51 us
  transfers between devices with their start and end apart: 2, of which 2 were waited for; matrix products, arithmetic and copies ran while one was open for 3% of the time, Pallas kernels for 0%

profile of v12, /device:TPU:4, one launch (start us, length us, event | category | flops | bytes accessed | tf_op | source)
XLA Modules:
  0.0 168.6 jit_solution(7059916949070953307)
XLA Ops:
  6.5 0.0 copy-start
  6.5 0.0 copy-start.1
  6.5 0.0 copy-start.5
  6.5 0.0 all-gather.2.cloned.1.call-start
  6.6 1.2 copy-done
  7.7 0.8 dynamic-slice_bitcast_fusion
  8.5 0.0 all-gather.2.cloned.1.call-update
  8.6 0.0 copy-start.6
  8.6 0.8 broadcast_minimum_fusion
  9.3 0.2 fusion.4
  9.6 0.0 copy-done.1
  9.6 0.4 fusion
  10.0 0.0 copy-done.5
  10.0 1.6 fusion.2
  11.6 107.0 %all-gather.2.cloned.1.call-done = bf16[2560,2880]{1,0:T(8,128)(2,1)} async-done(((bf16[80,2880]{1,0:T(8,128)(2,1)}), bf16[2560,2880]{1,0:T(8,128)(2,1)}) %all-gather.2.cloned.1.call-update) | async-done | bytes 14745616 | tf_op jit(solution)/shard_map/all_gather | solution.py:154
  118.6 0.0 copy-done.6
  118.6 8.1 %convolution_add_fusion.q_ref = f32[256,2560]{1,0:T(8,128)S(1)} fusion(bf16[256,2880]{0,1:T(8,128)(2,1)} %fusion.2, bf16[2560,2880]{1,0:T(8,128)(2,1)} %all-gather.2.cloned.1.call-done, f32[2560]{0:T(1024)S(1)} %copy-done.6), kind=kOutput, calls=%fused_computation | convolution fusion | flops 3775528960 | bytes 18851840 | tf_op jit(solution)/shard_map/dot_general | solution.py:171
  126.7 0.0 copy-start.2
  126.7 0.0 copy-start.3
  126.7 0.0 copy-start.4
  126.7 1.4 copy-done.2
  128.2 0.1 copy.9
  128.4 0.1 copy.10
  128.5 2.6 %collective-permute-start = (bf16[2,128,256]{2,1,0:T(8,128)(2,1)S(1)}, bf16[2,128,256]{2,1,0:T(8,128)(2,1)S(1)}, u32[]{:S(2)}, u32[]{:S(2)}) collective-permute-start(bf16[2,128,256]{2,1,0:T(8,128)(2,1)S(1)} %pad_maximum_fusion), channel_id=1, source_target_pairs={{0,1},{1,2},{2,3},{3,4},{4,5},{5,6},{6,7},{7,8},{8,9},{9,10},{10,1... | collective-permute-start | bytes 393224 | tf_op jit(solution)/shard_map/ppermute | solution.py:17
  131.2 0.8 copy.15.limit_ref
  132.0 0.7 copy.16.cos_ref
  132.7 0.7 copy.17.sin_ref
  133.5 3.5 %collective-permute-done = bf16[2,128,256]{2,1,0:T(8,128)(2,1)S(1)} collective-permute-done((bf16[2,128,256]{2,1,0:T(8,128)(2,1)S(1)}, bf16[2,128,256]{2,1,0:T(8,128)(2,1)S(1)}, u32[]{:S(2)}, u32[]{:S(2)}) %collective-permute-start) | collective-permute-done | bytes 131104 | tf_op jit(solution)/shard_map/ppermute | solution.py:17
  137.0 0.0 copy-done.3
  137.0 0.0 copy-done.4
  137.1 0.2 copy.13
  137.3 0.9 copy.14
  138.2 0.2 copy.11
  138.4 1.0 copy.12
  139.3 22.5 %shard_map.82 = bf16[256,2048]{1,0:T(8,128)(2,1)} custom-call(f32[32]{0:T(128)} %sinks_ref.1, s32[256,1]{1,0:T(8,128)} %copy.15.limit_ref, f32[256,128]{1,0:T(8,128)} %copy.16.cos_ref, f32[256,128]{1,0:T(8,128)} %copy.17.sin_ref, f32[256,2560]{1,0:T(8,128)} %copy-done.2, bf16[4,384,64]{2,1,0:T(8,128)(2,1)} %bitcast.18, bf16[4,384,64]{2,1,0:T(8,128)(2,1)} %bitcast.17), custom_call_target="tpu_custom_call" | custom-call | tf_op jit(solution)/shard_map/pallas_call | solution.py:119
  (13 shorter events, 0.2 us)
Async XLA Ops:
  6.5 1.2 copy-start
  6.5 3.0 %copy-start.1 = (bf16[256,2880]{0,1:T(8,128)(2,1)S(1)}, bf16[256,2880]{0,1:T(8,128)(2,1)}, u32[]{:S(2)}) copy-start(bf16[256,2880]{0,1:T(8,128)(2,1)} %param.8) | copy-start | bytes 4423684
  6.5 3.5 %copy-start.5 = (f32[2880]{0:T(1024)S(1)}, f32[2880]{0:T(1024)}, u32[]{:S(2)}) copy-start(f32[2880]{0:T(1024)} %param.10) | copy-start | bytes 34564
  6.5 112.1 %all-gather.2.cloned.1.call-start = ((), (), s32[]{:S(2)}) async-start(), calls=%async_computation | async-start | bytes 15544320 | tf_op jit(solution)/shard_map/all_gather | solution.py:154
  8.6 110.1 %copy-start.6 = (f32[2560]{0:T(1024)S(1)}, f32[2560]{0:T(1024)}, u32[]{:S(2)}) copy-start(f32[2560]{0:T(1024)} %param.12) | copy-start | bytes 30724
  126.7 1.5 copy-start.2
  126.7 10.3 %copy-start.3 = (bf16[128,256]{1,0:T(8,128)(2,1)S(1)}, bf16[128,256]{1,0:T(8,128)(2,1)}, u32[]{:S(2)}) copy-start(bf16[128,256]{1,0:T(8,128)(2,1)} %param.15) | copy-start | bytes 196612
  126.7 10.3 %copy-start.4 = (bf16[128,256]{1,0:T(8,128)(2,1)S(1)}, bf16[128,256]{1,0:T(8,128)(2,1)}, u32[]{:S(2)}) copy-start(bf16[128,256]{1,0:T(8,128)(2,1)} %param.14) | copy-start | bytes 196612
  128.5 8.5 %collective-permute-start = (bf16[2,128,256]{2,1,0:T(8,128)(2,1)S(1)}, bf16[2,128,256]{2,1,0:T(8,128)(2,1)S(1)}, u32[]{:S(2)}, u32[]{:S(2)}) collective-permute-start(bf16[2,128,256]{2,1,0:T(8,128)(2,1)S(1)} %pad_maximum_fusion), channel_id=1, source_target_pairs={{0,1},{1,2},{2,3},{3,4},{4,5},{5,6},{6,7},{7,8},{8,9},{9,10},{10,1... | collective-permute-start | bytes 393224 | tf_op jit(solution)/shard_map/ppermute | solution.py:17
Sparse Core Ops, SparseCore 0:
  10.2 108.3 all-gather.1

commit v13 on v7

--- a/solution.py
+++ b/solution.py
@@ -64,6 +64,14 @@
         limit = limit_ref[part * block : (part + 1) * block, :]
         visible.append((rel >= 0) & (rel <= limit))
     heads_per_chunk = lanes // HEAD_SIZE
+    pick_first = group % 2 == 0
+    window_keys = []
+    window_values = []
+    for part in range(rows // block):
+        key_block = k_ref[part * block : part * block + 2 * block, :]
+        value_block = v_ref[part * block : part * block + 2 * block, :]
+        window_keys.append(jnp.where(pick_first, key_block[:, :HEAD_SIZE], key_block[:, HEAD_SIZE:]))
+        window_values.append(jnp.where(pick_first, value_block[:, :HEAD_SIZE], value_block[:, HEAD_SIZE:]))
     for chunk in range(q_ref.shape[1] // lanes):
         x = q_ref[:, chunk * lanes : (chunk + 1) * lanes]
         first = pltpu.roll(x, half, 1)
@@ -76,8 +84,8 @@
             query_head = rotated[:, inner * HEAD_SIZE : (inner + 1) * HEAD_SIZE]
             for part in range(rows // block):
                 queries = query_head[part * block : (part + 1) * block]
-                keys = k_ref[0, part * block : part * block + 2 * block, :]
-                values = v_ref[0, part * block : part * block + 2 * block, :]
+                keys = window_keys[part]
+                values = window_values[part]
                 scores = lax.dot_general(
                     queries, keys, (((1,), (1,)), ((), ())), preferred_element_type=jnp.float32
                 )
@@ -110,9 +118,9 @@
     group_width = query_group * HEAD_SIZE
     cos_table, sin_table, limit = tables
     lanes = cos_table.shape[1]
-    keys = jnp.moveaxis(joined_keys, 1, 0)
-    values = jnp.moveaxis(joined_values, 1, 0)
-    key_rows = keys.shape[1]
+    key_rows = joined_keys.shape[0]
+    keys = joined_keys.reshape(key_rows, -1)
+    values = joined_values.reshape(key_rows, -1)
     return pl.pallas_call(
         attention_kernel,
         grid=(KEY_VALUE_HEADS,),
@@ -122,8 +130,8 @@
             pl.BlockSpec((token_rows, lanes), lambda g: (0, 0)),
             pl.BlockSpec((token_rows, lanes), lambda g: (0, 0)),
             pl.BlockSpec((token_rows, group_width), lambda g: (0, g)),
-            pl.BlockSpec((1, key_rows, HEAD_SIZE), lambda g: (g, 0, 0)),
-            pl.BlockSpec((1, key_rows, HEAD_SIZE), lambda g: (g, 0, 0)),
+            pl.BlockSpec((key_rows, 2 * HEAD_SIZE), lambda g: (0, g // 2)),
+            pl.BlockSpec((key_rows, 2 * HEAD_SIZE), lambda g: (0, g // 2)),
         ],
         out_specs=pl.BlockSpec((token_rows, group_width), lambda g: (0, g)),
         out_shape=jax.ShapeDtypeStruct((token_rows, QUERY_HEADS * HEAD_SIZE), jnp.bfloat16),

time: 159 us -> 158 us (level)
    squeeze x2 -> x0, local copies, waits for them, and re-layouts: 1.88 us -> none  [the longest x1 0.95 us: on_device(): padded_rows[0]]
where the time goes in v13:
time: 158 us
  waiting for transfers between devices  111 us (70%)
  between operations  13.6 us (9%)
  Pallas kernels  13.2 us (8%)
  matrix products  8.05 us (5%)
  local copies, waits for them, and re-layouts  6.81 us (4%)
  other arithmetic  3.1 us (2%)
  starting transfers between devices  2.47 us (2%)
    all_gather x1, waiting for transfers between devices, gather_weight(): return lax.all_gather(own.T, ('ctx', 'dp'), axis=0, tiled=True)  107 us
    pallas_call x1, Pallas kernels, attend(): pl.pallas_call(attention_kernel, grid=(KEY_VALUE_HEADS,), in_specs=[pl.Bl...  13.2 us
    dot_general x1, matrix products, on_device(): lax.dot_general(normed, gather_weight(qkv_weight), (((1,), (1,)), ((), ()...  8.05 us
    ppermute x1, waiting for transfers between devices, shifted(): lax.ppermute(value, axis, [(source, source + steps) for source in range(l...  3.69 us
  transfers between devices with their start and end apart: 2, of which 2 were waited for; matrix products, arithmetic and copies ran while one was open for 3% of the time, Pallas kernels for 0%

profile of v13, /device:TPU:4, one launch (start us, length us, event | category | flops | bytes accessed | tf_op | source)
XLA Modules:
  0.0 157.9 jit_solution(11272685943707972146)
XLA Ops:
  6.5 0.0 copy-start
  6.5 0.0 copy-start.1
  6.5 0.0 copy-start.5
  6.5 0.0 all-gather.2.cloned.1.call-start
  6.6 1.2 copy-done
  7.7 0.8 dynamic-slice_bitcast_fusion
  8.5 0.0 all-gather.2.cloned.1.call-update
  8.6 0.0 copy-start.6
  8.6 0.8 broadcast_minimum_fusion
  9.3 0.2 fusion.4
  9.6 0.0 copy-done.1
  9.6 0.4 fusion
  10.0 0.0 copy-done.5
  10.0 1.6 %fusion.2 = bf16[256,2880]{0,1:T(8,128)(2,1)} fusion(bf16[256,2880]{0,1:T(8,128)(2,1)S(1)} %copy-done.1, f32[2880]{0:T(1024)S(1)} %copy-done.5, f32[256]{0:T(256)S(1)} %add_rsqrt_fusion), kind=kLoop, calls=%fused_computation.5 | loop fusion | flops 2949120 | bytes 2961664 | tf_op jit(solution)/shard_map/convert_element_type | solution.py:180
  11.6 107.0 %all-gather.2.cloned.1.call-done = bf16[2560,2880]{1,0:T(8,128)(2,1)} async-done(((bf16[80,2880]{1,0:T(8,128)(2,1)}), bf16[2560,2880]{1,0:T(8,128)(2,1)}) %all-gather.2.cloned.1.call-update) | async-done | bytes 14745616 | tf_op jit(solution)/shard_map/all_gather | solution.py:168
  118.6 0.0 copy-done.6
  118.6 8.1 %convolution_add_fusion.q_ref = f32[256,2560]{1,0:T(8,128)S(1)} fusion(bf16[256,2880]{0,1:T(8,128)(2,1)} %fusion.2, bf16[2560,2880]{1,0:T(8,128)(2,1)} %all-gather.2.cloned.1.call-done, f32[2560]{0:T(1024)S(1)} %copy-done.6), kind=kOutput, calls=%fused_computation | convolution fusion | flops 3775528960 | bytes 18851840 | tf_op jit(solution)/shard_map/dot_general | solution.py:185
  126.7 0.0 copy-start.2
  126.7 0.0 copy-start.3
  126.7 0.0 copy-start.4
  126.7 1.4 copy-done.2
  128.2 0.1 copy.9
  128.4 0.1 copy.10
  128.5 2.5 %collective-permute-start = (bf16[2,128,256]{2,1,0:T(8,128)(2,1)S(1)}, bf16[2,128,256]{2,1,0:T(8,128)(2,1)S(1)}, u32[]{:S(2)}, u32[]{:S(2)}) collective-permute-start(bf16[2,128,256]{2,1,0:T(8,128)(2,1)S(1)} %pad_maximum_fusion), channel_id=1, source_target_pairs={{0,1},{1,2},{2,3},{3,4},{4,5},{5,6},{6,7},{7,8},{8,9},{9,10},{10,1... | collective-permute-start | bytes 393224 | tf_op jit(solution)/shard_map/ppermute | solution.py:17
  131.0 0.8 copy.11.limit_ref
  131.8 0.7 copy.12.cos_ref
  132.6 0.7 copy.13.sin_ref
  133.3 3.7 %collective-permute-done = bf16[2,128,256]{2,1,0:T(8,128)(2,1)S(1)} collective-permute-done((bf16[2,128,256]{2,1,0:T(8,128)(2,1)S(1)}, bf16[2,128,256]{2,1,0:T(8,128)(2,1)S(1)}, u32[]{:S(2)}, u32[]{:S(2)}) %collective-permute-start) | collective-permute-done | bytes 131104 | tf_op jit(solution)/shard_map/ppermute | solution.py:17
  137.0 0.0 copy-done.3
  137.0 0.0 copy-done.4
  137.1 0.8 slice_bitcast_fusion
  137.8 13.2 %shard_map.82 = bf16[256,2048]{1,0:T(8,128)(2,1)} custom-call(f32[32]{0:T(128)} %sinks_ref.1, s32[256,1]{1,0:T(8,128)} %copy.11.limit_ref, f32[256,128]{1,0:T(8,128)} %copy.12.cos_ref, f32[256,128]{1,0:T(8,128)} %copy.13.sin_ref, f32[256,2560]{1,0:T(8,128)} %copy-done.2, bf16[384,256]{1,0:T(8,128)(2,1)} %get-tuple-element.14.k_ref, ...), custom_call_target="tpu_custom_call" | custom-call | tf_op jit(solution)/shard_map/pallas_call | solution.py:124
  (12 shorter events, 0.2 us)
Async XLA Ops:
  6.5 1.2 copy-start
  6.5 3.0 %copy-start.1 = (bf16[256,2880]{0,1:T(8,128)(2,1)S(1)}, bf16[256,2880]{0,1:T(8,128)(2,1)}, u32[]{:S(2)}) copy-start(bf16[256,2880]{0,1:T(8,128)(2,1)} %param.8) | copy-start | bytes 4423684
  6.5 3.5 %copy-start.5 = (f32[2880]{0:T(1024)S(1)}, f32[2880]{0:T(1024)}, u32[]{:S(2)}) copy-start(f32[2880]{0:T(1024)} %param.10) | copy-start | bytes 34564
  6.5 112.1 %all-gather.2.cloned.1.call-start = ((), (), s32[]{:S(2)}) async-start(), calls=%async_computation | async-start | bytes 15544320 | tf_op jit(solution)/shard_map/all_gather | solution.py:168
  8.6 110.1 %copy-start.6 = (f32[2560]{0:T(1024)S(1)}, f32[2560]{0:T(1024)}, u32[]{:S(2)}) copy-start(f32[2560]{0:T(1024)} %param.12) | copy-start | bytes 30724
  126.7 1.5 copy-start.2
  126.7 10.3 %copy-start.3 = (bf16[128,256]{1,0:T(8,128)(2,1)S(1)}, bf16[128,256]{1,0:T(8,128)(2,1)}, u32[]{:S(2)}) copy-start(bf16[128,256]{1,0:T(8,128)(2,1)} %param.15) | copy-start | bytes 196612
  126.7 10.3 %copy-start.4 = (bf16[128,256]{1,0:T(8,128)(2,1)S(1)}, bf16[128,256]{1,0:T(8,128)(2,1)}, u32[]{:S(2)}) copy-start(bf16[128,256]{1,0:T(8,128)(2,1)} %param.14) | copy-start | bytes 196612
  128.5 8.5 %collective-permute-start = (bf16[2,128,256]{2,1,0:T(8,128)(2,1)S(1)}, bf16[2,128,256]{2,1,0:T(8,128)(2,1)S(1)}, u32[]{:S(2)}, u32[]{:S(2)}) collective-permute-start(bf16[2,128,256]{2,1,0:T(8,128)(2,1)S(1)} %pad_maximum_fusion), channel_id=1, source_target_pairs={{0,1},{1,2},{2,3},{3,4},{4,5},{5,6},{6,7},{7,8},{8,9},{9,10},{10,1... | collective-permute-start | bytes 393224 | tf_op jit(solution)/shard_map/ppermute | solution.py:17
Sparse Core Ops, SparseCore 0:
  10.2 108.3 all-gather.1

commit v14 on v13

--- a/solution.py
+++ b/solution.py
@@ -71,7 +71,9 @@
         key_block = k_ref[part * block : part * block + 2 * block, :]
         value_block = v_ref[part * block : part * block + 2 * block, :]
         window_keys.append(jnp.where(pick_first, key_block[:, :HEAD_SIZE], key_block[:, HEAD_SIZE:]))
-        window_values.append(jnp.where(pick_first, value_block[:, :HEAD_SIZE], value_block[:, HEAD_SIZE:]))
+        value_lane = lax.broadcasted_iota(jnp.int32, value_block.shape, 1)
+        own_lanes = value_lane // HEAD_SIZE == group % 2
+        window_values.append(jnp.where(own_lanes, value_block, jnp.ones_like(value_block)))
     for chunk in range(q_ref.shape[1] // lanes):
         x = q_ref[:, chunk * lanes : (chunk + 1) * lanes]
         first = pltpu.roll(x, half, 1)
@@ -91,10 +93,12 @@
                 )
                 scores = jnp.where(visible[part], scores, -1e30)
                 top = jnp.maximum(jnp.max(scores, axis=1, keepdims=True), sink)
-                expo = jnp.exp(scores - top)
-                total = jnp.sum(expo, axis=1, keepdims=True) + jnp.exp(sink - top)
-                probs = (expo * (1.0 / total)).astype(jnp.bfloat16)
-                out = jnp.dot(probs, values, preferred_element_type=jnp.float32)
+                expo = jnp.exp(scores - top).astype(jnp.bfloat16)
+                weighted = jnp.dot(expo, values, preferred_element_type=jnp.float32)
+                swapped = pltpu.roll(weighted, HEAD_SIZE, 1)
+                numerator = jnp.where(pick_first, weighted, swapped)[:, :HEAD_SIZE]
+                total = jnp.where(pick_first, swapped, weighted)[:, :HEAD_SIZE] + jnp.exp(sink - top)
+                out = numerator * (1.0 / total)
                 out_ref[part * block : (part + 1) * block, head * HEAD_SIZE : (head + 1) * HEAD_SIZE] = out.astype(
                     jnp.bfloat16
                 )

time: 158 us -> 158 us (level)
  no operation moved by 1% of the time
where the time goes in v14:
time: 158 us; the launch traced here: 157 us
  waiting for transfers between devices  111 us (70%)
  between operations  13.6 us (9%)
  Pallas kernels  12.6 us (8%)
  matrix products  8.05 us (5%)
  local copies, waits for them, and re-layouts  6.81 us (4%)
  other arithmetic  3.1 us (2%)
  starting transfers between devices  2.47 us (2%)
    all_gather x1, waiting for transfers between devices, gather_weight(): return lax.all_gather(own.T, ('ctx', 'dp'), axis=0, tiled=True)  107 us
    pallas_call x1, Pallas kernels, attend(): pl.pallas_call(attention_kernel, grid=(KEY_VALUE_HEADS,), in_specs=[pl.Bl...  12.6 us
    dot_general x1, matrix products, on_device(): lax.dot_general(normed, gather_weight(qkv_weight), (((1,), (1,)), ((), ()...  8.05 us
    ppermute x1, waiting for transfers between devices, shifted(): lax.ppermute(value, axis, [(source, source + steps) for source in range(l...  3.69 us
  transfers between devices with their start and end apart: 2, of which 2 were waited for; matrix products, arithmetic and copies ran while one was open for 3% of the time, Pallas kernels for 0%

profile of v14, /device:TPU:4, one launch (start us, length us, event | category | flops | bytes accessed | tf_op | source)
XLA Modules:
  0.0 157.3 jit_solution(7463509333194655498)
XLA Ops:
  6.5 0.0 copy-start
  6.5 0.0 copy-start.1
  6.5 0.0 copy-start.5
  6.5 0.0 all-gather.2.cloned.1.call-start
  6.6 1.2 copy-done
  7.7 0.8 dynamic-slice_bitcast_fusion
  8.5 0.0 all-gather.2.cloned.1.call-update
  8.6 0.0 copy-start.6
  8.6 0.8 broadcast_minimum_fusion
  9.3 0.2 fusion.4
  9.6 0.0 copy-done.1
  9.6 0.4 fusion
  10.0 0.0 copy-done.5
  10.0 1.6 %fusion.2 = bf16[256,2880]{0,1:T(8,128)(2,1)} fusion(bf16[256,2880]{0,1:T(8,128)(2,1)S(1)} %copy-done.1, f32[2880]{0:T(1024)S(1)} %copy-done.5, f32[256]{0:T(256)S(1)} %add_rsqrt_fusion), kind=kLoop, calls=%fused_computation.5 | loop fusion | flops 2949120 | bytes 2961664 | tf_op jit(solution)/shard_map/convert_element_type | solution.py:184
  11.6 107.0 %all-gather.2.cloned.1.call-done = bf16[2560,2880]{1,0:T(8,128)(2,1)} async-done(((bf16[80,2880]{1,0:T(8,128)(2,1)}), bf16[2560,2880]{1,0:T(8,128)(2,1)}) %all-gather.2.cloned.1.call-update) | async-done | bytes 14745616 | tf_op jit(solution)/shard_map/all_gather | solution.py:172
  118.6 0.0 copy-done.6
  118.6 8.1 %convolution_add_fusion.q_ref = f32[256,2560]{1,0:T(8,128)S(1)} fusion(bf16[256,2880]{0,1:T(8,128)(2,1)} %fusion.2, bf16[2560,2880]{1,0:T(8,128)(2,1)} %all-gather.2.cloned.1.call-done, f32[2560]{0:T(1024)S(1)} %copy-done.6), kind=kOutput, calls=%fused_computation | convolution fusion | flops 3775528960 | bytes 18851840 | tf_op jit(solution)/shard_map/dot_general | solution.py:189
  126.7 0.0 copy-start.2
  126.7 0.0 copy-start.3
  126.7 0.0 copy-start.4
  126.7 1.4 copy-done.2
  128.2 0.1 copy.9
  128.4 0.1 copy.10
  128.5 2.5 %collective-permute-start = (bf16[2,128,256]{2,1,0:T(8,128)(2,1)S(1)}, bf16[2,128,256]{2,1,0:T(8,128)(2,1)S(1)}, u32[]{:S(2)}, u32[]{:S(2)}) collective-permute-start(bf16[2,128,256]{2,1,0:T(8,128)(2,1)S(1)} %pad_maximum_fusion), channel_id=1, source_target_pairs={{0,1},{1,2},{2,3},{3,4},{4,5},{5,6},{6,7},{7,8},{8,9},{9,10},{10,1... | collective-permute-start | bytes 393224 | tf_op jit(solution)/shard_map/ppermute | solution.py:17
  131.0 0.8 copy.11.limit_ref
  131.8 0.7 copy.12.cos_ref
  132.6 0.7 copy.13.sin_ref
  133.3 3.7 %collective-permute-done = bf16[2,128,256]{2,1,0:T(8,128)(2,1)S(1)} collective-permute-done((bf16[2,128,256]{2,1,0:T(8,128)(2,1)S(1)}, bf16[2,128,256]{2,1,0:T(8,128)(2,1)S(1)}, u32[]{:S(2)}, u32[]{:S(2)}) %collective-permute-start) | collective-permute-done | bytes 131104 | tf_op jit(solution)/shard_map/ppermute | solution.py:17
  137.0 0.0 copy-done.3
  137.0 0.0 copy-done.4
  137.1 0.8 slice_bitcast_fusion
  137.8 12.6 %shard_map.82 = bf16[256,2048]{1,0:T(8,128)(2,1)} custom-call(f32[32]{0:T(128)} %sinks_ref.1, s32[256,1]{1,0:T(8,128)} %copy.11.limit_ref, f32[256,128]{1,0:T(8,128)} %copy.12.cos_ref, f32[256,128]{1,0:T(8,128)} %copy.13.sin_ref, f32[256,2560]{1,0:T(8,128)} %copy-done.2, bf16[384,256]{1,0:T(8,128)(2,1)} %get-tuple-element.14.k_ref, ...), custom_call_target="tpu_custom_call" | custom-call | tf_op jit(solution)/shard_map/pallas_call | solution.py:128
  (12 shorter events, 0.2 us)
Async XLA Ops:
  6.5 1.2 copy-start
  6.5 3.0 %copy-start.1 = (bf16[256,2880]{0,1:T(8,128)(2,1)S(1)}, bf16[256,2880]{0,1:T(8,128)(2,1)}, u32[]{:S(2)}) copy-start(bf16[256,2880]{0,1:T(8,128)(2,1)} %param.8) | copy-start | bytes 4423684
  6.5 3.5 %copy-start.5 = (f32[2880]{0:T(1024)S(1)}, f32[2880]{0:T(1024)}, u32[]{:S(2)}) copy-start(f32[2880]{0:T(1024)} %param.10) | copy-start | bytes 34564
  6.5 112.1 %all-gather.2.cloned.1.call-start = ((), (), s32[]{:S(2)}) async-start(), calls=%async_computation | async-start | bytes 15544320 | tf_op jit(solution)/shard_map/all_gather | solution.py:172
  8.6 110.1 %copy-start.6 = (f32[2560]{0:T(1024)S(1)}, f32[2560]{0:T(1024)}, u32[]{:S(2)}) copy-start(f32[2560]{0:T(1024)} %param.12) | copy-start | bytes 30724
  126.7 1.5 copy-start.2
  126.7 10.3 %copy-start.3 = (bf16[128,256]{1,0:T(8,128)(2,1)S(1)}, bf16[128,256]{1,0:T(8,128)(2,1)}, u32[]{:S(2)}) copy-start(bf16[128,256]{1,0:T(8,128)(2,1)} %param.15) | copy-start | bytes 196612
  126.7 10.3 %copy-start.4 = (bf16[128,256]{1,0:T(8,128)(2,1)S(1)}, bf16[128,256]{1,0:T(8,128)(2,1)}, u32[]{:S(2)}) copy-start(bf16[128,256]{1,0:T(8,128)(2,1)} %param.14) | copy-start | bytes 196612
  128.5 8.5 %collective-permute-start = (bf16[2,128,256]{2,1,0:T(8,128)(2,1)S(1)}, bf16[2,128,256]{2,1,0:T(8,128)(2,1)S(1)}, u32[]{:S(2)}, u32[]{:S(2)}) collective-permute-start(bf16[2,128,256]{2,1,0:T(8,128)(2,1)S(1)} %pad_maximum_fusion), channel_id=1, source_target_pairs={{0,1},{1,2},{2,3},{3,4},{4,5},{5,6},{6,7},{7,8},{8,9},{9,10},{10,1... | collective-permute-start | bytes 393224 | tf_op jit(solution)/shard_map/ppermute | solution.py:17
Sparse Core Ops, SparseCore 0:
  10.2 108.3 all-gather.1

commit v15 on v13

--- a/solution.py
+++ b/solution.py
@@ -43,10 +43,16 @@
     return out.astype(jnp.bfloat16)
 
 
-def attention_kernel(sinks_ref, limit_ref, cos_ref, sin_ref, q_ref, k_ref, v_ref, out_ref):
+def attention_kernel(
+    sinks_ref, limit_ref, cos_ref, sin_ref, normed_ref, weight_ref, bias_ref, k_ref, v_ref, out_ref
+):
     group = pl.program_id(0)
-    rows = q_ref.shape[0]
-    query_group = q_ref.shape[1] // HEAD_SIZE
+    queries_all = lax.dot_general(
+        normed_ref[...], weight_ref[...], (((1,), (1,)), ((), ())), preferred_element_type=jnp.float32
+    )
+    queries_all = queries_all + bias_ref[...]
+    rows = queries_all.shape[0]
+    query_group = queries_all.shape[1] // HEAD_SIZE
     half = HEAD_SIZE // 2
     lanes = cos_ref.shape[1]
     cosine = cos_ref[...]
@@ -72,8 +78,8 @@
         value_block = v_ref[part * block : part * block + 2 * block, :]
         window_keys.append(jnp.where(pick_first, key_block[:, :HEAD_SIZE], key_block[:, HEAD_SIZE:]))
         window_values.append(jnp.where(pick_first, value_block[:, :HEAD_SIZE], value_block[:, HEAD_SIZE:]))
-    for chunk in range(q_ref.shape[1] // lanes):
-        x = q_ref[:, chunk * lanes : (chunk + 1) * lanes]
+    for chunk in range(queries_all.shape[1] // lanes):
+        x = queries_all[:, chunk * lanes : (chunk + 1) * lanes]
         first = pltpu.roll(x, half, 1)
         second = pltpu.roll(x, lanes - half, 1)
         partner = jnp.where(take_first, first, second)
@@ -112,8 +118,9 @@
     return cos_table, sin_table
 
 
-def attend(combined_output, joined_keys, joined_values, tables, sinks):
-    token_rows = combined_output.shape[0]
+def attend(normed, weight_rows, query_bias, joined_keys, joined_values, tables, sinks):
+    token_rows = normed.shape[0]
+    model_width = normed.shape[1]
     query_group = QUERY_HEADS // KEY_VALUE_HEADS
     group_width = query_group * HEAD_SIZE
     cos_table, sin_table, limit = tables
@@ -129,13 +136,15 @@
             pl.BlockSpec((token_rows, 1), lambda g: (0, 0)),
             pl.BlockSpec((token_rows, lanes), lambda g: (0, 0)),
             pl.BlockSpec((token_rows, lanes), lambda g: (0, 0)),
-            pl.BlockSpec((token_rows, group_width), lambda g: (0, g)),
+            pl.BlockSpec((token_rows, model_width), lambda g: (0, 0)),
+            pl.BlockSpec((group_width, model_width), lambda g: (g, 0)),
+            pl.BlockSpec((1, group_width), lambda g: (0, g)),
             pl.BlockSpec((key_rows, 2 * HEAD_SIZE), lambda g: (0, g // 2)),
             pl.BlockSpec((key_rows, 2 * HEAD_SIZE), lambda g: (0, g // 2)),
         ],
         out_specs=pl.BlockSpec((token_rows, group_width), lambda g: (0, g)),
         out_shape=jax.ShapeDtypeStruct((token_rows, QUERY_HEADS * HEAD_SIZE), jnp.bfloat16),
-    )(sinks, limit, cos_table, sin_table, combined_output, keys, values)
+    )(sinks, limit, cos_table, sin_table, normed, weight_rows, query_bias, keys, values)
 
 
 def send_rim(window_output, token_rows):
@@ -182,20 +191,19 @@
         jnp.minimum(positions, WINDOW_TOKENS - 1).astype(jnp.int32)[:, None],
     )
     normed, tables = lax.optimization_barrier((normed, tables))
-    combined_output = lax.dot_general(
+    weight_rows = gather_weight(qkv_weight)
+    key_value_output = lax.dot_general(
         normed,
-        gather_weight(qkv_weight),
+        weight_rows[query_length:],
         (((1,), (1,)), ((), ())),
         preferred_element_type=jnp.float32,
     )
-    combined_output = combined_output + qkv_bias[None, :]
+    key_value_output = key_value_output + qkv_bias[None, query_length:]
     key_rows = apply_rotation(
-        combined_output[:, query_length : query_length + key_length].reshape(
-            token_rows, KEY_VALUE_HEADS, HEAD_SIZE
-        ),
+        key_value_output[:, :key_length].reshape(token_rows, KEY_VALUE_HEADS, HEAD_SIZE),
         positions,
     ).astype(jnp.bfloat16)
-    value_rows = combined_output[:, query_length + key_length :].astype(jnp.bfloat16)
+    value_rows = key_value_output[:, key_length:].astype(jnp.bfloat16)
     window_output = jnp.stack([key_rows.reshape(token_rows, key_length), value_rows])
     received = send_rim(window_output, token_rows)
     prior = jnp.stack([earlier_keys, earlier_values])
@@ -203,7 +211,15 @@
     padded_rows = jnp.concatenate([border_tokens, window_output], axis=1).reshape(
         2, WINDOW_TOKENS + token_rows, KEY_VALUE_HEADS, HEAD_SIZE
     )
-    return attend(combined_output, padded_rows[0], padded_rows[1], tables, sinks)
+    return attend(
+        normed,
+        weight_rows,
+        qkv_bias[None, :query_length],
+        padded_rows[0],
+        padded_rows[1],
+        tables,
+        sinks,
+    )
 
 
 def solution(mesh):

time: 158 us -> 154 us (0.975)
  matrix products: 8.05 us -> 3.32 us
  waiting for transfers between devices: 111 us -> 109 us
  Pallas kernels: 13.2 us -> 15 us
    dot_general x1, matrix products: 8.05 us -> 3.32 us  [on_device(): lax.dot_general(normed, weight_rows[query_length:], (((1,), (1,)), ((), (...]
    pallas_call x1, Pallas kernels: 13.2 us -> 15 us  [attend(): pl.pallas_call(attention_kernel, grid=(KEY_VALUE_HEADS,), in_specs=[pl.Bl...]
  transfers between devices with their start and end apart: 2 -> 2, of which waited for: 2 -> 2; matrix products, arithmetic and copies ran while one was open for 3% -> 5% of each run, Pallas kernels for 0% -> 0%
where the time goes in v15:
time: 154 us
  waiting for transfers between devices  109 us (71%)
  Pallas kernels  15 us (10%)
  between operations  13.6 us (9%)
  local copies, waits for them, and re-layouts  7.79 us (5%)
  matrix products  3.32 us (2%)
  starting transfers between devices  2.47 us (2%)
  other arithmetic  2.31 us (2%)
    all_gather x1, waiting for transfers between devices, gather_weight(): return lax.all_gather(own.T, ('ctx', 'dp'), axis=0, tiled=True)  106 us
    pallas_call x1, Pallas kernels, attend(): pl.pallas_call(attention_kernel, grid=(KEY_VALUE_HEADS,), in_specs=[pl.Bl...  15 us
    dot_general x1, matrix products, on_device(): lax.dot_general(normed, weight_rows[query_length:], (((1,), (1,)), ((), (...  3.32 us
    ppermute x1, waiting for transfers between devices, shifted(): lax.ppermute(value, axis, [(source, source + steps) for source in range(l...  3.1 us
  transfers between devices with their start and end apart: 2, of which 2 were waited for; matrix products, arithmetic and copies ran while one was open for 5% of the time, Pallas kernels for 0%

profile of v15, /device:TPU:4, one launch (start us, length us, event | category | flops | bytes accessed | tf_op | source)
XLA Modules:
  0.0 153.5 jit_solution(18147395888939810439)
XLA Ops:
  6.5 0.0 copy-start
  6.5 0.0 copy-start.5
  6.5 0.0 all-gather.2.cloned.1.call-start
  6.5 1.2 copy-done
  7.7 0.0 copy-start.3
  7.7 0.8 dynamic-slice_bitcast_fusion
  8.5 0.0 all-gather.2.cloned.1.call-update
  8.6 1.8 %copy.10 = bf16[256,2880]{1,0:T(8,128)(2,1)S(1)} copy(bf16[256,2880]{0,1:T(8,128)(2,1)} %param.8) | data formatting | bytes 2949120 | tf_op args[0]
  10.4 0.0 slice-start
  10.4 0.0 copy-done.5
  10.4 0.2 fusion.9
  10.7 0.4 fusion
  11.0 0.0 copy-done.3
  11.1 1.6 %fusion.2.normed_ref = bf16[256,2880]{1,0:T(8,128)(2,1)} fusion(bf16[256,2880]{1,0:T(8,128)(2,1)S(1)} %copy.10, f32[2880]{0:T(1024)S(1)} %copy-done.3, f32[256]{0:T(256)S(1)} %add_rsqrt_fusion), kind=kLoop, calls=%fused_computation.4 | loop fusion | flops 2949120 | bytes 2961664 | tf_op jit(solution)/shard_map/convert_element_type | solution.py:189
  12.7 0.0 copy-start.4
  12.7 105.9 %all-gather.2.cloned.1.call-done.weight_ref = bf16[2560,2880]{1,0:T(8,128)(2,1)} async-done(((bf16[80,2880]{1,0:T(8,128)(2,1)}), bf16[2560,2880]{1,0:T(8,128)(2,1)}) %all-gather.2.cloned.1.call-update) | async-done | bytes 14745616 | tf_op jit(solution)/shard_map/all_gather | solution.py:177
  118.6 0.0 slice-done
  118.6 3.3 %fusion.5 = f32[256,512]{1,0:T(8,128)S(1)} fusion(bf16[256,2880]{1,0:T(8,128)(2,1)} %fusion.2.normed_ref, bf16[2560,2880]{1,0:T(8,128)(2,1)} %all-gather.2.cloned.1.call-done.weight_ref, f32[512]{0:T(512)S(1)} %slice-done), kind=kOutput, calls=%fused_computation.7 | convolution fusion | flops 755105792 | bytes 5048320 | tf_op jit(solution)/shard_map/dot_general | solution.py:195
  121.9 0.0 copy-start.1
  122.0 0.0 copy-start.2
  122.0 0.1 copy.11
  122.2 0.1 copy.12
  122.4 2.5 %collective-permute-start = (bf16[2,128,256]{2,1,0:T(8,128)(2,1)S(1)}, bf16[2,128,256]{2,1,0:T(8,128)(2,1)S(1)}, u32[]{:S(2)}, u32[]{:S(2)}) collective-permute-start(bf16[2,128,256]{2,1,0:T(8,128)(2,1)S(1)} %pad_maximum_fusion), channel_id=1, source_target_pairs={{0,1},{1,2},{2,3},{3,4},{4,5},{5,6},{6,7},{7,8},{8,9},{9,10},{10,1... | collective-permute-start | bytes 393224 | tf_op jit(solution)/shard_map/ppermute | solution.py:17
  124.8 0.0 copy-done.4
  124.8 0.6 slice.33
  125.4 0.8 copy.13.limit_ref
  126.2 0.7 copy.14.cos_ref
  127.0 0.7 copy.15.sin_ref
  127.7 3.1 %collective-permute-done = bf16[2,128,256]{2,1,0:T(8,128)(2,1)S(1)} collective-permute-done((bf16[2,128,256]{2,1,0:T(8,128)(2,1)S(1)}, bf16[2,128,256]{2,1,0:T(8,128)(2,1)S(1)}, u32[]{:S(2)}, u32[]{:S(2)}) %collective-permute-start) | collective-permute-done | bytes 131104 | tf_op jit(solution)/shard_map/ppermute | solution.py:17
  130.8 0.0 copy-done.1
  130.8 0.0 copy-done.2
  130.9 0.8 slice_bitcast_fusion
  131.7 15.0 %shard_map.82 = bf16[256,2048]{1,0:T(8,128)(2,1)} custom-call(f32[32]{0:T(128)} %sinks_ref.1, s32[256,1]{1,0:T(8,128)} %copy.13.limit_ref, f32[256,128]{1,0:T(8,128)} %copy.14.cos_ref, f32[256,128]{1,0:T(8,128)} %copy.15.sin_ref, bf16[256,2880]{1,0:T(8,128)(2,1)} %fusion.2.normed_ref, bf16[2560,2880]{1,0:T(8,128)(2,1)} %all-gather.2.cloned.1.call-done.weight_ref, ...), custom_call_target="tpu_custom_call" | custom-call | tf_op jit(solution)/shard_map/pallas_call | solution.py:131
  (13 shorter events, 0.2 us)
Async XLA Ops:
  6.5 1.2 copy-start
  6.5 3.9 %copy-start.5 = (s32[256]{0:T(256)S(1)}, s32[256]{0:T(256)}, u32[]{:S(2)}) copy-start(s32[256]{0:T(256)} %param.9) | copy-start | bytes 3076
  6.5 112.1 %all-gather.2.cloned.1.call-start = ((), (), s32[]{:S(2)}) async-start(), calls=%async_computation | async-start | bytes 15544320 | tf_op jit(solution)/shard_map/all_gather | solution.py:177
  7.7 3.3 %copy-start.3 = (f32[2880]{0:T(1024)S(1)}, f32[2880]{0:T(1024)}, u32[]{:S(2)}) copy-start(f32[2880]{0:T(1024)} %param.10) | copy-start | bytes 34564
  10.4 108.2 %slice-start = ((f32[2560]{0:T(1024)}), f32[512]{0:T(512)S(1)}, s32[]{:S(2)}) async-start(f32[2560]{0:T(1024)} %param.12), calls=%async_computation.1 | async-start | bytes 4096 | tf_op jit(solution)/shard_map/slice | solution.py:201
  12.7 112.1 %copy-start.4 = (f32[2560]{0:T(1024)S(1)}, f32[2560]{0:T(1024)}, u32[]{:S(2)}) copy-start(f32[2560]{0:T(1024)} %param.12) | copy-start | bytes 30724
  121.9 8.9 %copy-start.1 = (bf16[128,256]{1,0:T(8,128)(2,1)S(1)}, bf16[128,256]{1,0:T(8,128)(2,1)}, u32[]{:S(2)}) copy-start(bf16[128,256]{1,0:T(8,128)(2,1)} %param.15) | copy-start | bytes 196612
  122.0 8.9 %copy-start.2 = (bf16[128,256]{1,0:T(8,128)(2,1)S(1)}, bf16[128,256]{1,0:T(8,128)(2,1)}, u32[]{:S(2)}) copy-start(bf16[128,256]{1,0:T(8,128)(2,1)} %param.14) | copy-start | bytes 196612
  122.4 8.5 %collective-permute-start = (bf16[2,128,256]{2,1,0:T(8,128)(2,1)S(1)}, bf16[2,128,256]{2,1,0:T(8,128)(2,1)S(1)}, u32[]{:S(2)}, u32[]{:S(2)}) collective-permute-start(bf16[2,128,256]{2,1,0:T(8,128)(2,1)S(1)} %pad_maximum_fusion), channel_id=1, source_target_pairs={{0,1},{1,2},{2,3},{3,4},{4,5},{5,6},{6,7},{7,8},{8,9},{9,10},{10,1... | collective-permute-start | bytes 393224 | tf_op jit(solution)/shard_map/ppermute | solution.py:17
Sparse Core Ops, SparseCore 0:
  10.2 108.3 all-gather.1

commit v16 on v15

--- a/solution.py
+++ b/solution.py
@@ -77,7 +77,9 @@
         key_block = k_ref[part * block : part * block + 2 * block, :]
         value_block = v_ref[part * block : part * block + 2 * block, :]
         window_keys.append(jnp.where(pick_first, key_block[:, :HEAD_SIZE], key_block[:, HEAD_SIZE:]))
-        window_values.append(jnp.where(pick_first, value_block[:, :HEAD_SIZE], value_block[:, HEAD_SIZE:]))
+        value_lane = lax.broadcasted_iota(jnp.int32, value_block.shape, 1)
+        own_lanes = value_lane // HEAD_SIZE == group % 2
+        window_values.append(jnp.where(own_lanes, value_block, jnp.ones_like(value_block)))
     for chunk in range(queries_all.shape[1] // lanes):
         x = queries_all[:, chunk * lanes : (chunk + 1) * lanes]
         first = pltpu.roll(x, half, 1)
@@ -97,10 +99,12 @@
                 )
                 scores = jnp.where(visible[part], scores, -1e30)
                 top = jnp.maximum(jnp.max(scores, axis=1, keepdims=True), sink)
-                expo = jnp.exp(scores - top)
-                total = jnp.sum(expo, axis=1, keepdims=True) + jnp.exp(sink - top)
-                probs = (expo * (1.0 / total)).astype(jnp.bfloat16)
-                out = jnp.dot(probs, values, preferred_element_type=jnp.float32)
+                expo = jnp.exp(scores - top).astype(jnp.bfloat16)
+                weighted = jnp.dot(expo, values, preferred_element_type=jnp.float32)
+                swapped = pltpu.roll(weighted, HEAD_SIZE, 1)
+                numerator = jnp.where(pick_first, weighted, swapped)[:, :HEAD_SIZE]
+                total = jnp.where(pick_first, swapped, weighted)[:, :HEAD_SIZE] + jnp.exp(sink - top)
+                out = numerator * (1.0 / total)
                 out_ref[part * block : (part + 1) * block, head * HEAD_SIZE : (head + 1) * HEAD_SIZE] = out.astype(
                     jnp.bfloat16
                 )

time: 154 us -> 156 us (1.013)
  Pallas kernels: 15 us -> 17 us
    pallas_call x1, Pallas kernels: 15 us -> 17 us  [attend(): pl.pallas_call(attention_kernel, grid=(KEY_VALUE_HEADS,), in_specs=[pl.Bl...]
  transfers between devices with their start and end apart: 2 -> 2, of which waited for: 2 -> 2; matrix products, arithmetic and copies ran while one was open for 5% -> 4% of each run, Pallas kernels for 0% -> 0%
where the time goes in v16:
time: 156 us; the launch traced here: 155 us
  waiting for transfers between devices  109 us (70%)
  Pallas kernels  17 us (11%)
  between operations  13.6 us (9%)
  local copies, waits for them, and re-layouts  7.79 us (5%)
  matrix products  3.32 us (2%)
  starting transfers between devices  2.47 us (2%)
  other arithmetic  2.31 us (1%)
    all_gather x1, waiting for transfers between devices, gather_weight(): return lax.all_gather(own.T, ('ctx', 'dp'), axis=0, tiled=True)  106 us
    pallas_call x1, Pallas kernels, attend(): pl.pallas_call(attention_kernel, grid=(KEY_VALUE_HEADS,), in_specs=[pl.Bl...  17 us
    dot_general x1, matrix products, on_device(): lax.dot_general(normed, weight_rows[query_length:], (((1,), (1,)), ((), (...  3.32 us
  transfers between devices with their start and end apart: 2, of which 2 were waited for; matrix products, arithmetic and copies ran while one was open for 4% of the time, Pallas kernels for 0%

profile of v16, /device:TPU:4, one launch (start us, length us, event | category | flops | bytes accessed | tf_op | source)
XLA Modules:
  0.0 155.5 jit_solution(3834688581711573409)
XLA Ops:
  6.5 0.0 copy-start
  6.5 0.0 copy-start.5
  6.5 0.0 all-gather.2.cloned.1.call-start
  6.5 1.2 copy-done
  7.7 0.0 copy-start.3
  7.7 0.8 dynamic-slice_bitcast_fusion
  8.5 0.0 all-gather.2.cloned.1.call-update
  8.6 1.8 %copy.10 = bf16[256,2880]{1,0:T(8,128)(2,1)S(1)} copy(bf16[256,2880]{0,1:T(8,128)(2,1)} %param.8) | data formatting | bytes 2949120 | tf_op args[0]
  10.4 0.0 slice-start
  10.4 0.0 copy-done.5
  10.4 0.2 fusion.9
  10.7 0.4 fusion
  11.0 0.0 copy-done.3
  11.1 1.6 %fusion.2.normed_ref = bf16[256,2880]{1,0:T(8,128)(2,1)} fusion(bf16[256,2880]{1,0:T(8,128)(2,1)S(1)} %copy.10, f32[2880]{0:T(1024)S(1)} %copy-done.3, f32[256]{0:T(256)S(1)} %add_rsqrt_fusion), kind=kLoop, calls=%fused_computation.4 | loop fusion | flops 2949120 | bytes 2961664 | tf_op jit(solution)/shard_map/convert_element_type | solution.py:193
  12.7 0.0 copy-start.4
  12.7 105.9 %all-gather.2.cloned.1.call-done.weight_ref = bf16[2560,2880]{1,0:T(8,128)(2,1)} async-done(((bf16[80,2880]{1,0:T(8,128)(2,1)}), bf16[2560,2880]{1,0:T(8,128)(2,1)}) %all-gather.2.cloned.1.call-update) | async-done | bytes 14745616 | tf_op jit(solution)/shard_map/all_gather | solution.py:181
  118.6 0.0 slice-done
  118.6 3.3 %fusion.5 = f32[256,512]{1,0:T(8,128)S(1)} fusion(bf16[256,2880]{1,0:T(8,128)(2,1)} %fusion.2.normed_ref, bf16[2560,2880]{1,0:T(8,128)(2,1)} %all-gather.2.cloned.1.call-done.weight_ref, f32[512]{0:T(512)S(1)} %slice-done), kind=kOutput, calls=%fused_computation.7 | convolution fusion | flops 755105792 | bytes 5048320 | tf_op jit(solution)/shard_map/dot_general | solution.py:199
  121.9 0.0 copy-start.1
  122.0 0.0 copy-start.2
  122.0 0.1 copy.11
  122.2 0.1 copy.12
  122.4 2.5 %collective-permute-start = (bf16[2,128,256]{2,1,0:T(8,128)(2,1)S(1)}, bf16[2,128,256]{2,1,0:T(8,128)(2,1)S(1)}, u32[]{:S(2)}, u32[]{:S(2)}) collective-permute-start(bf16[2,128,256]{2,1,0:T(8,128)(2,1)S(1)} %pad_maximum_fusion), channel_id=1, source_target_pairs={{0,1},{1,2},{2,3},{3,4},{4,5},{5,6},{6,7},{7,8},{8,9},{9,10},{10,1... | collective-permute-start | bytes 393224 | tf_op jit(solution)/shard_map/ppermute | solution.py:17
  124.8 0.0 copy-done.4
  124.8 0.6 slice.33
  125.4 0.8 copy.13.limit_ref
  126.2 0.7 copy.14.cos_ref
  127.0 0.7 copy.15.sin_ref
  127.7 3.1 %collective-permute-done = bf16[2,128,256]{2,1,0:T(8,128)(2,1)S(1)} collective-permute-done((bf16[2,128,256]{2,1,0:T(8,128)(2,1)S(1)}, bf16[2,128,256]{2,1,0:T(8,128)(2,1)S(1)}, u32[]{:S(2)}, u32[]{:S(2)}) %collective-permute-start) | collective-permute-done | bytes 131104 | tf_op jit(solution)/shard_map/ppermute | solution.py:17
  130.8 0.0 copy-done.1
  130.8 0.0 copy-done.2
  130.9 0.8 slice_bitcast_fusion
  131.7 17.0 %shard_map.82 = bf16[256,2048]{1,0:T(8,128)(2,1)} custom-call(f32[32]{0:T(128)} %sinks_ref.1, s32[256,1]{1,0:T(8,128)} %copy.13.limit_ref, f32[256,128]{1,0:T(8,128)} %copy.14.cos_ref, f32[256,128]{1,0:T(8,128)} %copy.15.sin_ref, bf16[256,2880]{1,0:T(8,128)(2,1)} %fusion.2.normed_ref, bf16[2560,2880]{1,0:T(8,128)(2,1)} %all-gather.2.cloned.1.call-done.weight_ref, ...), custom_call_target="tpu_custom_call" | custom-call | tf_op jit(solution)/shard_map/pallas_call | solution.py:135
  (13 shorter events, 0.2 us)
Async XLA Ops:
  6.5 1.2 copy-start
  6.5 3.9 %copy-start.5 = (s32[256]{0:T(256)S(1)}, s32[256]{0:T(256)}, u32[]{:S(2)}) copy-start(s32[256]{0:T(256)} %param.9) | copy-start | bytes 3076
  6.5 112.1 %all-gather.2.cloned.1.call-start = ((), (), s32[]{:S(2)}) async-start(), calls=%async_computation | async-start | bytes 15544320 | tf_op jit(solution)/shard_map/all_gather | solution.py:181
  7.7 3.3 %copy-start.3 = (f32[2880]{0:T(1024)S(1)}, f32[2880]{0:T(1024)}, u32[]{:S(2)}) copy-start(f32[2880]{0:T(1024)} %param.10) | copy-start | bytes 34564
  10.4 108.2 %slice-start = ((f32[2560]{0:T(1024)}), f32[512]{0:T(512)S(1)}, s32[]{:S(2)}) async-start(f32[2560]{0:T(1024)} %param.12), calls=%async_computation.1 | async-start | bytes 4096 | tf_op jit(solution)/shard_map/slice | solution.py:205
  12.7 112.1 %copy-start.4 = (f32[2560]{0:T(1024)S(1)}, f32[2560]{0:T(1024)}, u32[]{:S(2)}) copy-start(f32[2560]{0:T(1024)} %param.12) | copy-start | bytes 30724
  121.9 8.9 %copy-start.1 = (bf16[128,256]{1,0:T(8,128)(2,1)S(1)}, bf16[128,256]{1,0:T(8,128)(2,1)}, u32[]{:S(2)}) copy-start(bf16[128,256]{1,0:T(8,128)(2,1)} %param.15) | copy-start | bytes 196612
  122.0 8.9 %copy-start.2 = (bf16[128,256]{1,0:T(8,128)(2,1)S(1)}, bf16[128,256]{1,0:T(8,128)(2,1)}, u32[]{:S(2)}) copy-start(bf16[128,256]{1,0:T(8,128)(2,1)} %param.14) | copy-start | bytes 196612
  122.4 8.5 %collective-permute-start = (bf16[2,128,256]{2,1,0:T(8,128)(2,1)S(1)}, bf16[2,128,256]{2,1,0:T(8,128)(2,1)S(1)}, u32[]{:S(2)}, u32[]{:S(2)}) collective-permute-start(bf16[2,128,256]{2,1,0:T(8,128)(2,1)S(1)} %pad_maximum_fusion), channel_id=1, source_target_pairs={{0,1},{1,2},{2,3},{3,4},{4,5},{5,6},{6,7},{7,8},{8,9},{9,10},{10,1... | collective-permute-start | bytes 393224 | tf_op jit(solution)/shard_map/ppermute | solution.py:17
Sparse Core Ops, SparseCore 0:
  10.2 108.3 all-gather.1

commit v17 on v15

--- a/solution.py
+++ b/solution.py
@@ -106,6 +106,47 @@
                 )
 
 
+def key_value_kernel(cos_ref, sin_ref, normed_ref, weight_ref, bias_ref, out_ref):
+    column = pl.program_id(0)
+    x = lax.dot_general(
+        normed_ref[...], weight_ref[...], (((1,), (1,)), ((), ())), preferred_element_type=jnp.float32
+    )
+    x = x + bias_ref[...]
+    rows, lanes = x.shape
+    half = HEAD_SIZE // 2
+    lane = lax.broadcasted_iota(jnp.int32, (rows, lanes), 1)
+    source = pltpu.roll(lane, half, 1)
+    partner_lane = jnp.where(lane % HEAD_SIZE < half, lane + half, lane - half)
+    first = pltpu.roll(x, half, 1)
+    second = pltpu.roll(x, lanes - half, 1)
+    partner = jnp.where(source == partner_lane, first, second)
+    rotated = x * cos_ref[...] + partner * sin_ref[...]
+    is_key = column < (KEY_VALUE_HEADS * HEAD_SIZE) // lanes
+    out_ref[...] = jnp.where(is_key, rotated, x).astype(jnp.bfloat16)
+
+
+def project_keys_values(normed, weight_rows, qkv_bias, tables, query_length):
+    token_rows, model_width = normed.shape
+    cos_table, sin_table, _ = tables
+    lanes = cos_table.shape[1]
+    width = weight_rows.shape[0] - query_length
+    first_block = query_length // lanes
+    bias = qkv_bias[None, :]
+    return pl.pallas_call(
+        key_value_kernel,
+        grid=(width // lanes,),
+        in_specs=[
+            pl.BlockSpec((token_rows, lanes), lambda j: (0, 0)),
+            pl.BlockSpec((token_rows, lanes), lambda j: (0, 0)),
+            pl.BlockSpec((token_rows, model_width), lambda j: (0, 0)),
+            pl.BlockSpec((lanes, model_width), lambda j: (first_block + j, 0)),
+            pl.BlockSpec((1, lanes), lambda j: (0, first_block + j)),
+        ],
+        out_specs=pl.BlockSpec((token_rows, lanes), lambda j: (0, j)),
+        out_shape=jax.ShapeDtypeStruct((token_rows, width), jnp.bfloat16),
+    )(cos_table, sin_table, normed, weight_rows, bias)
+
+
 def rotation_tables(positions, lanes):
     half = HEAD_SIZE // 2
     freq = 150000.0 ** (-(jnp.arange(half, dtype=jnp.float32) * 2.0 / HEAD_SIZE))
@@ -192,19 +233,8 @@
     )
     normed, tables = lax.optimization_barrier((normed, tables))
     weight_rows = gather_weight(qkv_weight)
-    key_value_output = lax.dot_general(
-        normed,
-        weight_rows[query_length:],
-        (((1,), (1,)), ((), ())),
-        preferred_element_type=jnp.float32,
-    )
-    key_value_output = key_value_output + qkv_bias[None, query_length:]
-    key_rows = apply_rotation(
-        key_value_output[:, :key_length].reshape(token_rows, KEY_VALUE_HEADS, HEAD_SIZE),
-        positions,
-    ).astype(jnp.bfloat16)
-    value_rows = key_value_output[:, key_length:].astype(jnp.bfloat16)
-    window_output = jnp.stack([key_rows.reshape(token_rows, key_length), value_rows])
+    key_value_output = project_keys_values(normed, weight_rows, qkv_bias, tables, query_length)
+    window_output = jnp.moveaxis(key_value_output.reshape(token_rows, 2, key_length), 1, 0)
     received = send_rim(window_output, token_rows)
     prior = jnp.stack([earlier_keys, earlier_values])
     border_tokens = jnp.where(lax.axis_index("ctx") == 0, prior, received)

time: 154 us -> 157 us (1.019)
  Pallas kernels: 15 us -> 20.5 us
  matrix products: 3.32 us -> 0 us
    pallas_call x0 -> x1, Pallas kernels: none -> 5.52 us  [project_keys_values(): pl.pallas_call(key_value_kernel, grid=(width // lanes,), in_specs=[pl.Blo...]
    dot_general x1 -> x0, matrix products: 3.32 us -> none  [on_device(): lax.dot_general(normed, weight_rows[query_length:], (((1,), (1,)), ((), (...]
    all_gather x1, waiting for transfers between devices: 106 us -> 103 us  [gather_weight(): return lax.all_gather(own.T, ('ctx', 'dp'), axis=0, tiled=True)]
where the time goes in v17:
time: 157 us; the launch traced here: 156 us
  waiting for transfers between devices  108 us (69%)
  Pallas kernels  20.5 us (13%)
  between operations  13.5 us (9%)
  local copies, waits for them, and re-layouts  9.26 us (6%)
  other arithmetic  3 us (2%)
  starting transfers between devices  2.46 us (2%)
    all_gather x1, waiting for transfers between devices, gather_weight(): return lax.all_gather(own.T, ('ctx', 'dp'), axis=0, tiled=True)  103 us
    pallas_call x1, Pallas kernels, attend(): pl.pallas_call(attention_kernel, grid=(KEY_VALUE_HEADS,), in_specs=[pl.Bl...  15 us
    pallas_call x1, Pallas kernels, project_keys_values(): pl.pallas_call(key_value_kernel, grid=(width // lanes,), in_specs=[pl.Blo...  5.52 us
    ppermute x1, waiting for transfers between devices, shifted(): lax.ppermute(value, axis, [(source, source + steps) for source in range(l...  4.59 us
  transfers between devices with their start and end apart: 2, of which 2 were waited for; matrix products, arithmetic and copies ran while one was open for 5% of the time, Pallas kernels for 0%

profile of v17, /device:TPU:4, one launch (start us, length us, event | category | flops | bytes accessed | tf_op | source)
XLA Modules:
  0.0 156.5 jit_solution(7373835828642234539)
XLA Ops:
  6.5 0.0 copy-start
  6.5 0.0 copy-start.5
  6.5 0.0 all-gather.2.cloned.1.call-start
  6.5 1.2 copy-done
  7.7 0.0 copy-start.4
  7.7 0.8 dynamic-slice_bitcast_fusion
  8.5 0.0 all-gather.2.cloned.1.call-update
  8.6 1.3 broadcast_in_dim.15.bias_ref
  9.9 1.8 %copy.10 = bf16[256,2880]{1,0:T(8,128)(2,1)S(1)} copy(bf16[256,2880]{0,1:T(8,128)(2,1)} %param.8) | data formatting | bytes 2949120 | tf_op args[0]
  11.7 0.0 copy-done.5
  11.7 0.2 fusion.6
  11.9 0.4 fusion
  12.3 0.0 copy-done.4
  12.3 1.6 %fusion.2.normed_ref = bf16[256,2880]{1,0:T(8,128)(2,1)} fusion(bf16[256,2880]{1,0:T(8,128)(2,1)S(1)} %copy.10, f32[2880]{0:T(1024)S(1)} %copy-done.4, f32[256]{0:T(256)S(1)} %add_rsqrt_fusion), kind=kLoop, calls=%fused_computation.4 | loop fusion | flops 2949120 | bytes 2961664 | tf_op jit(solution)/shard_map/convert_element_type | solution.py:230
  14.0 0.8 copy.16.cos_ref
  14.7 0.8 copy.17.sin_ref
  15.5 0.0 copy-start.3
  15.5 0.0 copy-start.1
  15.5 0.0 copy-start.2
  15.5 103.1 %all-gather.2.cloned.1.call-done.weight_ref = bf16[2560,2880]{1,0:T(8,128)(2,1)} async-done(((bf16[80,2880]{1,0:T(8,128)(2,1)}), bf16[2560,2880]{1,0:T(8,128)(2,1)}) %all-gather.2.cloned.1.call-update) | async-done | bytes 14745616 | tf_op jit(solution)/shard_map/all_gather | solution.py:218
  118.6 5.5 %shard_map.82 = bf16[256,512]{1,0:T(8,128)(2,1)} custom-call(f32[256,128]{1,0:T(8,128)} %copy.16.cos_ref, f32[256,128]{1,0:T(8,128)} %copy.17.sin_ref, bf16[256,2880]{1,0:T(8,128)(2,1)} %fusion.2.normed_ref, bf16[2560,2880]{1,0:T(8,128)(2,1)} %all-gather.2.cloned.1.call-done.weight_ref, f32[1,2560]{1,0:T(1,128)} %broadcast_in_dim.15.bias_ref), custom_call_target="tpu_custom_call" | custom-call | tf_op jit(solution)/shard_map/pallas_call | solution.py:135
  124.1 1.1 copy.13
  125.2 0.1 copy.14
  125.4 2.5 %collective-permute-start = (bf16[2,128,256]{2,1,0:T(8,128)(2,1)S(1)}, bf16[2,128,256]{2,1,0:T(8,128)(2,1)S(1)}, u32[]{:S(2)}, u32[]{:S(2)}) collective-permute-start(bf16[2,128,256]{2,1,0:T(8,128)(2,1)S(1)} %slice.18), channel_id=1, source_target_pairs={{0,1},{1,2},{2,3},{3,4},{4,5},{5,6},{6,7},{7,8},{8,9},{9,10},{10,1... | collective-permute-start | bytes 393224 | tf_op jit(solution)/shard_map/ppermute | solution.py:17
  127.8 0.0 copy-done.3
  127.9 0.6 slice.14
  128.5 0.8 copy.15.limit_ref
  129.2 4.6 %collective-permute-done = bf16[2,128,256]{2,1,0:T(8,128)(2,1)S(1)} collective-permute-done((bf16[2,128,256]{2,1,0:T(8,128)(2,1)S(1)}, bf16[2,128,256]{2,1,0:T(8,128)(2,1)S(1)}, u32[]{:S(2)}, u32[]{:S(2)}) %collective-permute-start) | collective-permute-done | bytes 131104 | tf_op jit(solution)/shard_map/ppermute | solution.py:17
  133.8 0.0 copy-done.1
  133.8 0.0 copy-done.2
  133.9 0.8 fusion.5
  134.6 15.0 %shard_map.83 = bf16[256,2048]{1,0:T(8,128)(2,1)} custom-call(f32[32]{0:T(128)} %sinks_ref.1, s32[256,1]{1,0:T(8,128)} %copy.15.limit_ref, f32[256,128]{1,0:T(8,128)} %copy.16.cos_ref, f32[256,128]{1,0:T(8,128)} %copy.17.sin_ref, bf16[256,2880]{1,0:T(8,128)(2,1)} %fusion.2.normed_ref, bf16[2560,2880]{1,0:T(8,128)(2,1)} %all-gather.2.cloned.1.call-done.weight_ref, ...), custom_call_target="tpu_custom_call" | custom-call | tf_op jit(solution)/shard_map/pallas_call | solution.py:172
  (8 shorter events, 0.1 us)
Async XLA Ops:
  6.5 1.2 copy-start
  6.5 5.2 %copy-start.5 = (s32[256]{0:T(256)S(1)}, s32[256]{0:T(256)}, u32[]{:S(2)}) copy-start(s32[256]{0:T(256)} %param.9) | copy-start | bytes 3076
  6.5 112.1 %all-gather.2.cloned.1.call-start = ((), (), s32[]{:S(2)}) async-start(), calls=%async_computation | async-start | bytes 15544320 | tf_op jit(solution)/shard_map/all_gather | solution.py:218
  7.7 4.6 %copy-start.4 = (f32[2880]{0:T(1024)S(1)}, f32[2880]{0:T(1024)}, u32[]{:S(2)}) copy-start(f32[2880]{0:T(1024)} %param.10) | copy-start | bytes 34564
  15.5 112.4 %copy-start.3 = (f32[2560]{0:T(1024)S(1)}, f32[2560]{0:T(1024)}, u32[]{:S(2)}) copy-start(f32[2560]{0:T(1024)} %param.12) | copy-start | bytes 30724
  15.5 118.3 %copy-start.1 = (bf16[128,256]{1,0:T(8,128)(2,1)S(1)}, bf16[128,256]{1,0:T(8,128)(2,1)}, u32[]{:S(2)}) copy-start(bf16[128,256]{1,0:T(8,128)(2,1)} %param.15) | copy-start | bytes 196612
  15.5 118.3 %copy-start.2 = (bf16[128,256]{1,0:T(8,128)(2,1)S(1)}, bf16[128,256]{1,0:T(8,128)(2,1)}, u32[]{:S(2)}) copy-start(bf16[128,256]{1,0:T(8,128)(2,1)} %param.14) | copy-start | bytes 196612
  125.4 8.5 %collective-permute-start = (bf16[2,128,256]{2,1,0:T(8,128)(2,1)S(1)}, bf16[2,128,256]{2,1,0:T(8,128)(2,1)S(1)}, u32[]{:S(2)}, u32[]{:S(2)}) collective-permute-start(bf16[2,128,256]{2,1,0:T(8,128)(2,1)S(1)} %slice.18), channel_id=1, source_target_pairs={{0,1},{1,2},{2,3},{3,4},{4,5},{5,6},{6,7},{7,8},{8,9},{9,10},{10,1... | collective-permute-start | bytes 393224 | tf_op jit(solution)/shard_map/ppermute | solution.py:17
Sparse Core Ops, SparseCore 0:
  10.2 108.3 all-gather.1

commit v18 on v15

--- a/solution.py
+++ b/solution.py
@@ -126,8 +126,8 @@
     cos_table, sin_table, limit = tables
     lanes = cos_table.shape[1]
     key_rows = joined_keys.shape[0]
-    keys = joined_keys.reshape(key_rows, -1)
-    values = joined_values.reshape(key_rows, -1)
+    keys = joined_keys
+    values = joined_values
     return pl.pallas_call(
         attention_kernel,
         grid=(KEY_VALUE_HEADS,),
@@ -208,18 +208,28 @@
     received = send_rim(window_output, token_rows)
     prior = jnp.stack([earlier_keys, earlier_values])
     border_tokens = jnp.where(lax.axis_index("ctx") == 0, prior, received)
-    padded_rows = jnp.concatenate([border_tokens, window_output], axis=1).reshape(
-        2, WINDOW_TOKENS + token_rows, KEY_VALUE_HEADS, HEAD_SIZE
-    )
-    return attend(
-        normed,
-        weight_rows,
-        qkv_bias[None, :query_length],
-        padded_rows[0],
-        padded_rows[1],
-        tables,
-        sinks,
-    )
+    padded_rows = jnp.concatenate([border_tokens, window_output], axis=1)
+    query_bias = qkv_bias[None, :query_length]
+    outputs = []
+    for start in range(token_rows - WINDOW_TOKENS, -1, -WINDOW_TOKENS):
+        rows = slice(start, start + WINDOW_TOKENS)
+        if start >= WINDOW_TOKENS:
+            window = window_output[:, start - WINDOW_TOKENS : start + WINDOW_TOKENS]
+        else:
+            window = padded_rows[:, start : start + 2 * WINDOW_TOKENS]
+        outputs.insert(
+            0,
+            attend(
+                normed[rows],
+                weight_rows,
+                query_bias,
+                window[0],
+                window[1],
+                tuple(table[rows] for table in tables),
+                sinks,
+            ),
+        )
+    return jnp.concatenate(outputs, axis=0)
 
 
 def solution(mesh):

time: 154 us -> 163 us (1.058); the launches traced: 154 us -> 160 us
  Pallas kernels: 15 us -> 24.1 us
  waiting for transfers between devices: 109 us -> 102 us
  other arithmetic: 2.31 us -> 5.19 us
  local copies, waits for them, and re-layouts: 7.79 us -> 10.4 us
    pallas_call x1 -> x2, Pallas kernels: 15 us -> 24.1 us  [attend(): pl.pallas_call(attention_kernel, grid=(KEY_VALUE_HEADS,), in_specs=[pl.Bl...]
    slice x1 -> x6, local copies, waits for them, and re-layouts: 0.6 us -> 5.2 us  [the longest x3 2 us: on_device(): table[rows]]
    all_gather x1, waiting for transfers between devices: 106 us -> 102 us  [gather_weight(): return lax.all_gather(own.T, ('ctx', 'dp'), axis=0, tiled=True)]
    ppermute x1, waiting for transfers between devices: 3.1 us -> 0.01 us  [shifted(): lax.ppermute(value, axis, [(source, source + steps) for source in range(l...]
    concatenate x2 -> x1, other arithmetic: 0.04 us -> 2.18 us  [on_device(): return jnp.concatenate(outputs, axis=0)]
    optimization_barrier x3, local copies, waits for them, and re-layouts: 2.28 us -> 0.32 us  [on_device(): normed, tables = lax.optimization_barrier((normed, tables))]
  transfers between devices with their start and end apart: 2 -> 2, of which waited for: 2 -> 1; matrix products, arithmetic and copies ran while one was open for 5% -> 6% of each run, Pallas kernels for 0% -> 8%
where the time goes in v18:
time: 163 us; the launch traced here: 160 us
  waiting for transfers between devices  102 us (63%)
  Pallas kernels  24.1 us (15%)
  between operations  13.6 us (8%)
  local copies, waits for them, and re-layouts  10.4 us (6%)
  other arithmetic  5.19 us (3%)
  matrix products  2.89 us (2%)
  starting transfers between devices  2.46 us (2%)
    all_gather x1, waiting for transfers between devices, gather_weight(): return lax.all_gather(own.T, ('ctx', 'dp'), axis=0, tiled=True)  102 us
    pallas_call x2, Pallas kernels, attend(): pl.pallas_call(attention_kernel, grid=(KEY_VALUE_HEADS,), in_specs=[pl.Bl...  24.1 us
  transfers between devices with their start and end apart: 2, of which 1 were waited for; matrix products, arithmetic and copies ran while one was open for 6% of the time, Pallas kernels for 8%

profile of v18, /device:TPU:4, one launch (start us, length us, event | category | flops | bytes accessed | tf_op | source)
XLA Modules:
  0.0 160.3 jit_solution(6272991151313908337)
XLA Ops:
  6.5 0.0 copy-start
  6.5 0.0 all-gather.2.cloned.1.call-start
  6.5 1.2 copy-done
  7.7 0.0 copy-start.6
  7.7 0.8 dynamic-slice_bitcast_fusion
  8.5 0.0 all-gather.2.cloned.1.call-update
  8.6 1.3 slice.62
  9.8 0.0 copy-start.5
  9.8 1.8 %copy.10 = bf16[256,2880]{1,0:T(8,128)(2,1)S(1)} copy(bf16[256,2880]{0,1:T(8,128)(2,1)} %param.8) | data formatting | bytes 2949120 | tf_op args[0]
  11.7 0.0 copy-done.6
  11.7 0.2 fusion.9
  11.9 0.4 fusion
  12.3 0.0 copy-done.5
  12.3 1.6 fusion.2
  13.9 0.0 copy-start.1
  14.0 0.0 slice-start
  14.0 0.1 copy.11
  14.1 0.1 copy.12
  14.2 0.1 copy.13
  14.3 0.7 fusion.13
  15.0 0.7 fusion.12
  15.7 0.0 copy-done.1
  15.7 1.2 fusion.10
  16.9 101.7 %all-gather.2.cloned.1.call-done.weight_ref = bf16[2560,2880]{1,0:T(8,128)(2,1)} async-done(((bf16[80,2880]{1,0:T(8,128)(2,1)}), bf16[2560,2880]{1,0:T(8,128)(2,1)}) %all-gather.2.cloned.1.call-update) | async-done | bytes 14745616 | tf_op jit(solution)/shard_map/all_gather | solution.py:177
  118.6 0.0 slice-done
  118.6 2.9 %fusion.5 = f32[256,512]{1,0:T(8,128)S(1)} fusion(bf16[256,2880]{1,0:T(8,128)(2,1)S(1)} %copy-done.1, bf16[2560,2880]{1,0:T(8,128)(2,1)} %all-gather.2.cloned.1.call-done.weight_ref, f32[512]{0:T(512)S(1)} %slice-done), kind=kOutput, calls=%fused_computation.7 | convolution fusion | flops 755105792 | bytes 5015552 | tf_op jit(solution)/shard_map/dot_general | solution.py:195
  121.6 0.1 copy.14
  121.8 0.1 copy.15
  121.9 2.5 %collective-permute-start = (bf16[2,128,256]{2,1,0:T(8,128)(2,1)S(1)}, bf16[2,128,256]{2,1,0:T(8,128)(2,1)S(1)}, u32[]{:S(2)}, u32[]{:S(2)}) collective-permute-start(bf16[2,128,256]{2,1,0:T(8,128)(2,1)S(1)} %pad_maximum_fusion.3), channel_id=1, source_target_pairs={{0,1},{1,2},{2,3},{3,4},{4,5},{5,6},{6,7},{7,8},{8,9},{9,10},{10,1... | collective-permute-start | bytes 393224 | tf_op jit(solution)/shard_map/ppermute | solution.py:17
  124.4 0.7 fusion.11
  125.0 0.7 slice.96.v_ref
  125.7 0.8 copy.19.k_ref
  126.4 0.0 copy-start.3
  126.4 0.0 copy-start.4
  126.4 12.0 %shard_map.83 = bf16[128,2048]{1,0:T(8,128)(2,1)} custom-call(f32[32]{0:T(128)} %sinks_ref.3, s32[128,1]{1,0:T(8,128)} %get-tuple-element.24.limit_ref, f32[128,128]{1,0:T(8,128)} %get-tuple-element.22.cos_ref, f32[128,128]{1,0:T(8,128)} %get-tuple-element.20.sin_ref, bf16[128,2880]{1,0:T(8,128)(2,1)} %get-tuple-element.14.normed_ref, ...), custom_call_target="tpu_custom_call" | custom-call | tf_op jit(solution)/shard_map/pallas_call | solution.py:131
  138.5 0.0 collective-permute-done
  138.5 0.0 copy-done.3
  138.5 0.0 copy-done.4
  138.5 0.7 fusion.8
  139.3 0.0 copy-start.2
  139.3 12.0 %shard_map.82 = bf16[128,2048]{1,0:T(8,128)(2,1)} custom-call(f32[32]{0:T(128)} %sinks_ref.3, s32[128,1]{1,0:T(8,128)} %get-tuple-element.23.limit_ref, f32[128,128]{1,0:T(8,128)} %get-tuple-element.21.cos_ref, f32[128,128]{1,0:T(8,128)} %get-tuple-element.19.sin_ref, bf16[128,2880]{1,0:T(8,128)(2,1)} %get-tuple-element.13.normed_ref, ...), custom_call_target="tpu_custom_call" | custom-call | tf_op jit(solution)/shard_map/pallas_call | solution.py:131
  151.3 0.0 copy-done.2
  151.3 2.2 %pad_maximum_fusion = bf16[256,2048]{1,0:T(8,128)(2,1)} fusion(bf16[128,2048]{1,0:T(8,128)(2,1)S(1)} %copy-done.2, bf16[128,2048]{1,0:T(8,128)(2,1)} %shard_map.82), kind=kLoop, calls=%fused_computation.8 | loop fusion | flops 2097152 | bytes 2097152 | tf_op jit(solution)/shard_map/concatenate | solution.py:232
  (12 shorter events, 0.2 us)
Async XLA Ops:
  6.5 1.2 copy-start
  6.5 112.1 %all-gather.2.cloned.1.call-start = ((), (), s32[]{:S(2)}) async-start(), calls=%async_computation | async-start | bytes 15544320 | tf_op jit(solution)/shard_map/all_gather | solution.py:177
  7.7 4.0 %copy-start.6 = (s32[256]{0:T(256)S(1)}, s32[256]{0:T(256)}, u32[]{:S(2)}) copy-start(s32[256]{0:T(256)} %param.9) | copy-start | bytes 3076
  9.8 2.5 %copy-start.5 = (f32[2880]{0:T(1024)S(1)}, f32[2880]{0:T(1024)}, u32[]{:S(2)}) copy-start(f32[2880]{0:T(1024)} %param.10) | copy-start | bytes 34564
  13.9 1.7 %copy-start.1 = (bf16[256,2880]{1,0:T(8,128)(2,1)S(1)}, bf16[256,2880]{1,0:T(8,128)(2,1)}, u32[]{:S(2)}) copy-start(bf16[256,2880]{1,0:T(8,128)(2,1)} %fusion.2) | copy-start | bytes 4423684
  14.0 104.6 %slice-start = ((f32[2560]{0:T(1024)}), f32[512]{0:T(512)S(1)}, s32[]{:S(2)}) async-start(f32[2560]{0:T(1024)} %param.12), calls=%async_computation.1 | async-start | bytes 4096 | tf_op jit(solution)/shard_map/slice | solution.py:201
  121.9 16.6 %collective-permute-start = (bf16[2,128,256]{2,1,0:T(8,128)(2,1)S(1)}, bf16[2,128,256]{2,1,0:T(8,128)(2,1)S(1)}, u32[]{:S(2)}, u32[]{:S(2)}) collective-permute-start(bf16[2,128,256]{2,1,0:T(8,128)(2,1)S(1)} %pad_maximum_fusion.3), channel_id=1, source_target_pairs={{0,1},{1,2},{2,3},{3,4},{4,5},{5,6},{6,7},{7,8},{8,9},{9,10},{10,1... | collective-permute-start | bytes 393224 | tf_op jit(solution)/shard_map/ppermute | solution.py:17
  126.4 12.1 %copy-start.3 = (bf16[128,256]{1,0:T(8,128)(2,1)S(1)}, bf16[128,256]{1,0:T(8,128)(2,1)}, u32[]{:S(2)}) copy-start(bf16[128,256]{1,0:T(8,128)(2,1)} %param.15) | copy-start | bytes 196612
  126.4 12.1 %copy-start.4 = (bf16[128,256]{1,0:T(8,128)(2,1)S(1)}, bf16[128,256]{1,0:T(8,128)(2,1)}, u32[]{:S(2)}) copy-start(bf16[128,256]{1,0:T(8,128)(2,1)} %param.14) | copy-start | bytes 196612
  139.3 12.0 %copy-start.2 = (bf16[128,2048]{1,0:T(8,128)(2,1)S(1)}, bf16[128,2048]{1,0:T(8,128)(2,1)}, u32[]{:S(2)}) copy-start(bf16[128,2048]{1,0:T(8,128)(2,1)} %shard_map.83) | copy-start | bytes 1572868
Sparse Core Ops, SparseCore 0:
  10.2 108.3 all-gather.1

commit v19 on v15

--- a/solution.py
+++ b/solution.py
@@ -118,16 +118,14 @@
     return cos_table, sin_table
 
 
-def attend(normed, weight_rows, query_bias, joined_keys, joined_values, tables, sinks):
+def attend(normed, weight_rows, query_bias, joined_rows, tables, sinks):
     token_rows = normed.shape[0]
     model_width = normed.shape[1]
     query_group = QUERY_HEADS // KEY_VALUE_HEADS
     group_width = query_group * HEAD_SIZE
     cos_table, sin_table, limit = tables
     lanes = cos_table.shape[1]
-    key_rows = joined_keys.shape[0]
-    keys = joined_keys.reshape(key_rows, -1)
-    values = joined_values.reshape(key_rows, -1)
+    key_rows = joined_rows.shape[1]
     return pl.pallas_call(
         attention_kernel,
         grid=(KEY_VALUE_HEADS,),
@@ -139,12 +137,12 @@
             pl.BlockSpec((token_rows, model_width), lambda g: (0, 0)),
             pl.BlockSpec((group_width, model_width), lambda g: (g, 0)),
             pl.BlockSpec((1, group_width), lambda g: (0, g)),
-            pl.BlockSpec((key_rows, 2 * HEAD_SIZE), lambda g: (0, g // 2)),
-            pl.BlockSpec((key_rows, 2 * HEAD_SIZE), lambda g: (0, g // 2)),
+            pl.BlockSpec((None, key_rows, 2 * HEAD_SIZE), lambda g: (0, 0, g // 2)),
+            pl.BlockSpec((None, key_rows, 2 * HEAD_SIZE), lambda g: (1, 0, g // 2)),
         ],
         out_specs=pl.BlockSpec((token_rows, group_width), lambda g: (0, g)),
         out_shape=jax.ShapeDtypeStruct((token_rows, QUERY_HEADS * HEAD_SIZE), jnp.bfloat16),
-    )(sinks, limit, cos_table, sin_table, normed, weight_rows, query_bias, keys, values)
+    )(sinks, limit, cos_table, sin_table, normed, weight_rows, query_bias, joined_rows, joined_rows)
 
 
 def send_rim(window_output, token_rows):
@@ -208,18 +206,8 @@
     received = send_rim(window_output, token_rows)
     prior = jnp.stack([earlier_keys, earlier_values])
     border_tokens = jnp.where(lax.axis_index("ctx") == 0, prior, received)
-    padded_rows = jnp.concatenate([border_tokens, window_output], axis=1).reshape(
-        2, WINDOW_TOKENS + token_rows, KEY_VALUE_HEADS, HEAD_SIZE
-    )
-    return attend(
-        normed,
-        weight_rows,
-        qkv_bias[None, :query_length],
-        padded_rows[0],
-        padded_rows[1],
-        tables,
-        sinks,
-    )
+    padded_rows = jnp.concatenate([border_tokens, window_output], axis=1)
+    return attend(normed, weight_rows, qkv_bias[None, :query_length], padded_rows, tables, sinks)
 
 
 def solution(mesh):

time: 154 us -> 154 us (level)
  no operation moved by 1% of the time
where the time goes in v19:
time: 154 us; the launch traced here: 153 us
  waiting for transfers between devices  109 us (71%)
  Pallas kernels  15 us (10%)
  between operations  13.6 us (9%)
  local copies, waits for them, and re-layouts  7.01 us (5%)
  matrix products  3.32 us (2%)
  other arithmetic  3.06 us (2%)
  starting transfers between devices  2.47 us (2%)
    all_gather x1, waiting for transfers between devices, gather_weight(): return lax.all_gather(own.T, ('ctx', 'dp'), axis=0, tiled=True)  106 us
    pallas_call x1, Pallas kernels, attend(): pl.pallas_call(attention_kernel, grid=(KEY_VALUE_HEADS,), in_specs=[pl.Bl...  15 us
    dot_general x1, matrix products, on_device(): lax.dot_general(normed, weight_rows[query_length:], (((1,), (1,)), ((), (...  3.32 us
    ppermute x1, waiting for transfers between devices, shifted(): lax.ppermute(value, axis, [(source, source + steps) for source in range(l...  3.09 us
  transfers between devices with their start and end apart: 2, of which 2 were waited for; matrix products, arithmetic and copies ran while one was open for 5% of the time, Pallas kernels for 0%

profile of v19, /device:TPU:4, one launch (start us, length us, event | category | flops | bytes accessed | tf_op | source)
XLA Modules:
  0.0 153.5 jit_solution(18127160185311490881)
XLA Ops:
  6.5 0.0 copy-start
  6.5 0.0 copy-start.5
  6.5 0.0 all-gather.2.cloned.1.call-start
  6.5 1.2 copy-done
  7.7 0.0 copy-start.3
  7.7 0.8 dynamic-slice_bitcast_fusion
  8.5 0.0 all-gather.2.cloned.1.call-update
  8.6 1.8 %copy.10 = bf16[256,2880]{1,0:T(8,128)(2,1)S(1)} copy(bf16[256,2880]{0,1:T(8,128)(2,1)} %param.8) | data formatting | bytes 2949120 | tf_op args[0]
  10.4 0.0 slice-start
  10.4 0.0 copy-done.5
  10.4 0.2 fusion.9
  10.7 0.4 fusion
  11.0 0.0 copy-done.3
  11.1 1.6 %fusion.2.normed_ref = bf16[256,2880]{1,0:T(8,128)(2,1)} fusion(bf16[256,2880]{1,0:T(8,128)(2,1)S(1)} %copy.10, f32[2880]{0:T(1024)S(1)} %copy-done.3, f32[256]{0:T(256)S(1)} %add_rsqrt_fusion), kind=kLoop, calls=%fused_computation.4 | loop fusion | flops 2949120 | bytes 2961664 | tf_op jit(solution)/shard_map/convert_element_type | solution.py:187
  12.7 0.0 copy-start.4
  12.7 105.9 %all-gather.2.cloned.1.call-done.weight_ref = bf16[2560,2880]{1,0:T(8,128)(2,1)} async-done(((bf16[80,2880]{1,0:T(8,128)(2,1)}), bf16[2560,2880]{1,0:T(8,128)(2,1)}) %all-gather.2.cloned.1.call-update) | async-done | bytes 14745616 | tf_op jit(solution)/shard_map/all_gather | solution.py:175
  118.6 0.0 slice-done
  118.6 3.3 %fusion.5 = f32[256,512]{1,0:T(8,128)S(1)} fusion(bf16[256,2880]{1,0:T(8,128)(2,1)} %fusion.2.normed_ref, bf16[2560,2880]{1,0:T(8,128)(2,1)} %all-gather.2.cloned.1.call-done.weight_ref, f32[512]{0:T(512)S(1)} %slice-done), kind=kOutput, calls=%fused_computation.7 | convolution fusion | flops 755105792 | bytes 5048320 | tf_op jit(solution)/shard_map/dot_general | solution.py:193
  121.9 0.0 copy-start.1
  122.0 0.0 copy-start.2
  122.0 0.1 copy.11
  122.2 0.1 copy.12
  122.3 2.5 %collective-permute-start = (bf16[2,128,256]{2,1,0:T(8,128)(2,1)S(1)}, bf16[2,128,256]{2,1,0:T(8,128)(2,1)S(1)}, u32[]{:S(2)}, u32[]{:S(2)}) collective-permute-start(bf16[2,128,256]{2,1,0:T(8,128)(2,1)S(1)} %pad_maximum_fusion), channel_id=1, source_target_pairs={{0,1},{1,2},{2,3},{3,4},{4,5},{5,6},{6,7},{7,8},{8,9},{9,10},{10,1... | collective-permute-start | bytes 393224 | tf_op jit(solution)/shard_map/ppermute | solution.py:17
  124.8 0.0 copy-done.4
  124.8 0.6 slice.25
  125.4 0.8 copy.13.limit_ref
  126.2 0.8 copy.14.cos_ref
  127.0 0.7 copy.15.sin_ref
  127.7 3.1 %collective-permute-done = bf16[2,128,256]{2,1,0:T(8,128)(2,1)S(1)} collective-permute-done((bf16[2,128,256]{2,1,0:T(8,128)(2,1)S(1)}, bf16[2,128,256]{2,1,0:T(8,128)(2,1)S(1)}, u32[]{:S(2)}, u32[]{:S(2)}) %collective-permute-start) | collective-permute-done | bytes 131104 | tf_op jit(solution)/shard_map/ppermute | solution.py:17
  130.8 0.0 copy-done.1
  130.8 0.0 copy-done.2
  130.8 0.8 maximum_maximum_fusion.k_ref.v_ref
  131.6 15.0 %shard_map.82 = bf16[256,2048]{1,0:T(8,128)(2,1)} custom-call(f32[32]{0:T(128)} %sinks_ref.1, s32[256,1]{1,0:T(8,128)} %copy.13.limit_ref, f32[256,128]{1,0:T(8,128)} %copy.14.cos_ref, f32[256,128]{1,0:T(8,128)} %copy.15.sin_ref, bf16[256,2880]{1,0:T(8,128)(2,1)} %fusion.2.normed_ref, bf16[2560,2880]{1,0:T(8,128)(2,1)} %all-gather.2.cloned.1.call-done.weight_ref, ...), custom_call_target="tpu_custom_call" | custom-call | tf_op jit(solution)/shard_map/pallas_call | solution.py:129
  (12 shorter events, 0.2 us)
Async XLA Ops:
  6.5 1.2 copy-start
  6.5 3.9 %copy-start.5 = (s32[256]{0:T(256)S(1)}, s32[256]{0:T(256)}, u32[]{:S(2)}) copy-start(s32[256]{0:T(256)} %param.9) | copy-start | bytes 3076
  6.5 112.1 %all-gather.2.cloned.1.call-start = ((), (), s32[]{:S(2)}) async-start(), calls=%async_computation | async-start | bytes 15544320 | tf_op jit(solution)/shard_map/all_gather | solution.py:175
  7.7 3.3 %copy-start.3 = (f32[2880]{0:T(1024)S(1)}, f32[2880]{0:T(1024)}, u32[]{:S(2)}) copy-start(f32[2880]{0:T(1024)} %param.10) | copy-start | bytes 34564
  10.4 108.2 %slice-start = ((f32[2560]{0:T(1024)}), f32[512]{0:T(512)S(1)}, s32[]{:S(2)}) async-start(f32[2560]{0:T(1024)} %param.12), calls=%async_computation.1 | async-start | bytes 4096 | tf_op jit(solution)/shard_map/slice | solution.py:199
  12.7 112.1 %copy-start.4 = (f32[2560]{0:T(1024)S(1)}, f32[2560]{0:T(1024)}, u32[]{:S(2)}) copy-start(f32[2560]{0:T(1024)} %param.12) | copy-start | bytes 30724
  121.9 8.9 %copy-start.1 = (bf16[128,256]{1,0:T(8,128)(2,1)S(1)}, bf16[128,256]{1,0:T(8,128)(2,1)}, u32[]{:S(2)}) copy-start(bf16[128,256]{1,0:T(8,128)(2,1)} %param.15) | copy-start | bytes 196612
  122.0 8.9 %copy-start.2 = (bf16[128,256]{1,0:T(8,128)(2,1)S(1)}, bf16[128,256]{1,0:T(8,128)(2,1)}, u32[]{:S(2)}) copy-start(bf16[128,256]{1,0:T(8,128)(2,1)} %param.14) | copy-start | bytes 196612
  122.3 8.5 %collective-permute-start = (bf16[2,128,256]{2,1,0:T(8,128)(2,1)S(1)}, bf16[2,128,256]{2,1,0:T(8,128)(2,1)S(1)}, u32[]{:S(2)}, u32[]{:S(2)}) collective-permute-start(bf16[2,128,256]{2,1,0:T(8,128)(2,1)S(1)} %pad_maximum_fusion), channel_id=1, source_target_pairs={{0,1},{1,2},{2,3},{3,4},{4,5},{5,6},{6,7},{7,8},{8,9},{9,10},{10,1... | collective-permute-start | bytes 393224 | tf_op jit(solution)/shard_map/ppermute | solution.py:17
Sparse Core Ops, SparseCore 0:
  10.2 108.3 all-gather.1

commit v20 on v19

--- a/solution.py
+++ b/solution.py
@@ -109,13 +109,11 @@
 def rotation_tables(positions, lanes):
     half = HEAD_SIZE // 2
     freq = 150000.0 ** (-(jnp.arange(half, dtype=jnp.float32) * 2.0 / HEAD_SIZE))
-    angle = positions.astype(jnp.float32)[:, None] * freq[None, :]
-    cosine = jnp.cos(angle)
-    sine = jnp.sin(angle)
-    repeats = lanes // HEAD_SIZE
-    cos_table = jnp.tile(jnp.concatenate([cosine, cosine], axis=1), (1, repeats))
-    sin_table = jnp.tile(jnp.concatenate([-sine, sine], axis=1), (1, repeats))
-    return cos_table, sin_table
+    repeats = lanes // half
+    lane_freq = jnp.tile(freq, repeats)
+    sign = jnp.tile(jnp.concatenate([-jnp.ones(half), jnp.ones(half)]).astype(jnp.float32), lanes // HEAD_SIZE)
+    angle = positions.astype(jnp.float32)[:, None] * lane_freq[None, :]
+    return jnp.cos(angle), sign[None, :] * jnp.sin(angle)
 
 
 def attend(normed, weight_rows, query_bias, joined_rows, tables, sinks):

time: 154 us -> 154 us (level)
    all_gather x1, waiting for transfers between devices: 106 us -> 104 us  [gather_weight(): return lax.all_gather(own.T, ('ctx', 'dp'), axis=0, tiled=True)]
where the time goes in v20:
time: 154 us; the launch traced here: 153 us
  waiting for transfers between devices  108 us (70%)
  Pallas kernels  15 us (10%)
  between operations  13.5 us (9%)
  local copies, waits for them, and re-layouts  6.33 us (4%)
  other arithmetic  4.29 us (3%)
  matrix products  3.32 us (2%)
  starting transfers between devices  2.47 us (2%)
    all_gather x1, waiting for transfers between devices, gather_weight(): return lax.all_gather(own.T, ('ctx', 'dp'), axis=0, tiled=True)  104 us
    pallas_call x1, Pallas kernels, attend(): pl.pallas_call(attention_kernel, grid=(KEY_VALUE_HEADS,), in_specs=[pl.Bl...  15 us
    ppermute x1, waiting for transfers between devices, shifted(): lax.ppermute(value, axis, [(source, source + steps) for source in range(l...  4.59 us
    dot_general x1, matrix products, on_device(): lax.dot_general(normed, weight_rows[query_length:], (((1,), (1,)), ((), (...  3.32 us
  transfers between devices with their start and end apart: 2, of which 2 were waited for; matrix products, arithmetic and copies ran while one was open for 5% of the time, Pallas kernels for 0%

profile of v20, /device:TPU:4, one launch (start us, length us, event | category | flops | bytes accessed | tf_op | source)
XLA Modules:
  0.0 153.4 jit_solution(4492719255477368781)
XLA Ops:
  6.5 0.0 copy-start
  6.5 0.0 copy-start.5
  6.5 0.0 all-gather.2.cloned.1.call-start
  6.5 1.2 copy-done
  7.7 0.0 copy-start.3
  7.7 0.8 dynamic-slice_bitcast_fusion
  8.5 0.0 all-gather.2.cloned.1.call-update
  8.6 0.7 tile.5
  9.2 0.1 mul.107
  9.3 0.1 mul.104
  9.4 1.8 %copy.10 = bf16[256,2880]{1,0:T(8,128)(2,1)S(1)} copy(bf16[256,2880]{0,1:T(8,128)(2,1)} %param.8) | data formatting | bytes 2949120 | tf_op args[0]
  11.2 0.0 slice-start
  11.2 0.4 fusion
  11.6 0.0 copy-done.5
  11.7 1.2 fusion.8
  12.9 0.0 copy-done.3
  12.9 1.6 %fusion.2.normed_ref = bf16[256,2880]{1,0:T(8,128)(2,1)} fusion(bf16[256,2880]{1,0:T(8,128)(2,1)S(1)} %copy.10, f32[2880]{0:T(1024)S(1)} %copy-done.3, f32[256]{0:T(256)S(1)} %add_rsqrt_fusion), kind=kLoop, calls=%fused_computation.4 | loop fusion | flops 2949120 | bytes 2961664 | tf_op jit(solution)/shard_map/convert_element_type | solution.py:185
  14.5 0.2 multiply_cosine_fusion.1
  14.7 0.0 copy-start.4
  14.7 0.0 copy-start.1
  14.7 0.0 copy-start.2
  14.7 103.9 %all-gather.2.cloned.1.call-done.weight_ref = bf16[2560,2880]{1,0:T(8,128)(2,1)} async-done(((bf16[80,2880]{1,0:T(8,128)(2,1)}), bf16[2560,2880]{1,0:T(8,128)(2,1)}) %all-gather.2.cloned.1.call-update) | async-done | bytes 14745616 | tf_op jit(solution)/shard_map/all_gather | solution.py:173
  118.6 0.0 slice-done
  118.6 3.3 %fusion.5 = f32[256,512]{1,0:T(8,128)S(1)} fusion(bf16[256,2880]{1,0:T(8,128)(2,1)} %fusion.2.normed_ref, bf16[2560,2880]{1,0:T(8,128)(2,1)} %all-gather.2.cloned.1.call-done.weight_ref, f32[512]{0:T(512)S(1)} %slice-done), kind=kOutput, calls=%fused_computation.7 | convolution fusion | flops 755105792 | bytes 5048320 | tf_op jit(solution)/shard_map/dot_general | solution.py:191
  122.0 0.1 copy.11
  122.2 0.1 copy.12
  122.3 2.5 %collective-permute-start = (bf16[2,128,256]{2,1,0:T(8,128)(2,1)S(1)}, bf16[2,128,256]{2,1,0:T(8,128)(2,1)S(1)}, u32[]{:S(2)}, u32[]{:S(2)}) collective-permute-start(bf16[2,128,256]{2,1,0:T(8,128)(2,1)S(1)} %pad_maximum_fusion), channel_id=1, source_target_pairs={{0,1},{1,2},{2,3},{3,4},{4,5},{5,6},{6,7},{7,8},{8,9},{9,10},{10,1... | collective-permute-start | bytes 393224 | tf_op jit(solution)/shard_map/ppermute | solution.py:17
  124.8 0.0 copy-done.4
  124.8 0.6 slice.25
  125.4 0.8 copy.13.limit_ref
  126.2 4.6 %collective-permute-done = bf16[2,128,256]{2,1,0:T(8,128)(2,1)S(1)} collective-permute-done((bf16[2,128,256]{2,1,0:T(8,128)(2,1)S(1)}, bf16[2,128,256]{2,1,0:T(8,128)(2,1)S(1)}, u32[]{:S(2)}, u32[]{:S(2)}) %collective-permute-start) | collective-permute-done | bytes 131104 | tf_op jit(solution)/shard_map/ppermute | solution.py:17
  130.8 0.0 copy-done.1
  130.8 0.0 copy-done.2
  130.8 0.8 maximum_maximum_fusion.k_ref.v_ref
  131.6 15.0 %shard_map.82 = bf16[256,2048]{1,0:T(8,128)(2,1)} custom-call(f32[32]{0:T(128)} %sinks_ref.1, s32[256,1]{1,0:T(8,128)} %copy.13.limit_ref, f32[256,128]{1,0:T(8,128)} %get-tuple-element.10.cos_ref, f32[256,128]{1,0:T(8,128)} %get-tuple-element.11.sin_ref, bf16[256,2880]{1,0:T(8,128)(2,1)} %fusion.2.normed_ref, ...), custom_call_target="tpu_custom_call" | custom-call | tf_op jit(solution)/shard_map/pallas_call | solution.py:127
  (10 shorter events, 0.1 us)
Async XLA Ops:
  6.5 1.2 copy-start
  6.5 5.1 %copy-start.5 = (s32[256]{0:T(256)S(1)}, s32[256]{0:T(256)}, u32[]{:S(2)}) copy-start(s32[256]{0:T(256)} %param.9) | copy-start | bytes 3076
  6.5 112.1 %all-gather.2.cloned.1.call-start = ((), (), s32[]{:S(2)}) async-start(), calls=%async_computation | async-start | bytes 15544320 | tf_op jit(solution)/shard_map/all_gather | solution.py:173
  7.7 5.2 %copy-start.3 = (f32[2880]{0:T(1024)S(1)}, f32[2880]{0:T(1024)}, u32[]{:S(2)}) copy-start(f32[2880]{0:T(1024)} %param.10) | copy-start | bytes 34564
  11.2 107.4 %slice-start = ((f32[2560]{0:T(1024)}), f32[512]{0:T(512)S(1)}, s32[]{:S(2)}) async-start(f32[2560]{0:T(1024)} %param.12), calls=%async_computation.1 | async-start | bytes 4096 | tf_op jit(solution)/shard_map/slice | solution.py:197
  14.7 110.1 %copy-start.4 = (f32[2560]{0:T(1024)S(1)}, f32[2560]{0:T(1024)}, u32[]{:S(2)}) copy-start(f32[2560]{0:T(1024)} %param.12) | copy-start | bytes 30724
  14.7 116.1 %copy-start.1 = (bf16[128,256]{1,0:T(8,128)(2,1)S(1)}, bf16[128,256]{1,0:T(8,128)(2,1)}, u32[]{:S(2)}) copy-start(bf16[128,256]{1,0:T(8,128)(2,1)} %param.15) | copy-start | bytes 196612
  14.7 116.1 %copy-start.2 = (bf16[128,256]{1,0:T(8,128)(2,1)S(1)}, bf16[128,256]{1,0:T(8,128)(2,1)}, u32[]{:S(2)}) copy-start(bf16[128,256]{1,0:T(8,128)(2,1)} %param.14) | copy-start | bytes 196612
  122.3 8.5 %collective-permute-start = (bf16[2,128,256]{2,1,0:T(8,128)(2,1)S(1)}, bf16[2,128,256]{2,1,0:T(8,128)(2,1)S(1)}, u32[]{:S(2)}, u32[]{:S(2)}) collective-permute-start(bf16[2,128,256]{2,1,0:T(8,128)(2,1)S(1)} %pad_maximum_fusion), channel_id=1, source_target_pairs={{0,1},{1,2},{2,3},{3,4},{4,5},{5,6},{6,7},{7,8},{8,9},{9,10},{10,1... | collective-permute-start | bytes 393224 | tf_op jit(solution)/shard_map/ppermute | solution.py:17
Sparse Core Ops, SparseCore 0:
  10.2 108.3 all-gather.1

commit v21 on v20

--- a/solution.py
+++ b/solution.py
@@ -188,20 +188,25 @@
     )
     normed, tables = lax.optimization_barrier((normed, tables))
     weight_rows = gather_weight(qkv_weight)
-    key_value_output = lax.dot_general(
-        normed,
-        weight_rows[query_length:],
-        (((1,), (1,)), ((), ())),
-        preferred_element_type=jnp.float32,
-    )
-    key_value_output = key_value_output + qkv_bias[None, query_length:]
-    key_rows = apply_rotation(
-        key_value_output[:, :key_length].reshape(token_rows, KEY_VALUE_HEADS, HEAD_SIZE),
-        positions,
-    ).astype(jnp.bfloat16)
-    value_rows = key_value_output[:, key_length:].astype(jnp.bfloat16)
-    window_output = jnp.stack([key_rows.reshape(token_rows, key_length), value_rows])
-    received = send_rim(window_output, token_rows)
+    def key_value_rows(rows):
+        output = lax.dot_general(
+            normed[rows],
+            weight_rows[query_length:],
+            (((1,), (1,)), ((), ())),
+            preferred_element_type=jnp.float32,
+        )
+        output = output + qkv_bias[None, query_length:]
+        count = output.shape[0]
+        keys = apply_rotation(
+            output[:, :key_length].reshape(count, KEY_VALUE_HEADS, HEAD_SIZE), positions[rows]
+        ).astype(jnp.bfloat16)
+        values = output[:, key_length:].astype(jnp.bfloat16)
+        return jnp.stack([keys.reshape(count, key_length), values])
+
+    late_rows = key_value_rows(slice(token_rows - WINDOW_TOKENS, token_rows))
+    received = shifted(late_rows, "ctx", 1)
+    early_rows = key_value_rows(slice(0, token_rows - WINDOW_TOKENS))
+    window_output = jnp.concatenate([early_rows, late_rows], axis=1)
     prior = jnp.stack([earlier_keys, earlier_values])
     border_tokens = jnp.where(lax.axis_index("ctx") == 0, prior, received)
     padded_rows = jnp.concatenate([border_tokens, window_output], axis=1)

time: 154 us -> 157 us (1.019)
  matrix products: 3.32 us -> 6.2 us
    dot_general x1 -> x2, matrix products: 3.32 us -> 6.2 us  [key_value_rows(): lax.dot_general(normed[rows], weight_rows[query_length:], (((1,), (1,)),...]
    all_gather x1, waiting for transfers between devices: 104 us -> 101 us  [gather_weight(): return lax.all_gather(own.T, ('ctx', 'dp'), axis=0, tiled=True)]
  transfers between devices with their start and end apart: 2 -> 2, of which waited for: 2 -> 2; matrix products, arithmetic and copies ran while one was open for 5% -> 6% of each run, Pallas kernels for 0% -> 0%
where the time goes in v21:
time: 157 us
  waiting for transfers between devices  107 us (68%)
  Pallas kernels  15 us (10%)
  between operations  13.6 us (9%)
  local copies, waits for them, and re-layouts  7.88 us (5%)
  matrix products  6.2 us (4%)
  other arithmetic  4.3 us (3%)
  starting transfers between devices  2.47 us (2%)
    all_gather x1, waiting for transfers between devices, gather_weight(): return lax.all_gather(own.T, ('ctx', 'dp'), axis=0, tiled=True)  101 us
    pallas_call x1, Pallas kernels, attend(): pl.pallas_call(attention_kernel, grid=(KEY_VALUE_HEADS,), in_specs=[pl.Bl...  15 us
    dot_general x2, matrix products, key_value_rows(): lax.dot_general(normed[rows], weight_rows[query_length:], (((1,), (1,)),...  6.2 us
    ppermute x1, waiting for transfers between devices, shifted(): lax.ppermute(value, axis, [(source, source + steps) for source in range(l...  5.96 us
  transfers between devices with their start and end apart: 2, of which 2 were waited for; matrix products, arithmetic and copies ran while one was open for 6% of the time, Pallas kernels for 0%

profile of v21, /device:TPU:4, one launch (start us, length us, event | category | flops | bytes accessed | tf_op | source)
XLA Modules:
  0.0 156.5 jit_solution(3020075415226086562)
XLA Ops:
  6.5 0.0 copy-start
  6.5 0.0 copy-start.5
  6.5 0.0 all-gather.2.cloned.1.call-start
  6.5 1.2 copy-done
  7.7 0.0 copy-start.4
  7.7 0.8 dynamic-slice_bitcast_fusion
  8.5 0.0 all-gather.2.cloned.1.call-update
  8.6 0.7 slice.52
  9.2 1.3 slice.49
  10.5 0.7 tile.5
  11.2 0.1 mul.156
  11.3 0.1 mul.153
  11.4 1.8 %copy.10 = bf16[256,2880]{1,0:T(8,128)(2,1)S(1)} copy(bf16[256,2880]{0,1:T(8,128)(2,1)} %param.8) | data formatting | bytes 2949120 | tf_op args[0]
  13.2 0.4 fusion
  13.6 0.0 copy-done.5
  13.6 1.2 fusion.15
  14.9 0.0 copy-done.4
  14.9 1.6 %fusion.2.normed_ref = bf16[256,2880]{1,0:T(8,128)(2,1)} fusion(bf16[256,2880]{1,0:T(8,128)(2,1)S(1)} %copy.10, f32[2880]{0:T(1024)S(1)} %copy-done.4, f32[256]{0:T(256)S(1)} %add_rsqrt_fusion), kind=kLoop, calls=%fused_computation.4 | loop fusion | flops 2949120 | bytes 2961664 | tf_op jit(solution)/shard_map/convert_element_type | solution.py:185
  16.5 0.0 copy-start.1
  16.5 0.8 copy.15.limit_ref
  17.3 0.2 multiply_cosine_fusion.1
  17.5 101.1 %all-gather.2.cloned.1.call-done.weight_ref = bf16[2560,2880]{1,0:T(8,128)(2,1)} async-done(((bf16[80,2880]{1,0:T(8,128)(2,1)}), bf16[2560,2880]{1,0:T(8,128)(2,1)}) %all-gather.2.cloned.1.call-update) | async-done | bytes 14745616 | tf_op jit(solution)/shard_map/all_gather | solution.py:173
  118.6 3.2 %fusion.7 = f32[128,512]{1,0:T(8,128)S(1)} fusion(bf16[2560,2880]{1,0:T(8,128)(2,1)} %all-gather.2.cloned.1.call-done.weight_ref, bf16[256,2880]{1,0:T(8,128)(2,1)} %fusion.2.normed_ref, f32[512]{0:T(512)S(1)} %slice.52), kind=kOutput, calls=%fused_computation.9 | convolution fusion | flops 377552896 | bytes 4032512 | tf_op jit(solution)/shard_map/dot_general | solution.py:192
  121.9 0.0 copy-done.1
  121.9 0.0 copy-start.2
  121.9 0.0 copy-start.3
  121.9 3.0 %fusion.10 = f32[128,512]{1,0:T(8,128)S(1)} fusion(bf16[2560,2880]{1,0:T(8,128)(2,1)} %all-gather.2.cloned.1.call-done.weight_ref, bf16[256,2880]{1,0:T(8,128)(2,1)S(1)} %copy-done.1, f32[512]{0:T(512)S(1)} %slice.52), kind=kOutput, calls=%fused_computation.10 | convolution fusion | flops 377552896 | bytes 4032512 | tf_op jit(solution)/shard_map/dot_general | solution.py:192
  124.9 0.1 copy.13
  125.0 0.1 copy.11
  125.2 0.1 copy.14
  125.3 0.1 copy.12
  125.4 2.5 %collective-permute-start = (bf16[2,128,256]{2,1,0:T(8,128)(2,1)S(1)}, bf16[2,128,256]{2,1,0:T(8,128)(2,1)S(1)}, u32[]{:S(2)}, u32[]{:S(2)}) collective-permute-start(bf16[2,128,256]{2,1,0:T(8,128)(2,1)S(1)} %pad_maximum_fusion), channel_id=1, source_target_pairs={{0,1},{1,2},{2,3},{3,4},{4,5},{5,6},{6,7},{7,8},{8,9},{9,10},{10,1... | collective-permute-start | bytes 393224 | tf_op jit(solution)/shard_map/ppermute | solution.py:17
  127.9 6.0 %collective-permute-done = bf16[2,128,256]{2,1,0:T(8,128)(2,1)S(1)} collective-permute-done((bf16[2,128,256]{2,1,0:T(8,128)(2,1)S(1)}, bf16[2,128,256]{2,1,0:T(8,128)(2,1)S(1)}, u32[]{:S(2)}, u32[]{:S(2)}) %collective-permute-start) | collective-permute-done | bytes 131104 | tf_op jit(solution)/shard_map/ppermute | solution.py:17
  133.9 0.0 copy-done.2
  133.9 0.0 copy-done.3
  133.9 0.8 maximum_maximum_fusion.k_ref.v_ref
  134.7 15.0 %shard_map.82 = bf16[256,2048]{1,0:T(8,128)(2,1)} custom-call(f32[32]{0:T(128)} %sinks_ref.1, s32[256,1]{1,0:T(8,128)} %copy.15.limit_ref, f32[256,128]{1,0:T(8,128)} %get-tuple-element.10.cos_ref, f32[256,128]{1,0:T(8,128)} %get-tuple-element.11.sin_ref, bf16[256,2880]{1,0:T(8,128)(2,1)} %fusion.2.normed_ref, ...), custom_call_target="tpu_custom_call" | custom-call | tf_op jit(solution)/shard_map/pallas_call | solution.py:127
  (14 shorter events, 0.2 us)
Async XLA Ops:
  6.5 1.2 copy-start
  6.5 7.1 %copy-start.5 = (s32[256]{0:T(256)S(1)}, s32[256]{0:T(256)}, u32[]{:S(2)}) copy-start(s32[256]{0:T(256)} %param.9) | copy-start | bytes 3076
  6.5 112.1 %all-gather.2.cloned.1.call-start = ((), (), s32[]{:S(2)}) async-start(), calls=%async_computation | async-start | bytes 15544320 | tf_op jit(solution)/shard_map/all_gather | solution.py:173
  7.7 7.1 %copy-start.4 = (f32[2880]{0:T(1024)S(1)}, f32[2880]{0:T(1024)}, u32[]{:S(2)}) copy-start(f32[2880]{0:T(1024)} %param.10) | copy-start | bytes 34564
  16.5 105.4 %copy-start.1 = (bf16[256,2880]{1,0:T(8,128)(2,1)S(1)}, bf16[256,2880]{1,0:T(8,128)(2,1)}, u32[]{:S(2)}) copy-start(bf16[256,2880]{1,0:T(8,128)(2,1)} %fusion.2.normed_ref) | copy-start | bytes 4423684
  121.9 12.0 %copy-start.2 = (bf16[128,256]{1,0:T(8,128)(2,1)S(1)}, bf16[128,256]{1,0:T(8,128)(2,1)}, u32[]{:S(2)}) copy-start(bf16[128,256]{1,0:T(8,128)(2,1)} %param.15) | copy-start | bytes 196612
  121.9 12.0 %copy-start.3 = (bf16[128,256]{1,0:T(8,128)(2,1)S(1)}, bf16[128,256]{1,0:T(8,128)(2,1)}, u32[]{:S(2)}) copy-start(bf16[128,256]{1,0:T(8,128)(2,1)} %param.14) | copy-start | bytes 196612
  125.4 8.5 %collective-permute-start = (bf16[2,128,256]{2,1,0:T(8,128)(2,1)S(1)}, bf16[2,128,256]{2,1,0:T(8,128)(2,1)S(1)}, u32[]{:S(2)}, u32[]{:S(2)}) collective-permute-start(bf16[2,128,256]{2,1,0:T(8,128)(2,1)S(1)} %pad_maximum_fusion), channel_id=1, source_target_pairs={{0,1},{1,2},{2,3},{3,4},{4,5},{5,6},{6,7},{7,8},{8,9},{9,10},{10,1... | collective-permute-start | bytes 393224 | tf_op jit(solution)/shard_map/ppermute | solution.py:17
Sparse Core Ops, SparseCore 0:
  10.2 108.3 all-gather.1
